TPU v7x, 256 devices: a whole 4x4x8 slice. The times are simulated.
256 devices in a mesh: section: 4 (over y_lo, core), dp: 64 (over y_hi, z, x).
Axes of the slice: x: 4, y: 4 (y_hi: 2, y_lo: 2; y = y_hi * 2 + y_lo), z: 8, core: 2. Of those that a mesh axis runs over, the one named last changes fastest.
Arguments:
- token_states: bfloat16 [4, 1024, 8192], P(None, 'dp'), may hold values from -10 to 10
- norm_gains: float32 [4, 8192], P('section'), may hold values from 1 to 4
- prompt_kv: bfloat16 [4, 1024, 2048], P('section'), may hold values from -11 to 11
- history_kv: bfloat16 [4, 1024, 28, 2048], P('section', 'dp'), may hold values from -6 to 6
- new_kv: bfloat16 [4, 4, 1024, 2048], P('section', None, 'dp'), may hold values from -6 to 6
- ancestors: int32 [1024], replicated, may hold values from 0 to 1023, as said below
Outputs:
- attention_out: bfloat16 [4, 4, 1024, 8192], P('section', None, 'dp')
- forked_kv: bfloat16 [4, 1024, 32, 2048], P('section', 'dp')
Inputs may be any that keep to these rules, and one draw needn't show every extreme that they name: Of the 16 ancestors of particles p * 16 .. p * 16 + 15, at most one distinct value lies in any block q * 16 .. q * 16 + 15; ancestors may repeat.
All inputs are finite; a program needn't handle non-finite values.
Results may differ from a plain program's by a relative error of at most 0.0086.
Values may be sent and summed in bfloat16 or wider, within the bound.
No kernel may reach another device: no remote copies, remote signals or barrier semaphores. Data moves between devices by JAX's collectives and lax.ppermute only.
A program may use at most 128 MiB of HBM per device.

v0:
```python
import jax
import jax.numpy as jnp
from jax import lax
from jax.sharding import PartitionSpec as P

HEADS = 64
KV_HEADS = 8
HEAD_DIM = 128


NEG_FILL = -1e30


def passed_along(block, axis, distance):
    devices = range(lax.axis_size(axis))
    route = [((i - distance) % len(devices), i) for i in devices]
    return lax.ppermute(block, axis, route)


def normalize(values):
    return values * lax.rsqrt(jnp.mean(values * values, axis=-1, keepdims=True) + 1e-05)


def attend(hidden, gains_row, prompt, history, recent, step_now):
    rows = hidden.shape[0]
    half = KV_HEADS * HEAD_DIM
    share = HEADS // KV_HEADS
    queries = (
        (normalize(hidden) * gains_row)
        .astype(jnp.bfloat16)
        .reshape(rows, KV_HEADS, share, HEAD_DIM)
    )
    prompt_keys = prompt[:, :half].reshape(-1, KV_HEADS, HEAD_DIM)
    prompt_vals = prompt[:, half:].reshape(-1, KV_HEADS, HEAD_DIM)
    past_keys = history[..., :half].reshape(rows, -1, KV_HEADS, HEAD_DIM)
    past_vals = history[..., half:].reshape(rows, -1, KV_HEADS, HEAD_DIM)
    recent_keys = recent[..., :half].reshape(-1, rows, KV_HEADS, HEAD_DIM)
    recent_vals = recent[..., half:].reshape(-1, rows, KV_HEADS, HEAD_DIM)
    score_scale = HEAD_DIM ** (-0.5)
    prompt_scores = (
        jnp.einsum("pkgd,nkd->pkgn", queries, prompt_keys, preferred_element_type=jnp.float32)
        * score_scale
    )
    past_scores = (
        jnp.einsum("pkgd,pnkd->pkgn", queries, past_keys, preferred_element_type=jnp.float32)
        * score_scale
    )
    recent_scores = (
        jnp.einsum("pkgd,npkd->pkgn", queries, recent_keys, preferred_element_type=jnp.float32)
        * score_scale
    )
    present = jnp.arange(recent.shape[0]) <= step_now
    recent_scores = jnp.where(present, recent_scores, NEG_FILL)
    highest = jnp.maximum(
        jnp.max(prompt_scores, -1, keepdims=True), jnp.max(past_scores, -1, keepdims=True)
    )
    highest = jnp.maximum(highest, jnp.max(recent_scores, -1, keepdims=True))
    prompt_exp = jnp.exp(prompt_scores - highest)
    past_exp = jnp.exp(past_scores - highest)
    recent_exp = jnp.exp(recent_scores - highest)
    denominator = (
        jnp.sum(prompt_exp, -1, keepdims=True)
        + jnp.sum(past_exp, -1, keepdims=True)
        + jnp.sum(recent_exp, -1, keepdims=True)
    )
    mixed = jnp.einsum(
        "pkgn,nkd->pkgd",
        (prompt_exp / denominator).astype(jnp.bfloat16),
        prompt_vals,
        preferred_element_type=jnp.float32,
    )
    mixed = mixed + jnp.einsum(
        "pkgn,pnkd->pkgd",
        (past_exp / denominator).astype(jnp.bfloat16),
        past_vals,
        preferred_element_type=jnp.float32,
    )
    mixed = mixed + jnp.einsum(
        "pkgn,npkd->pkgd",
        (recent_exp / denominator).astype(jnp.bfloat16),
        recent_vals,
        preferred_element_type=jnp.float32,
    )
    return mixed.reshape(rows, HEADS * HEAD_DIM)


def fork_cache(history, recent, ancestors, part_dev):
    shards = lax.axis_size("dp")
    own_index = lax.axis_index("dp")
    particle_cache = jnp.concatenate([history, jnp.transpose(recent, (1, 0, 2))], axis=1)
    owners = ancestors.reshape(shards, part_dev)
    picked = jnp.max(jnp.where(owners // part_dev == own_index, owners % part_dev, 0), axis=1)
    outgoing = jnp.take(particle_cache, picked, axis=0)
    incoming = lax.all_to_all(outgoing, "dp", split_axis=0, concat_axis=0, tiled=True)
    own_ancestors = lax.dynamic_slice_in_dim(ancestors, own_index * part_dev, part_dev)
    return jnp.take(incoming, own_ancestors // part_dev, axis=0)[None]


def local(token_states, norm_gains, prompt_kv, history_kv, new_kv, ancestors):
    section_count = lax.axis_size("section")
    section_index = lax.axis_index("section")
    part_dev = history_kv.shape[1]
    steps = new_kv.shape[1]
    model_width = token_states.shape[2]
    gains_row = norm_gains[0]
    prompt = prompt_kv[0]
    history = history_kv[0]
    recent = new_kv[0]
    groups = 1
    group_rows = part_dev // groups
    moments = steps * section_count + groups - 1

    def advance(moment, carry):
        arrived, outbuf = carry
        offset = moment - section_index
        step_raw = jnp.floor_divide(offset, section_count)
        group_raw = jnp.mod(offset, section_count)
        active = (offset >= 0) & (step_raw < steps) & (group_raw < groups)
        step_now = jnp.clip(step_raw, 0, steps - 1)
        group_now = jnp.clip(group_raw, 0, groups - 1)
        start = group_now * group_rows
        zero = jnp.zeros((), jnp.int32)
        token_rows = lax.dynamic_slice(
            token_states, (step_now, start, zero), (1, group_rows, model_width)
        )[0].astype(jnp.float32)
        carried = jnp.where(step_now > 0, normalize(arrived), 0.0)
        hidden = jnp.where(section_index == 0, token_rows + carried, arrived)
        mixed = attend(hidden, gains_row, prompt, history, recent, step_now)
        previous = lax.dynamic_slice(outbuf, (step_now, start, zero), (1, group_rows, model_width))
        written = jnp.where(active, mixed.astype(jnp.bfloat16)[None], previous)
        outbuf = lax.dynamic_update_slice(outbuf, written, (step_now, start, zero))
        passed = passed_along(hidden + mixed, "section", 1)
        return (passed, outbuf)

    start_carry = (
        jnp.zeros((group_rows, model_width), jnp.float32),
        jnp.zeros((steps, part_dev, model_width), jnp.bfloat16),
    )
    arrived, outbuf = lax.fori_loop(0, moments, advance, start_carry)
    forked_kv = fork_cache(history, recent, ancestors, part_dev)
    return (outbuf[None], forked_kv)


def solution(mesh):
    in_specs = (
        P(None, "dp", None),
        P("section", None),
        P("section", None, None),
        P("section", "dp", None, None),
        P("section", None, "dp", None),
        P(),
    )
    out_specs = (P("section", None, "dp", None), P("section", "dp", None, None))
    return jax.shard_map(local, mesh=mesh, in_specs=in_specs, out_specs=out_specs, check_vma=False)
```

profile of v0, /device:TPU:6, one launch (start us, length us, event | category | flops | bytes accessed | tf_op | source)
XLA Modules:
  0.0 965.0 jit_solution(10456727009098260094)
XLA Ops:
  5.6 5.3 gather_fusion
  10.9 7.5 broadcast_select_fusion
  18.4 14.8 %all-to-all-start = ((bf16[64,32,2048]{2,1,0:T(8,128)(2,1)}), bf16[64,32,2048]{2,1,0:T(8,128)(2,1)}, u32[]{:S(2)}, u32[]{:S(2)}) async-start(bf16[64,32,2048]{2,1,0:T(8,128)(2,1)} %broadcast_select_fusion), calls=%async_computation | async-start | bytes 16777216 | tf_op jit(solution)/shard_map/all_to_all | solution.py:94
  34.0 6.4 copy.118
  41.2 179.9 %all-to-all-done = bf16[64,32,2048]{2,1,0:T(8,128)(2,1)} async-done(((bf16[64,32,2048]{2,1,0:T(8,128)(2,1)}), bf16[64,32,2048]{2,1,0:T(8,128)(2,1)}, u32[]{:S(2)}, u32[]{:S(2)}) %all-to-all-start) | async-done | bytes 8388640 | tf_op jit(solution)/shard_map/all_to_all | solution.py:94
  221.0 5.4 gather_fusion.1
  226.4 3.2 bitcast_select_fusion
  230.7 734.3 %while.17 = (s32[]{:T(128)}, f32[16,8192]{1,0:T(8,128)S(1)}, bf16[4,16,8192]{2,1,0:T(8,128)(2,1)}, pred[]{:T(512)}, s32[]{:T(128)}, /*index=5*/bf16[4,16,8192]{2...) while((s32[]{:T(128)}, f32[16,8192]{1,0:T(8,128)S(1)}, ...), condition=%wide.region_9.10_spmd, body=%wide.region_0.9_spmd.sunk | while | flops 566855744 | bytes 50689240 | solution.py:139
  233.4 4.0 fusion.63
  252.8 3.1 fusion.67
  260.9 4.0 fusion.70
  270.0 6.6 collective-permute-done
  279.3 4.0 fusion.63
  298.7 3.1 fusion.67
  306.8 4.0 fusion.70
  315.9 6.6 collective-permute-done
  325.2 4.0 fusion.63
  344.6 3.1 fusion.67
  352.7 4.0 fusion.70
  361.8 6.6 collective-permute-done
  371.1 4.0 fusion.63
  390.5 3.1 fusion.67
  398.6 4.0 fusion.70
  407.7 6.6 collective-permute-done
  417.0 4.0 fusion.63
  436.4 3.1 fusion.67
  444.5 4.0 fusion.70
  453.6 6.6 collective-permute-done
  462.9 4.0 fusion.63
  482.3 3.1 fusion.67
  490.4 4.0 fusion.70
  499.4 6.6 collective-permute-done
  508.8 4.0 fusion.63
  536.3 4.0 fusion.70
  545.3 6.6 collective-permute-done
  554.7 4.0 fusion.63
  582.1 4.0 fusion.70
  591.2 6.6 collective-permute-done
  600.6 4.0 fusion.63
  628.0 4.0 fusion.70
  637.1 6.6 collective-permute-done
  646.5 4.0 fusion.63
  665.8 3.1 fusion.67
  673.9 4.0 fusion.70
  683.0 6.6 collective-permute-done
  692.4 4.0 fusion.63
  719.8 4.0 fusion.70
  728.9 6.6 collective-permute-done
  738.3 4.0 fusion.63
  765.7 4.0 fusion.70
  774.8 6.6 collective-permute-done
  784.1 4.0 fusion.63
  811.6 4.0 fusion.70
  820.7 6.6 collective-permute-done
  830.0 4.0 fusion.63
  857.5 4.0 fusion.70
  866.6 6.6 collective-permute-done
  875.9 4.0 fusion.63
  895.3 3.1 fusion.67
  903.4 4.0 fusion.70
  912.5 6.6 collective-permute-done
  921.8 4.0 fusion.63
  949.3 4.0 fusion.70
  958.4 6.6 collective-permute-done
  (759 shorter events, 480.1 us)
Async XLA Ops:
  18.4 202.7 %all-to-all-start = ((bf16[64,32,2048]{2,1,0:T(8,128)(2,1)}), bf16[64,32,2048]{2,1,0:T(8,128)(2,1)}, u32[]{:S(2)}, u32[]{:S(2)}) async-start(bf16[64,32,2048]{2,1,0:T(8,128)(2,1)} %broadcast_select_fusion), calls=%async_computation | async-start | bytes 16777216 | tf_op jit(solution)/shard_map/all_to_all | solution.py:94
  41.2 189.5 %copy-start = (bf16[1,16,28,2048]{3,1,2,0:T(8,128)(2,1)S(1)}, bf16[1,16,28,2048]{3,1,2,0:T(8,128)(2,1)}, u32[]{:S(2)}) copy-start(bf16[1,16,28,2048]{3,1,2,0:T(8,128)(2,1)} %param.11) | copy-start | bytes 5505028
  248.1 12.5 %copy-start.2 = (bf16[4,16,1024]{2,1,0:T(8,128)(2,1)S(1)}, bf16[4,16,1024]{2,1,0:T(8,128)(2,1)}, u32[]{:S(2)}) copy-start(bf16[4,16,1024]{2,1,0:T(8,128)(2,1)} %get-tuple-element.385) | copy-start | bytes 393220 | tf_op jit(solution)/shard_map/while
  260.9 4.0 copy-start.3
  260.9 4.4 copy-start.1
  267.9 8.7 collective-permute-start
  294.0 12.5 %copy-start.2 = (bf16[4,16,1024]{2,1,0:T(8,128)(2,1)S(1)}, bf16[4,16,1024]{2,1,0:T(8,128)(2,1)}, u32[]{:S(2)}) copy-start(bf16[4,16,1024]{2,1,0:T(8,128)(2,1)} %get-tuple-element.385) | copy-start | bytes 393220 | tf_op jit(solution)/shard_map/while
  306.8 4.0 copy-start.3
  306.8 4.4 copy-start.1
  313.8 8.7 collective-permute-start
  339.9 12.5 %copy-start.2 = (bf16[4,16,1024]{2,1,0:T(8,128)(2,1)S(1)}, bf16[4,16,1024]{2,1,0:T(8,128)(2,1)}, u32[]{:S(2)}) copy-start(bf16[4,16,1024]{2,1,0:T(8,128)(2,1)} %get-tuple-element.385) | copy-start | bytes 393220 | tf_op jit(solution)/shard_map/while
  352.7 4.0 copy-start.3
  352.7 4.4 copy-start.1
  359.7 8.7 collective-permute-start
  385.8 12.5 %copy-start.2 = (bf16[4,16,1024]{2,1,0:T(8,128)(2,1)S(1)}, bf16[4,16,1024]{2,1,0:T(8,128)(2,1)}, u32[]{:S(2)}) copy-start(bf16[4,16,1024]{2,1,0:T(8,128)(2,1)} %get-tuple-element.385) | copy-start | bytes 393220 | tf_op jit(solution)/shard_map/while
  398.5 4.0 copy-start.3
  398.6 4.4 copy-start.1
  405.6 8.7 collective-permute-start
  431.7 12.5 %copy-start.2 = (bf16[4,16,1024]{2,1,0:T(8,128)(2,1)S(1)}, bf16[4,16,1024]{2,1,0:T(8,128)(2,1)}, u32[]{:S(2)}) copy-start(bf16[4,16,1024]{2,1,0:T(8,128)(2,1)} %get-tuple-element.385) | copy-start | bytes 393220 | tf_op jit(solution)/shard_map/while
  444.4 4.0 copy-start.3
  444.5 4.4 copy-start.1
  451.5 8.7 collective-permute-start
  477.6 12.5 %copy-start.2 = (bf16[4,16,1024]{2,1,0:T(8,128)(2,1)S(1)}, bf16[4,16,1024]{2,1,0:T(8,128)(2,1)}, u32[]{:S(2)}) copy-start(bf16[4,16,1024]{2,1,0:T(8,128)(2,1)} %get-tuple-element.385) | copy-start | bytes 393220 | tf_op jit(solution)/shard_map/while
  490.3 4.0 copy-start.3
  490.4 4.4 copy-start.1
  497.4 8.7 collective-permute-start
  523.5 12.5 %copy-start.2 = (bf16[4,16,1024]{2,1,0:T(8,128)(2,1)S(1)}, bf16[4,16,1024]{2,1,0:T(8,128)(2,1)}, u32[]{:S(2)}) copy-start(bf16[4,16,1024]{2,1,0:T(8,128)(2,1)} %get-tuple-element.385) | copy-start | bytes 393220 | tf_op jit(solution)/shard_map/while
  536.2 4.4 copy-start.1
  543.3 8.7 collective-permute-start
  569.4 12.5 %copy-start.2 = (bf16[4,16,1024]{2,1,0:T(8,128)(2,1)S(1)}, bf16[4,16,1024]{2,1,0:T(8,128)(2,1)}, u32[]{:S(2)}) copy-start(bf16[4,16,1024]{2,1,0:T(8,128)(2,1)} %get-tuple-element.385) | copy-start | bytes 393220 | tf_op jit(solution)/shard_map/while
  582.1 4.0 copy-start.3
  582.1 4.4 copy-start.1
  589.2 8.7 collective-permute-start
  615.3 12.5 %copy-start.2 = (bf16[4,16,1024]{2,1,0:T(8,128)(2,1)S(1)}, bf16[4,16,1024]{2,1,0:T(8,128)(2,1)}, u32[]{:S(2)}) copy-start(bf16[4,16,1024]{2,1,0:T(8,128)(2,1)} %get-tuple-element.385) | copy-start | bytes 393220 | tf_op jit(solution)/shard_map/while
  628.0 4.0 copy-start.3
  628.0 4.4 copy-start.1
  635.1 8.7 collective-permute-start
  661.2 12.5 %copy-start.2 = (bf16[4,16,1024]{2,1,0:T(8,128)(2,1)S(1)}, bf16[4,16,1024]{2,1,0:T(8,128)(2,1)}, u32[]{:S(2)}) copy-start(bf16[4,16,1024]{2,1,0:T(8,128)(2,1)} %get-tuple-element.385) | copy-start | bytes 393220 | tf_op jit(solution)/shard_map/while
  673.9 4.0 copy-start.3
  673.9 4.4 copy-start.1
  681.0 8.7 collective-permute-start
  707.1 12.5 %copy-start.2 = (bf16[4,16,1024]{2,1,0:T(8,128)(2,1)S(1)}, bf16[4,16,1024]{2,1,0:T(8,128)(2,1)}, u32[]{:S(2)}) copy-start(bf16[4,16,1024]{2,1,0:T(8,128)(2,1)} %get-tuple-element.385) | copy-start | bytes 393220 | tf_op jit(solution)/shard_map/while
  719.8 4.0 copy-start.3
  719.8 4.4 copy-start.1
  726.9 8.7 collective-permute-start
  752.9 12.5 %copy-start.2 = (bf16[4,16,1024]{2,1,0:T(8,128)(2,1)S(1)}, bf16[4,16,1024]{2,1,0:T(8,128)(2,1)}, u32[]{:S(2)}) copy-start(bf16[4,16,1024]{2,1,0:T(8,128)(2,1)} %get-tuple-element.385) | copy-start | bytes 393220 | tf_op jit(solution)/shard_map/while
  765.7 4.0 copy-start.3
  765.7 4.4 copy-start.1
  772.8 8.7 collective-permute-start
  798.8 12.5 %copy-start.2 = (bf16[4,16,1024]{2,1,0:T(8,128)(2,1)S(1)}, bf16[4,16,1024]{2,1,0:T(8,128)(2,1)}, u32[]{:S(2)}) copy-start(bf16[4,16,1024]{2,1,0:T(8,128)(2,1)} %get-tuple-element.385) | copy-start | bytes 393220 | tf_op jit(solution)/shard_map/while
  811.6 4.0 copy-start.3
  811.6 4.4 copy-start.1
  818.7 8.7 collective-permute-start
  844.7 12.5 %copy-start.2 = (bf16[4,16,1024]{2,1,0:T(8,128)(2,1)S(1)}, bf16[4,16,1024]{2,1,0:T(8,128)(2,1)}, u32[]{:S(2)}) copy-start(bf16[4,16,1024]{2,1,0:T(8,128)(2,1)} %get-tuple-element.385) | copy-start | bytes 393220 | tf_op jit(solution)/shard_map/while
  857.5 4.4 copy-start.1
  864.5 8.7 collective-permute-start
  890.6 12.5 %copy-start.2 = (bf16[4,16,1024]{2,1,0:T(8,128)(2,1)S(1)}, bf16[4,16,1024]{2,1,0:T(8,128)(2,1)}, u32[]{:S(2)}) copy-start(bf16[4,16,1024]{2,1,0:T(8,128)(2,1)} %get-tuple-element.385) | copy-start | bytes 393220 | tf_op jit(solution)/shard_map/while
  903.4 4.0 copy-start.3
  903.4 4.4 copy-start.1
  910.4 8.7 collective-permute-start
  936.5 12.5 %copy-start.2 = (bf16[4,16,1024]{2,1,0:T(8,128)(2,1)S(1)}, bf16[4,16,1024]{2,1,0:T(8,128)(2,1)}, u32[]{:S(2)}) copy-start(bf16[4,16,1024]{2,1,0:T(8,128)(2,1)} %get-tuple-element.385) | copy-start | bytes 393220 | tf_op jit(solution)/shard_map/while
  949.3 4.0 copy-start.3
  949.3 4.4 copy-start.1
  956.3 8.7 collective-permute-start
  (18 other events, 72.8 us)
where the time goes:
time: 972 us; the launch traced here: 965 us
  waiting for transfers between devices  286 us (29%)
  local copies, waits for them, and re-layouts  247 us (25%)
  other arithmetic  218 us (22%)
  matrix products  194 us (20%)
  starting transfers between devices  16.1 us (2%)
    all_to_all x1, waiting for transfers between devices, fork_cache(): lax.all_to_all(outgoing, 'dp', split_axis=0, concat_axis=0, tiled=True)  180 us
    ppermute x16, waiting for transfers between devices, passed_along(): return lax.ppermute(block, axis, route)  106 us
    dot_general x16, matrix products, attend(): jnp.einsum('pkgn,nkd->pkgd', (prompt_exp / denominator).astype(jnp.bfloat...  64.2 us
    slice x16, local copies, waits for them, and re-layouts, attend(): prompt_vals = prompt[:, half:].reshape(-1, KV_HEADS, HEAD_DIM)  63.9 us
    reduce_sum x16, other arithmetic, attend(): jnp.sum(prompt_exp, -1, keepdims=True)  48.8 us
    dot_general x16, matrix products, attend(): jnp.einsum('pkgd,nkd->pkgn', queries, prompt_keys, preferred_element_type...  42.4 us
    dot_general x16, matrix products, attend(): jnp.einsum('pkgd,pnkd->pkgn', queries, past_keys, preferred_element_type=...  33.9 us
    dynamic_update_slice x16, other arithmetic, advance(): outbuf = lax.dynamic_update_slice(outbuf, written, (step_now, start, zero))  27.5 us
  transfers between devices with their start and end apart: 17, of which 17 were waited for; matrix products, arithmetic and copies ran while one was open for 4% of the time, Pallas kernels for 0%

commit v1 on v0

v1 whole, which is shorter than its diff:
```python
import jax
import jax.numpy as jnp
from jax import lax
from jax.experimental import pallas as pl
from jax.experimental.pallas import tpu as pltpu
from jax.sharding import PartitionSpec as P


HEADS = 64
KV_HEADS = 8
HEAD_DIM = 128


NEG_FILL = -1e30


def passed_along(block, axis, distance):
    devices = range(lax.axis_size(axis))
    route = [((i - distance) % len(devices), i) for i in devices]
    return lax.ppermute(block, axis, route)


def normalize(values):
    return values * lax.rsqrt(jnp.mean(values * values, axis=-1, keepdims=True) + 1e-05)


HEAD_BLOCK = 2
INTERPRET = False


def stage_kernel(tokens, hist, head_block):
    score_scale = HEAD_DIM ** (-0.5)

    def kernel(sc_ref, q_ref, pk_ref, pv_ref, ck_ref, cv_ref, o_ref):
        step_now = sc_ref[0]
        rows = q_ref.shape[1]
        width = ck_ref.shape[0]
        row_id = lax.broadcasted_iota(jnp.int32, (rows, width), 0)
        col_id = lax.broadcasted_iota(jnp.int32, (rows, width), 1)
        share = HEADS // KV_HEADS
        valid = (row_id // share == col_id // tokens) & (col_id % tokens < hist + 1 + step_now)
        for h in range(head_block):
            cols = slice(h * HEAD_DIM, (h + 1) * HEAD_DIM)
            q = q_ref[h]
            dims = (((1,), (1,)), ((), ()))
            prompt_scores = (
                lax.dot_general(q, pk_ref[:, cols], dims, preferred_element_type=jnp.float32)
                * score_scale
            )
            cache_scores = (
                lax.dot_general(q, ck_ref[:, cols], dims, preferred_element_type=jnp.float32)
                * score_scale
            )
            cache_scores = jnp.where(valid, cache_scores, NEG_FILL)
            highest = jnp.maximum(
                jnp.max(prompt_scores, -1, keepdims=True), jnp.max(cache_scores, -1, keepdims=True)
            )
            prompt_exp = jnp.exp(prompt_scores - highest)
            cache_exp = jnp.exp(cache_scores - highest)
            denominator = jnp.sum(prompt_exp, -1, keepdims=True) + jnp.sum(
                cache_exp, -1, keepdims=True
            )
            mixed = jnp.dot(
                (prompt_exp / denominator).astype(jnp.bfloat16),
                pv_ref[:, cols],
                preferred_element_type=jnp.float32,
            )
            mixed = mixed + jnp.dot(
                (cache_exp / denominator).astype(jnp.bfloat16),
                cv_ref[:, cols],
                preferred_element_type=jnp.float32,
            )
            o_ref[h] = mixed

    return kernel


def attend(hidden, gains_row, prompt, cache, step_now, group_now, hist_len, tokens):
    rows = hidden.shape[0]
    share = HEADS // KV_HEADS
    queries = (
        (normalize(hidden) * gains_row)
        .astype(jnp.bfloat16)
        .reshape(rows, KV_HEADS, share, HEAD_DIM)
        .transpose(1, 0, 2, 3)
        .reshape(KV_HEADS, rows * share, HEAD_DIM)
    )
    hb = HEAD_BLOCK
    nb = KV_HEADS // hb
    width = hb * HEAD_DIM
    scalars = jnp.stack([step_now, group_now]).astype(jnp.int32)
    grid_spec = pltpu.PrefetchScalarGridSpec(
        num_scalar_prefetch=1,
        grid=(nb,),
        in_specs=[
            pl.BlockSpec((hb, rows * share, HEAD_DIM), lambda i, sc: (i, 0, 0)),
            pl.BlockSpec((prompt.shape[0], width), lambda i, sc: (0, i)),
            pl.BlockSpec((prompt.shape[0], width), lambda i, sc: (0, i + nb)),
            pl.BlockSpec((rows * tokens, width), lambda i, sc: (sc[1], i)),
            pl.BlockSpec((rows * tokens, width), lambda i, sc: (sc[1], i + nb)),
        ],
        out_specs=pl.BlockSpec((hb, rows * share, HEAD_DIM), lambda i, sc: (i, 0, 0)),
    )
    mixed = pl.pallas_call(
        stage_kernel(tokens, hist_len, hb),
        grid_spec=grid_spec,
        out_shape=jax.ShapeDtypeStruct((KV_HEADS, rows * share, HEAD_DIM), jnp.float32),
        compiler_params=pltpu.CompilerParams(dimension_semantics=("arbitrary",)),
        interpret=INTERPRET,
    )(scalars, queries, prompt, prompt, cache, cache)
    return (
        mixed.reshape(KV_HEADS, rows, share, HEAD_DIM)
        .transpose(1, 0, 2, 3)
        .reshape(rows, HEADS * HEAD_DIM)
    )


def fork_cache(history, recent, ancestors, part_dev):
    shards = lax.axis_size("dp")
    own_index = lax.axis_index("dp")
    particle_cache = jnp.concatenate([history, jnp.transpose(recent, (1, 0, 2))], axis=1)
    owners = ancestors.reshape(shards, part_dev)
    picked = jnp.max(jnp.where(owners // part_dev == own_index, owners % part_dev, 0), axis=1)
    outgoing = jnp.take(particle_cache, picked, axis=0)
    incoming = lax.all_to_all(outgoing, "dp", split_axis=0, concat_axis=0, tiled=True)
    own_ancestors = lax.dynamic_slice_in_dim(ancestors, own_index * part_dev, part_dev)
    return jnp.take(incoming, own_ancestors // part_dev, axis=0)[None]


def local(token_states, norm_gains, prompt_kv, history_kv, new_kv, ancestors):
    section_count = lax.axis_size("section")
    section_index = lax.axis_index("section")
    part_dev = history_kv.shape[1]
    steps = new_kv.shape[1]
    model_width = token_states.shape[2]
    gains_row = norm_gains[0]
    prompt = prompt_kv[0]
    history = history_kv[0]
    recent = new_kv[0]
    cache = jnp.concatenate([history, jnp.transpose(recent, (1, 0, 2))], axis=1).reshape(
        -1, history.shape[2]
    )
    groups = 4
    group_rows = part_dev // groups
    moments = steps * section_count + groups - 1

    def advance(moment, carry):
        arrived, outbuf = carry
        offset = moment - section_index
        step_raw = jnp.floor_divide(offset, section_count)
        group_raw = jnp.mod(offset, section_count)
        active = (offset >= 0) & (step_raw < steps) & (group_raw < groups)
        step_now = jnp.clip(step_raw, 0, steps - 1)
        group_now = jnp.clip(group_raw, 0, groups - 1)
        start = group_now * group_rows
        zero = jnp.zeros((), jnp.int32)
        token_rows = lax.dynamic_slice(
            token_states, (step_now, start, zero), (1, group_rows, model_width)
        )[0].astype(jnp.float32)
        carried = jnp.where(step_now > 0, normalize(arrived), 0.0)
        hidden = jnp.where(section_index == 0, token_rows + carried, arrived)
        mixed = attend(
            hidden, gains_row, prompt, cache, step_now, group_now, history.shape[1], history.shape[1] + steps
        )
        previous = lax.dynamic_slice(outbuf, (step_now, start, zero), (1, group_rows, model_width))
        written = jnp.where(active, mixed.astype(jnp.bfloat16)[None], previous)
        outbuf = lax.dynamic_update_slice(outbuf, written, (step_now, start, zero))
        passed = passed_along(hidden + mixed, "section", 1)
        return (passed, outbuf)

    start_carry = (
        jnp.zeros((group_rows, model_width), jnp.float32),
        jnp.zeros((steps, part_dev, model_width), jnp.bfloat16),
    )
    forked_kv = fork_cache(history, recent, ancestors, part_dev)
    _, outbuf = lax.fori_loop(0, moments, advance, start_carry)
    return (outbuf[None], forked_kv)


def solution(mesh):
    in_specs = (
        P(None, "dp", None),
        P("section", None),
        P("section", None, None),
        P("section", "dp", None, None),
        P("section", None, "dp", None),
        P(),
    )
    out_specs = (P("section", None, "dp", None), P("section", "dp", None, None))
    return jax.shard_map(local, mesh=mesh, in_specs=in_specs, out_specs=out_specs, check_vma=False)
```

time: 972 us -> 538 us (0.55)
  local copies, waits for them, and re-layouts: 247 us -> 46.1 us
  matrix products: 194 us -> 0 us
  Pallas kernels: 0 us -> 132 us
  other arithmetic: 218 us -> 86.5 us
  waiting for transfers between devices: 286 us -> 250 us
    dot_general x96 -> x0, matrix products: 194 us -> none  [the longest x16 64.2 us: attend(): jnp.einsum('pkgn,nkd->pkgd', (prompt_exp / denominator).astype(jnp.bfloat...]
    pallas_call x0 -> x19, Pallas kernels: none -> 132 us  [attend(): pl.pallas_call(stage_kernel(tokens, hist_len, hb), grid_spec=grid_spec, o...]
    slice x48 -> x0, local copies, waits for them, and re-layouts: 92.2 us -> none  [the longest x16 63.9 us: attend(): prompt_vals = prompt[:, half:].reshape(-1, KV_HEADS, HEAD_DIM)]
    reduce_sum x48 -> x0, other arithmetic: 90.6 us -> none  [the longest x16 48.8 us: attend(): jnp.sum(prompt_exp, -1, keepdims=True)]
    reduce_max x48 -> x0, local copies, waits for them, and re-layouts: 50.6 us -> none  [the longest x16 24.4 us: attend(): jnp.max(past_scores, -1, keepdims=True)]
    ppermute x16 -> x19, waiting for transfers between devices: 106 us -> 62.6 us  [passed_along(): return lax.ppermute(block, axis, route)]
    reduce_sum x48 -> x0, local copies, waits for them, and re-layouts: 33.2 us -> none  [the longest x16 11.1 us: attend(): jnp.sum(recent_exp, -1, keepdims=True)]
    dynamic_update_slice x16 -> x19, other arithmetic: 27.5 us -> 1.62 us  [advance(): outbuf = lax.dynamic_update_slice(outbuf, written, (step_now, start, zero))]
  transfers between devices with their start and end apart: 17 -> 20, of which waited for: 17 -> 20; matrix products, arithmetic and copies ran while one was open for 4% -> 4% of each run, Pallas kernels for 0% -> 0%
where the time goes in v1:
time: 538 us; the launch traced here: 533 us
  waiting for transfers between devices  250 us (46%)
  Pallas kernels  132 us (25%)
  other arithmetic  86.5 us (16%)
  local copies, waits for them, and re-layouts  46.1 us (9%)
  starting transfers between devices  16.4 us (3%)
    all_to_all x1, waiting for transfers between devices, fork_cache(): lax.all_to_all(outgoing, 'dp', split_axis=0, concat_axis=0, tiled=True)  187 us
    pallas_call x19, Pallas kernels, attend(): pl.pallas_call(stage_kernel(tokens, hist_len, hb), grid_spec=grid_spec, o...  132 us
    ppermute x19, waiting for transfers between devices, passed_along(): return lax.ppermute(block, axis, route)  62.6 us
    reduce_sum x38, other arithmetic, normalize(): jnp.mean(values * values, axis=-1, keepdims=True) + 1e-05  25.5 us
    convert_element_type x19, other arithmetic, advance(): written = jnp.where(active, mixed.astype(jnp.bfloat16)[None], previous)  17.4 us
    while x19, local copies, waits for them, and re-layouts  17.3 us
    while x19, other arithmetic  16.4 us
    all_to_all x1, starting transfers between devices, fork_cache(): lax.all_to_all(outgoing, 'dp', split_axis=0, concat_axis=0, tiled=True)  14.8 us
  transfers between devices with their start and end apart: 20, of which 20 were waited for; matrix products, arithmetic and copies ran while one was open for 4% of the time, Pallas kernels for 0%

profile of v1, /device:TPU:6, one launch (start us, length us, event | category | flops | bytes accessed | tf_op | source)
XLA Modules:
  0.0 533.3 jit_solution(4642697823387339480)
XLA Ops:
  2.7 2.5 copy.26
  5.6 5.3 gather_fusion
  10.9 7.5 %broadcast_select_fusion = bf16[64,32,2048]{2,1,0:T(8,128)(2,1)} fusion(bf16[64,32,2048]{2,1,0:T(8,128)(2,1)} %gather_fusion, pred[64]{0:T(512)(128)(4,1)S(1)} %compare_and_fusion), kind=kLoop, calls=%fused_computation.17 | loop fusion | flops 4194304 | bytes 16777280 | tf_op jit(solution)/shard_map/jit(_take)/select_n | solution.py:124
  18.3 14.8 %all-to-all-start = ((bf16[64,32,2048]{2,1,0:T(8,128)(2,1)}), bf16[64,32,2048]{2,1,0:T(8,128)(2,1)}, u32[]{:S(2)}, u32[]{:S(2)}) async-start(bf16[64,32,2048]{2,1,0:T(8,128)(2,1)} %broadcast_select_fusion), calls=%async_computation | async-start | bytes 16777216 | tf_op jit(solution)/shard_map/all_to_all | solution.py:125
  33.9 187.1 %all-to-all-done = bf16[64,32,2048]{2,1,0:T(8,128)(2,1)} async-done(((bf16[64,32,2048]{2,1,0:T(8,128)(2,1)}), bf16[64,32,2048]{2,1,0:T(8,128)(2,1)}, u32[]{:S(2)}, u32[]{:S(2)}) %all-to-all-start) | async-done | bytes 8388640 | tf_op jit(solution)/shard_map/all_to_all | solution.py:125
  221.0 5.4 %gather_fusion.1 = bf16[16,32,2048]{2,1,0:T(8,128)(2,1)} fusion(bf16[64,32,2048]{2,1,0:T(8,128)(2,1)} %all-to-all-done, s32[1024]{0:T(1024)S(1)} %pad_clamp_fusion), kind=kCustom, calls=%fused_computation.1 | custom fusion | bytes 4194368 | tf_op jit(solution)/shard_map/jit(_take)/gather | solution.py:127
  226.4 3.2 bitcast_select_fusion
  229.7 302.7 %while.17 = (s32[]{:T(128)}, f32[4,8192]{1,0:T(4,128)S(1)}, bf16[4,16,8192]{2,1,0:T(8,128)(2,1)S(1)}, pred[]{:T(512)}, s32[]{:T(128)}, /*index=5*/bf16[4,16,8192...) while((s32[]{:T(128)}, f32[4,8192]{1,0:T(4,128)S(1)}, ...), condition=%wide.region_3.4_spmd, body=%wide.region_0.3_spmd.sunk | while | flops 491566 | bytes 2654895 | solution.py:176
  230.0 1.2 multiply_reduce_fusion.5
  233.2 6.9 %eval_jaxpr.8 = f32[8,32,128]{2,1,0:T(8,128)} custom-call(s32[2]{0:T(128)} %pad_add_fusion.2.sc_ref, bf16[8,32,128]{2,1,0:T(8,128)(2,1)} %copy_bitcast_fusion.10.q_ref, bf16[1024,2048]{1,0:T(8,128)(2,1)} %get-tuple-element.326.pk_ref.pv_ref, bf16[1024,2048]{1,0:T(8,128)(2,1)} %get-tuple-element.326.pk_ref.pv_ref, ...), custom_call_target="tpu_custom_call" | custom-call | tf_op jit(solution)/shard_map/while/body/eval_jaxpr/pallas_call | solution.py:104
  242.4 3.3 collective-permute-done
  245.9 1.2 multiply_reduce_fusion.5
  249.2 6.9 %eval_jaxpr.8 = f32[8,32,128]{2,1,0:T(8,128)} custom-call(s32[2]{0:T(128)} %pad_add_fusion.2.sc_ref, bf16[8,32,128]{2,1,0:T(8,128)(2,1)} %copy_bitcast_fusion.10.q_ref, bf16[1024,2048]{1,0:T(8,128)(2,1)} %get-tuple-element.326.pk_ref.pv_ref, bf16[1024,2048]{1,0:T(8,128)(2,1)} %get-tuple-element.326.pk_ref.pv_ref, ...), custom_call_target="tpu_custom_call" | custom-call | tf_op jit(solution)/shard_map/while/body/eval_jaxpr/pallas_call | solution.py:104
  258.3 3.3 collective-permute-done
  261.8 1.2 multiply_reduce_fusion.5
  265.1 6.9 %eval_jaxpr.8 = f32[8,32,128]{2,1,0:T(8,128)} custom-call(s32[2]{0:T(128)} %pad_add_fusion.2.sc_ref, bf16[8,32,128]{2,1,0:T(8,128)(2,1)} %copy_bitcast_fusion.10.q_ref, bf16[1024,2048]{1,0:T(8,128)(2,1)} %get-tuple-element.326.pk_ref.pv_ref, bf16[1024,2048]{1,0:T(8,128)(2,1)} %get-tuple-element.326.pk_ref.pv_ref, ...), custom_call_target="tpu_custom_call" | custom-call | tf_op jit(solution)/shard_map/while/body/eval_jaxpr/pallas_call | solution.py:104
  274.2 3.3 collective-permute-done
  277.7 1.2 multiply_reduce_fusion.5
  281.0 6.9 %eval_jaxpr.8 = f32[8,32,128]{2,1,0:T(8,128)} custom-call(s32[2]{0:T(128)} %pad_add_fusion.2.sc_ref, bf16[8,32,128]{2,1,0:T(8,128)(2,1)} %copy_bitcast_fusion.10.q_ref, bf16[1024,2048]{1,0:T(8,128)(2,1)} %get-tuple-element.326.pk_ref.pv_ref, bf16[1024,2048]{1,0:T(8,128)(2,1)} %get-tuple-element.326.pk_ref.pv_ref, ...), custom_call_target="tpu_custom_call" | custom-call | tf_op jit(solution)/shard_map/while/body/eval_jaxpr/pallas_call | solution.py:104
  290.2 3.3 collective-permute-done
  293.7 1.2 multiply_reduce_fusion.5
  296.9 6.9 %eval_jaxpr.8 = f32[8,32,128]{2,1,0:T(8,128)} custom-call(s32[2]{0:T(128)} %pad_add_fusion.2.sc_ref, bf16[8,32,128]{2,1,0:T(8,128)(2,1)} %copy_bitcast_fusion.10.q_ref, bf16[1024,2048]{1,0:T(8,128)(2,1)} %get-tuple-element.326.pk_ref.pv_ref, bf16[1024,2048]{1,0:T(8,128)(2,1)} %get-tuple-element.326.pk_ref.pv_ref, ...), custom_call_target="tpu_custom_call" | custom-call | tf_op jit(solution)/shard_map/while/body/eval_jaxpr/pallas_call | solution.py:104
  306.1 3.3 collective-permute-done
  309.6 1.2 multiply_reduce_fusion.5
  312.9 6.9 %eval_jaxpr.8 = f32[8,32,128]{2,1,0:T(8,128)} custom-call(s32[2]{0:T(128)} %pad_add_fusion.2.sc_ref, bf16[8,32,128]{2,1,0:T(8,128)(2,1)} %copy_bitcast_fusion.10.q_ref, bf16[1024,2048]{1,0:T(8,128)(2,1)} %get-tuple-element.326.pk_ref.pv_ref, bf16[1024,2048]{1,0:T(8,128)(2,1)} %get-tuple-element.326.pk_ref.pv_ref, ...), custom_call_target="tpu_custom_call" | custom-call | tf_op jit(solution)/shard_map/while/body/eval_jaxpr/pallas_call | solution.py:104
  322.0 3.3 collective-permute-done
  325.5 1.2 multiply_reduce_fusion.5
  328.8 6.9 %eval_jaxpr.8 = f32[8,32,128]{2,1,0:T(8,128)} custom-call(s32[2]{0:T(128)} %pad_add_fusion.2.sc_ref, bf16[8,32,128]{2,1,0:T(8,128)(2,1)} %copy_bitcast_fusion.10.q_ref, bf16[1024,2048]{1,0:T(8,128)(2,1)} %get-tuple-element.326.pk_ref.pv_ref, bf16[1024,2048]{1,0:T(8,128)(2,1)} %get-tuple-element.326.pk_ref.pv_ref, ...), custom_call_target="tpu_custom_call" | custom-call | tf_op jit(solution)/shard_map/while/body/eval_jaxpr/pallas_call | solution.py:104
  337.9 3.3 collective-permute-done
  341.5 1.2 multiply_reduce_fusion.5
  344.7 6.9 %eval_jaxpr.8 = f32[8,32,128]{2,1,0:T(8,128)} custom-call(s32[2]{0:T(128)} %pad_add_fusion.2.sc_ref, bf16[8,32,128]{2,1,0:T(8,128)(2,1)} %copy_bitcast_fusion.10.q_ref, bf16[1024,2048]{1,0:T(8,128)(2,1)} %get-tuple-element.326.pk_ref.pv_ref, bf16[1024,2048]{1,0:T(8,128)(2,1)} %get-tuple-element.326.pk_ref.pv_ref, ...), custom_call_target="tpu_custom_call" | custom-call | tf_op jit(solution)/shard_map/while/body/eval_jaxpr/pallas_call | solution.py:104
  353.9 3.3 collective-permute-done
  357.4 1.2 multiply_reduce_fusion.5
  360.7 6.9 %eval_jaxpr.8 = f32[8,32,128]{2,1,0:T(8,128)} custom-call(s32[2]{0:T(128)} %pad_add_fusion.2.sc_ref, bf16[8,32,128]{2,1,0:T(8,128)(2,1)} %copy_bitcast_fusion.10.q_ref, bf16[1024,2048]{1,0:T(8,128)(2,1)} %get-tuple-element.326.pk_ref.pv_ref, bf16[1024,2048]{1,0:T(8,128)(2,1)} %get-tuple-element.326.pk_ref.pv_ref, ...), custom_call_target="tpu_custom_call" | custom-call | tf_op jit(solution)/shard_map/while/body/eval_jaxpr/pallas_call | solution.py:104
  369.8 3.3 collective-permute-done
  373.3 1.2 multiply_reduce_fusion.5
  376.6 6.9 %eval_jaxpr.8 = f32[8,32,128]{2,1,0:T(8,128)} custom-call(s32[2]{0:T(128)} %pad_add_fusion.2.sc_ref, bf16[8,32,128]{2,1,0:T(8,128)(2,1)} %copy_bitcast_fusion.10.q_ref, bf16[1024,2048]{1,0:T(8,128)(2,1)} %get-tuple-element.326.pk_ref.pv_ref, bf16[1024,2048]{1,0:T(8,128)(2,1)} %get-tuple-element.326.pk_ref.pv_ref, ...), custom_call_target="tpu_custom_call" | custom-call | tf_op jit(solution)/shard_map/while/body/eval_jaxpr/pallas_call | solution.py:104
  385.7 3.3 collective-permute-done
  389.2 1.2 multiply_reduce_fusion.5
  392.5 6.9 %eval_jaxpr.8 = f32[8,32,128]{2,1,0:T(8,128)} custom-call(s32[2]{0:T(128)} %pad_add_fusion.2.sc_ref, bf16[8,32,128]{2,1,0:T(8,128)(2,1)} %copy_bitcast_fusion.10.q_ref, bf16[1024,2048]{1,0:T(8,128)(2,1)} %get-tuple-element.326.pk_ref.pv_ref, bf16[1024,2048]{1,0:T(8,128)(2,1)} %get-tuple-element.326.pk_ref.pv_ref, ...), custom_call_target="tpu_custom_call" | custom-call | tf_op jit(solution)/shard_map/while/body/eval_jaxpr/pallas_call | solution.py:104
  401.6 3.3 collective-permute-done
  405.2 1.2 multiply_reduce_fusion.5
  408.4 6.9 %eval_jaxpr.8 = f32[8,32,128]{2,1,0:T(8,128)} custom-call(s32[2]{0:T(128)} %pad_add_fusion.2.sc_ref, bf16[8,32,128]{2,1,0:T(8,128)(2,1)} %copy_bitcast_fusion.10.q_ref, bf16[1024,2048]{1,0:T(8,128)(2,1)} %get-tuple-element.326.pk_ref.pv_ref, bf16[1024,2048]{1,0:T(8,128)(2,1)} %get-tuple-element.326.pk_ref.pv_ref, ...), custom_call_target="tpu_custom_call" | custom-call | tf_op jit(solution)/shard_map/while/body/eval_jaxpr/pallas_call | solution.py:104
  417.6 3.3 collective-permute-done
  421.1 1.2 multiply_reduce_fusion.5
  424.4 6.9 %eval_jaxpr.8 = f32[8,32,128]{2,1,0:T(8,128)} custom-call(s32[2]{0:T(128)} %pad_add_fusion.2.sc_ref, bf16[8,32,128]{2,1,0:T(8,128)(2,1)} %copy_bitcast_fusion.10.q_ref, bf16[1024,2048]{1,0:T(8,128)(2,1)} %get-tuple-element.326.pk_ref.pv_ref, bf16[1024,2048]{1,0:T(8,128)(2,1)} %get-tuple-element.326.pk_ref.pv_ref, ...), custom_call_target="tpu_custom_call" | custom-call | tf_op jit(solution)/shard_map/while/body/eval_jaxpr/pallas_call | solution.py:104
  433.5 3.3 collective-permute-done
  437.0 1.2 multiply_reduce_fusion.5
  440.3 6.9 %eval_jaxpr.8 = f32[8,32,128]{2,1,0:T(8,128)} custom-call(s32[2]{0:T(128)} %pad_add_fusion.2.sc_ref, bf16[8,32,128]{2,1,0:T(8,128)(2,1)} %copy_bitcast_fusion.10.q_ref, bf16[1024,2048]{1,0:T(8,128)(2,1)} %get-tuple-element.326.pk_ref.pv_ref, bf16[1024,2048]{1,0:T(8,128)(2,1)} %get-tuple-element.326.pk_ref.pv_ref, ...), custom_call_target="tpu_custom_call" | custom-call | tf_op jit(solution)/shard_map/while/body/eval_jaxpr/pallas_call | solution.py:104
  449.4 3.3 collective-permute-done
  453.0 1.2 multiply_reduce_fusion.5
  456.2 6.9 %eval_jaxpr.8 = f32[8,32,128]{2,1,0:T(8,128)} custom-call(s32[2]{0:T(128)} %pad_add_fusion.2.sc_ref, bf16[8,32,128]{2,1,0:T(8,128)(2,1)} %copy_bitcast_fusion.10.q_ref, bf16[1024,2048]{1,0:T(8,128)(2,1)} %get-tuple-element.326.pk_ref.pv_ref, bf16[1024,2048]{1,0:T(8,128)(2,1)} %get-tuple-element.326.pk_ref.pv_ref, ...), custom_call_target="tpu_custom_call" | custom-call | tf_op jit(solution)/shard_map/while/body/eval_jaxpr/pallas_call | solution.py:104
  465.4 3.3 collective-permute-done
  472.2 6.9 %eval_jaxpr.8 = f32[8,32,128]{2,1,0:T(8,128)} custom-call(s32[2]{0:T(128)} %pad_add_fusion.2.sc_ref, bf16[8,32,128]{2,1,0:T(8,128)(2,1)} %copy_bitcast_fusion.10.q_ref, bf16[1024,2048]{1,0:T(8,128)(2,1)} %get-tuple-element.326.pk_ref.pv_ref, bf16[1024,2048]{1,0:T(8,128)(2,1)} %get-tuple-element.326.pk_ref.pv_ref, ...), custom_call_target="tpu_custom_call" | custom-call | tf_op jit(solution)/shard_map/while/body/eval_jaxpr/pallas_call | solution.py:104
  481.3 3.3 collective-permute-done
  484.8 1.2 multiply_reduce_fusion.5
  488.1 6.9 %eval_jaxpr.8 = f32[8,32,128]{2,1,0:T(8,128)} custom-call(s32[2]{0:T(128)} %pad_add_fusion.2.sc_ref, bf16[8,32,128]{2,1,0:T(8,128)(2,1)} %copy_bitcast_fusion.10.q_ref, bf16[1024,2048]{1,0:T(8,128)(2,1)} %get-tuple-element.326.pk_ref.pv_ref, bf16[1024,2048]{1,0:T(8,128)(2,1)} %get-tuple-element.326.pk_ref.pv_ref, ...), custom_call_target="tpu_custom_call" | custom-call | tf_op jit(solution)/shard_map/while/body/eval_jaxpr/pallas_call | solution.py:104
  497.2 3.3 collective-permute-done
  500.7 1.2 multiply_reduce_fusion.5
  504.0 6.9 %eval_jaxpr.8 = f32[8,32,128]{2,1,0:T(8,128)} custom-call(s32[2]{0:T(128)} %pad_add_fusion.2.sc_ref, bf16[8,32,128]{2,1,0:T(8,128)(2,1)} %copy_bitcast_fusion.10.q_ref, bf16[1024,2048]{1,0:T(8,128)(2,1)} %get-tuple-element.326.pk_ref.pv_ref, bf16[1024,2048]{1,0:T(8,128)(2,1)} %get-tuple-element.326.pk_ref.pv_ref, ...), custom_call_target="tpu_custom_call" | custom-call | tf_op jit(solution)/shard_map/while/body/eval_jaxpr/pallas_call | solution.py:104
  513.1 3.3 collective-permute-done
  516.7 1.2 multiply_reduce_fusion.5
  519.9 6.9 %eval_jaxpr.8 = f32[8,32,128]{2,1,0:T(8,128)} custom-call(s32[2]{0:T(128)} %pad_add_fusion.2.sc_ref, bf16[8,32,128]{2,1,0:T(8,128)(2,1)} %copy_bitcast_fusion.10.q_ref, bf16[1024,2048]{1,0:T(8,128)(2,1)} %get-tuple-element.326.pk_ref.pv_ref, bf16[1024,2048]{1,0:T(8,128)(2,1)} %get-tuple-element.326.pk_ref.pv_ref, ...), custom_call_target="tpu_custom_call" | custom-call | tf_op jit(solution)/shard_map/while/body/eval_jaxpr/pallas_call | solution.py:104
  529.1 3.3 collective-permute-done
  (261 shorter events, 89.5 us)
Async XLA Ops:
  18.3 202.7 %all-to-all-start = ((bf16[64,32,2048]{2,1,0:T(8,128)(2,1)}), bf16[64,32,2048]{2,1,0:T(8,128)(2,1)}, u32[]{:S(2)}, u32[]{:S(2)}) async-start(bf16[64,32,2048]{2,1,0:T(8,128)(2,1)} %broadcast_select_fusion), calls=%async_computation | async-start | bytes 16777216 | tf_op jit(solution)/shard_map/all_to_all | solution.py:125
  241.2 4.5 collective-permute-start
  257.1 4.5 collective-permute-start
  273.0 4.5 collective-permute-start
  289.0 4.5 collective-permute-start
  304.9 4.5 collective-permute-start
  320.8 4.5 collective-permute-start
  336.8 4.5 collective-permute-start
  352.7 4.5 collective-permute-start
  368.6 4.5 collective-permute-start
  384.5 4.5 collective-permute-start
  400.5 4.5 collective-permute-start
  416.4 4.5 collective-permute-start
  432.3 4.5 collective-permute-start
  448.3 4.5 collective-permute-start
  464.2 4.5 collective-permute-start
  480.1 4.5 collective-permute-start
  496.0 4.5 collective-permute-start
  512.0 4.5 collective-permute-start
  527.9 4.5 collective-permute-start
  532.4 1.0 copy-start

commit v2 on v1

--- a/solution.py
+++ b/solution.py
@@ -28,28 +28,42 @@
 INTERPRET = False
 
 
-def stage_kernel(tokens, hist, head_block):
+def stage_kernel(rows, tokens, hist, head_block):
     score_scale = HEAD_DIM ** (-0.5)
-
-    def kernel(sc_ref, q_ref, pk_ref, pv_ref, ck_ref, cv_ref, o_ref):
+    share = HEADS // KV_HEADS
+    group_width = share * HEAD_DIM
+
+    def kernel(
+        sc_ref, arr_ref, tok_ref, gain_ref, pk_ref, pv_ref, ck_ref, cv_ref,
+        res_ref, att_ref, hid_ref, q_ref,
+    ):
+        block = pl.program_id(0)
+
+        @pl.when(block == 0)
+        def _():
+            arrived = arr_ref[...]
+            carried = jnp.where(sc_ref[3] > 0, normalize(arrived), 0.0)
+            hidden = jnp.where(sc_ref[2] > 0, tok_ref[...].astype(jnp.float32) + carried, arrived)
+            queries = (normalize(hidden) * gain_ref[...]).astype(jnp.float32)
+            for k in range(KV_HEADS):
+                cols = slice(k * group_width, (k + 1) * group_width)
+                hid_ref[k] = hidden[:, cols]
+                q_ref[k] = queries[:, cols].reshape(rows * share, HEAD_DIM)
+
         step_now = sc_ref[0]
-        rows = q_ref.shape[1]
-        width = ck_ref.shape[0]
-        row_id = lax.broadcasted_iota(jnp.int32, (rows, width), 0)
-        col_id = lax.broadcasted_iota(jnp.int32, (rows, width), 1)
-        share = HEADS // KV_HEADS
+        width = ck_ref.shape[1]
+        row_id = lax.broadcasted_iota(jnp.int32, (rows * share, width), 0)
+        col_id = lax.broadcasted_iota(jnp.int32, (rows * share, width), 1)
         valid = (row_id // share == col_id // tokens) & (col_id % tokens < hist + 1 + step_now)
         for h in range(head_block):
+            head = block * head_block + h
             cols = slice(h * HEAD_DIM, (h + 1) * HEAD_DIM)
-            q = q_ref[h]
-            dims = (((1,), (1,)), ((), ()))
+            q = q_ref[head].astype(jnp.bfloat16)
             prompt_scores = (
-                lax.dot_general(q, pk_ref[:, cols], dims, preferred_element_type=jnp.float32)
-                * score_scale
+                jnp.dot(q, pk_ref[cols, :], preferred_element_type=jnp.float32) * score_scale
             )
             cache_scores = (
-                lax.dot_general(q, ck_ref[:, cols], dims, preferred_element_type=jnp.float32)
-                * score_scale
+                jnp.dot(q, ck_ref[cols, :], preferred_element_type=jnp.float32) * score_scale
             )
             cache_scores = jnp.where(valid, cache_scores, NEG_FILL)
             highest = jnp.maximum(
@@ -70,49 +84,52 @@
                 cv_ref[:, cols],
                 preferred_element_type=jnp.float32,
             )
-            o_ref[h] = mixed
+            mixed = mixed.reshape(rows, group_width)
+            out_cols = slice(h * group_width, (h + 1) * group_width)
+            res_ref[:, out_cols] = hid_ref[head] + mixed
+            att_ref[:, out_cols] = mixed.astype(jnp.bfloat16)
 
     return kernel
 
 
-def attend(hidden, gains_row, prompt, cache, step_now, group_now, hist_len, tokens):
-    rows = hidden.shape[0]
+def stage(scalars, arrived, grouped_tokens, gains, prompt_keys_t, prompt, cache_keys_t, cache, hist_len):
+    rows, model_width = arrived.shape
     share = HEADS // KV_HEADS
-    queries = (
-        (normalize(hidden) * gains_row)
-        .astype(jnp.bfloat16)
-        .reshape(rows, KV_HEADS, share, HEAD_DIM)
-        .transpose(1, 0, 2, 3)
-        .reshape(KV_HEADS, rows * share, HEAD_DIM)
-    )
+    tokens = cache.shape[0] // (grouped_tokens.shape[1] * rows)
     hb = HEAD_BLOCK
     nb = KV_HEADS // hb
     width = hb * HEAD_DIM
-    scalars = jnp.stack([step_now, group_now]).astype(jnp.int32)
     grid_spec = pltpu.PrefetchScalarGridSpec(
         num_scalar_prefetch=1,
         grid=(nb,),
         in_specs=[
-            pl.BlockSpec((hb, rows * share, HEAD_DIM), lambda i, sc: (i, 0, 0)),
-            pl.BlockSpec((prompt.shape[0], width), lambda i, sc: (0, i)),
+            pl.BlockSpec((rows, model_width), lambda i, sc: (0, 0)),
+            pl.BlockSpec((None, None, rows, model_width), lambda i, sc: (sc[0], sc[1], 0, 0)),
+            pl.BlockSpec((1, model_width), lambda i, sc: (0, 0)),
+            pl.BlockSpec((width, prompt_keys_t.shape[1]), lambda i, sc: (i, 0)),
             pl.BlockSpec((prompt.shape[0], width), lambda i, sc: (0, i + nb)),
-            pl.BlockSpec((rows * tokens, width), lambda i, sc: (sc[1], i)),
+            pl.BlockSpec((width, rows * tokens), lambda i, sc: (i, sc[1])),
             pl.BlockSpec((rows * tokens, width), lambda i, sc: (sc[1], i + nb)),
         ],
-        out_specs=pl.BlockSpec((hb, rows * share, HEAD_DIM), lambda i, sc: (i, 0, 0)),
-    )
-    mixed = pl.pallas_call(
-        stage_kernel(tokens, hist_len, hb),
+        out_specs=[
+            pl.BlockSpec((rows, hb * share * HEAD_DIM), lambda i, sc: (0, i)),
+            pl.BlockSpec((rows, hb * share * HEAD_DIM), lambda i, sc: (0, i)),
+        ],
+        scratch_shapes=[
+            pltpu.VMEM((KV_HEADS, rows, share * HEAD_DIM), jnp.float32),
+            pltpu.VMEM((KV_HEADS, rows * share, HEAD_DIM), jnp.float32),
+        ],
+    )
+    return pl.pallas_call(
+        stage_kernel(rows, tokens, hist_len, hb),
         grid_spec=grid_spec,
-        out_shape=jax.ShapeDtypeStruct((KV_HEADS, rows * share, HEAD_DIM), jnp.float32),
+        out_shape=[
+            jax.ShapeDtypeStruct((rows, model_width), jnp.float32),
+            jax.ShapeDtypeStruct((rows, model_width), jnp.bfloat16),
+        ],
         compiler_params=pltpu.CompilerParams(dimension_semantics=("arbitrary",)),
         interpret=INTERPRET,
-    )(scalars, queries, prompt, prompt, cache, cache)
-    return (
-        mixed.reshape(KV_HEADS, rows, share, HEAD_DIM)
-        .transpose(1, 0, 2, 3)
-        .reshape(rows, HEADS * HEAD_DIM)
-    )
+    )(scalars, arrived, grouped_tokens, gains, prompt_keys_t, prompt, cache_keys_t, cache)
 
 
 def fork_cache(history, recent, ancestors, part_dev):
@@ -133,15 +150,19 @@
     part_dev = history_kv.shape[1]
     steps = new_kv.shape[1]
     model_width = token_states.shape[2]
-    gains_row = norm_gains[0]
+    half = KV_HEADS * HEAD_DIM
+    gains = norm_gains
     prompt = prompt_kv[0]
     history = history_kv[0]
     recent = new_kv[0]
     cache = jnp.concatenate([history, jnp.transpose(recent, (1, 0, 2))], axis=1).reshape(
         -1, history.shape[2]
     )
+    prompt_keys_t = prompt[:, :half].T
+    cache_keys_t = cache[:, :half].T
     groups = 4
     group_rows = part_dev // groups
+    grouped_tokens = token_states.reshape(steps, groups, group_rows, model_width)
     moments = steps * section_count + groups - 1
 
     def advance(moment, carry):
@@ -154,18 +175,17 @@
         group_now = jnp.clip(group_raw, 0, groups - 1)
         start = group_now * group_rows
         zero = jnp.zeros((), jnp.int32)
-        token_rows = lax.dynamic_slice(
-            token_states, (step_now, start, zero), (1, group_rows, model_width)
-        )[0].astype(jnp.float32)
-        carried = jnp.where(step_now > 0, normalize(arrived), 0.0)
-        hidden = jnp.where(section_index == 0, token_rows + carried, arrived)
-        mixed = attend(
-            hidden, gains_row, prompt, cache, step_now, group_now, history.shape[1], history.shape[1] + steps
+        scalars = jnp.stack(
+            [step_now, group_now, (section_index == 0).astype(jnp.int32), (step_now > 0).astype(jnp.int32)]
+        ).astype(jnp.int32)
+        residual, mixed = stage(
+            scalars, arrived, grouped_tokens, gains, prompt_keys_t, prompt, cache_keys_t, cache,
+            history.shape[1],
         )
         previous = lax.dynamic_slice(outbuf, (step_now, start, zero), (1, group_rows, model_width))
-        written = jnp.where(active, mixed.astype(jnp.bfloat16)[None], previous)
+        written = jnp.where(active, mixed[None], previous)
         outbuf = lax.dynamic_update_slice(outbuf, written, (step_now, start, zero))
-        passed = passed_along(hidden + mixed, "section", 1)
+        passed = passed_along(residual, "section", 1)
         return (passed, outbuf)
 
     start_carry = (

time: 538 us -> 466 us (0.87)
  other arithmetic: 86.5 us -> 54.9 us
  local copies, waits for them, and re-layouts: 46.1 us -> 28 us
  waiting for transfers between devices: 250 us -> 232 us
    dynamic_update_slice x19, other arithmetic: 1.62 us -> 30.3 us  [advance(): outbuf = lax.dynamic_update_slice(outbuf, written, (step_now, start, zero))]
    reduce_sum x38 -> x0, other arithmetic: 25.5 us -> none  [normalize(): jnp.mean(values * values, axis=-1, keepdims=True) + 1e-05]
    convert_element_type x19 -> x0, other arithmetic: 17.4 us -> none  [advance(): written = jnp.where(active, mixed.astype(jnp.bfloat16)[None], previous)]
    while x19 -> x0, other arithmetic: 16.4 us -> none
    all_to_all x1, waiting for transfers between devices: 187 us -> 175 us  [fork_cache(): lax.all_to_all(outgoing, 'dp', split_axis=0, concat_axis=0, tiled=True)]
    while x19 -> x2, local copies, waits for them, and re-layouts: 17.3 us -> 6.23 us  [local(): _, outbuf = lax.fori_loop(0, moments, advance, start_carry)]
    reshape x19 -> x1, local copies, waits for them, and re-layouts: 12 us -> 1.46 us  [local(): token_states.reshape(steps, groups, group_rows, model_width)]
    ppermute x19, waiting for transfers between devices: 62.6 us -> 57.1 us  [passed_along(): return lax.ppermute(block, axis, route)]
  transfers between devices with their start and end apart: 20 -> 20, of which waited for: 20 -> 20; matrix products, arithmetic and copies ran while one was open for 4% -> 9% of each run, Pallas kernels for 0% -> 0%
where the time goes in v2:
time: 466 us; the launch traced here: 463 us
  waiting for transfers between devices  232 us (50%)
  Pallas kernels  133 us (29%)
  other arithmetic  54.9 us (12%)
  local copies, waits for them, and re-layouts  28 us (6%)
  starting transfers between devices  14.8 us (3%)
    all_to_all x1, waiting for transfers between devices, fork_cache(): lax.all_to_all(outgoing, 'dp', split_axis=0, concat_axis=0, tiled=True)  175 us
    pallas_call x19, Pallas kernels, stage(): pl.pallas_call(stage_kernel(rows, tokens, hist_len, hb), grid_spec=grid_s...  133 us
    ppermute x19, waiting for transfers between devices, passed_along(): return lax.ppermute(block, axis, route)  57.1 us
    dynamic_update_slice x19, other arithmetic, advance(): outbuf = lax.dynamic_update_slice(outbuf, written, (step_now, start, zero))  30.3 us
    all_to_all x1, starting transfers between devices, fork_cache(): lax.all_to_all(outgoing, 'dp', split_axis=0, concat_axis=0, tiled=True)  14.8 us
    another operation x19, other arithmetic, advance(): jnp.stack([step_now, group_now, (section_index == 0).astype(jnp.int32), (...  12.6 us
  transfers between devices with their start and end apart: 20, of which 20 were waited for; matrix products, arithmetic and copies ran while one was open for 9% of the time, Pallas kernels for 0%

profile of v2, /device:TPU:6, one launch (start us, length us, event | category | flops | bytes accessed | tf_op | source)
XLA Modules:
  0.0 463.5 jit_solution(1610559689332484703)
XLA Ops:
  2.7 2.5 copy.17
  5.6 5.3 %gather_fusion = bf16[64,32,2048]{2,1,0:T(8,128)(2,1)} fusion(bf16[16,32,2048]{2,1,0:T(8,128)(2,1)S(1)} %pad_maximum_fusion, s32[1024]{0:T(1024)S(1)} %pad_clamp_fusion.1), kind=kCustom, calls=%fused_computation | custom fusion | bytes 16777472 | tf_op jit(solution)/shard_map/jit(_take)/gather | solution.py:141
  10.9 7.5 %broadcast_select_fusion = bf16[64,32,2048]{2,1,0:T(8,128)(2,1)} fusion(bf16[64,32,2048]{2,1,0:T(8,128)(2,1)} %gather_fusion, pred[64]{0:T(512)(128)(4,1)S(1)} %compare_and_fusion), kind=kLoop, calls=%fused_computation.5 | loop fusion | flops 4194304 | bytes 16777280 | tf_op jit(solution)/shard_map/jit(_take)/select_n | solution.py:141
  18.4 14.8 %all-to-all-start = ((bf16[64,32,2048]{2,1,0:T(8,128)(2,1)}), bf16[64,32,2048]{2,1,0:T(8,128)(2,1)}, u32[]{:S(2)}, u32[]{:S(2)}) async-start(bf16[64,32,2048]{2,1,0:T(8,128)(2,1)} %broadcast_select_fusion), calls=%async_computation | async-start | bytes 16777216 | tf_op jit(solution)/shard_map/all_to_all | solution.py:142
  34.6 3.1 slice_bitcast_fusion
  37.7 3.9 copy.13
  42.7 2.3 copy.14
  45.8 175.3 %all-to-all-done = bf16[64,32,2048]{2,1,0:T(8,128)(2,1)} async-done(((bf16[64,32,2048]{2,1,0:T(8,128)(2,1)}), bf16[64,32,2048]{2,1,0:T(8,128)(2,1)}, u32[]{:S(2)}, u32[]{:S(2)}) %all-to-all-start) | async-done | bytes 8388640 | tf_op jit(solution)/shard_map/all_to_all | solution.py:142
  221.1 5.4 %gather_fusion.1 = bf16[16,32,2048]{2,1,0:T(8,128)(2,1)} fusion(bf16[64,32,2048]{2,1,0:T(8,128)(2,1)} %all-to-all-done, s32[1024]{0:T(1024)S(1)} %pad_clamp_fusion), kind=kCustom, calls=%fused_computation.1 | custom fusion | bytes 4194368 | tf_op jit(solution)/shard_map/jit(_take)/gather | solution.py:144
  226.4 3.2 bitcast_select_fusion.1
  230.7 232.8 %while.17 = (s32[]{:T(128)}, f32[4,8192]{1,0:T(4,128)S(1)}, bf16[4,16,8192]{2,1,0:T(8,128)(2,1)}, s32[]{:T(128)}, pred[]{:T(512)}, /*index=5*/bf16[4,4,4,8192]{3...) while((s32[]{:T(128)}, f32[4,8192]{1,0:T(4,128)S(1)}, ...), condition=%wide.region_1.2_spmd, body=%wide.region_0.1_spmd.sunk | while | flops 32818 | bytes 721995 | solution.py:196
  231.4 7.0 %eval_jaxpr.8 = (f32[4,8192]{1,0:T(4,128)}, bf16[4,8192]{1,0:T(4,128)(2,1)}) custom-call(s32[4]{0:T(128)} %pad_add_fusion.2.sc_ref, f32[4,8192]{1,0:T(4,128)S(1)} %get-tuple-element.377.arr_ref, bf16[4,4,4,8192]{3,2,1,0:T(4,128)(2,1)S(1)} %get-tuple-element.399.tok_ref, f32[1,8192]{1,0:T(1,128)S(1)} %get-tuple-element.400.gain_ref, ...), custom_call_target="tpu_custom_call" | custom-call | tf_op jit(solution)/shard_map/while/body/eval_jaxpr/pallas_call | solution.py:123
  238.3 1.6 fusion.8
  239.9 3.0 collective-permute-done
  243.6 7.0 %eval_jaxpr.8 = (f32[4,8192]{1,0:T(4,128)}, bf16[4,8192]{1,0:T(4,128)(2,1)}) custom-call(s32[4]{0:T(128)} %pad_add_fusion.2.sc_ref, f32[4,8192]{1,0:T(4,128)S(1)} %get-tuple-element.377.arr_ref, bf16[4,4,4,8192]{3,2,1,0:T(4,128)(2,1)S(1)} %get-tuple-element.399.tok_ref, f32[1,8192]{1,0:T(1,128)S(1)} %get-tuple-element.400.gain_ref, ...), custom_call_target="tpu_custom_call" | custom-call | tf_op jit(solution)/shard_map/while/body/eval_jaxpr/pallas_call | solution.py:123
  250.6 1.6 fusion.8
  252.2 3.0 collective-permute-done
  255.9 7.0 %eval_jaxpr.8 = (f32[4,8192]{1,0:T(4,128)}, bf16[4,8192]{1,0:T(4,128)(2,1)}) custom-call(s32[4]{0:T(128)} %pad_add_fusion.2.sc_ref, f32[4,8192]{1,0:T(4,128)S(1)} %get-tuple-element.377.arr_ref, bf16[4,4,4,8192]{3,2,1,0:T(4,128)(2,1)S(1)} %get-tuple-element.399.tok_ref, f32[1,8192]{1,0:T(1,128)S(1)} %get-tuple-element.400.gain_ref, ...), custom_call_target="tpu_custom_call" | custom-call | tf_op jit(solution)/shard_map/while/body/eval_jaxpr/pallas_call | solution.py:123
  262.8 1.6 fusion.8
  264.4 3.0 collective-permute-done
  268.1 7.0 %eval_jaxpr.8 = (f32[4,8192]{1,0:T(4,128)}, bf16[4,8192]{1,0:T(4,128)(2,1)}) custom-call(s32[4]{0:T(128)} %pad_add_fusion.2.sc_ref, f32[4,8192]{1,0:T(4,128)S(1)} %get-tuple-element.377.arr_ref, bf16[4,4,4,8192]{3,2,1,0:T(4,128)(2,1)S(1)} %get-tuple-element.399.tok_ref, f32[1,8192]{1,0:T(1,128)S(1)} %get-tuple-element.400.gain_ref, ...), custom_call_target="tpu_custom_call" | custom-call | tf_op jit(solution)/shard_map/while/body/eval_jaxpr/pallas_call | solution.py:123
  275.1 1.6 fusion.8
  276.7 3.0 collective-permute-done
  280.4 7.0 %eval_jaxpr.8 = (f32[4,8192]{1,0:T(4,128)}, bf16[4,8192]{1,0:T(4,128)(2,1)}) custom-call(s32[4]{0:T(128)} %pad_add_fusion.2.sc_ref, f32[4,8192]{1,0:T(4,128)S(1)} %get-tuple-element.377.arr_ref, bf16[4,4,4,8192]{3,2,1,0:T(4,128)(2,1)S(1)} %get-tuple-element.399.tok_ref, f32[1,8192]{1,0:T(1,128)S(1)} %get-tuple-element.400.gain_ref, ...), custom_call_target="tpu_custom_call" | custom-call | tf_op jit(solution)/shard_map/while/body/eval_jaxpr/pallas_call | solution.py:123
  287.3 1.6 fusion.8
  288.9 3.0 collective-permute-done
  292.6 7.0 %eval_jaxpr.8 = (f32[4,8192]{1,0:T(4,128)}, bf16[4,8192]{1,0:T(4,128)(2,1)}) custom-call(s32[4]{0:T(128)} %pad_add_fusion.2.sc_ref, f32[4,8192]{1,0:T(4,128)S(1)} %get-tuple-element.377.arr_ref, bf16[4,4,4,8192]{3,2,1,0:T(4,128)(2,1)S(1)} %get-tuple-element.399.tok_ref, f32[1,8192]{1,0:T(1,128)S(1)} %get-tuple-element.400.gain_ref, ...), custom_call_target="tpu_custom_call" | custom-call | tf_op jit(solution)/shard_map/while/body/eval_jaxpr/pallas_call | solution.py:123
  299.6 1.6 fusion.8
  301.2 3.0 collective-permute-done
  304.9 7.0 %eval_jaxpr.8 = (f32[4,8192]{1,0:T(4,128)}, bf16[4,8192]{1,0:T(4,128)(2,1)}) custom-call(s32[4]{0:T(128)} %pad_add_fusion.2.sc_ref, f32[4,8192]{1,0:T(4,128)S(1)} %get-tuple-element.377.arr_ref, bf16[4,4,4,8192]{3,2,1,0:T(4,128)(2,1)S(1)} %get-tuple-element.399.tok_ref, f32[1,8192]{1,0:T(1,128)S(1)} %get-tuple-element.400.gain_ref, ...), custom_call_target="tpu_custom_call" | custom-call | tf_op jit(solution)/shard_map/while/body/eval_jaxpr/pallas_call | solution.py:123
  311.9 1.6 fusion.8
  313.4 3.0 collective-permute-done
  317.1 7.0 %eval_jaxpr.8 = (f32[4,8192]{1,0:T(4,128)}, bf16[4,8192]{1,0:T(4,128)(2,1)}) custom-call(s32[4]{0:T(128)} %pad_add_fusion.2.sc_ref, f32[4,8192]{1,0:T(4,128)S(1)} %get-tuple-element.377.arr_ref, bf16[4,4,4,8192]{3,2,1,0:T(4,128)(2,1)S(1)} %get-tuple-element.399.tok_ref, f32[1,8192]{1,0:T(1,128)S(1)} %get-tuple-element.400.gain_ref, ...), custom_call_target="tpu_custom_call" | custom-call | tf_op jit(solution)/shard_map/while/body/eval_jaxpr/pallas_call | solution.py:123
  324.1 1.6 fusion.8
  325.7 3.0 collective-permute-done
  329.4 7.0 %eval_jaxpr.8 = (f32[4,8192]{1,0:T(4,128)}, bf16[4,8192]{1,0:T(4,128)(2,1)}) custom-call(s32[4]{0:T(128)} %pad_add_fusion.2.sc_ref, f32[4,8192]{1,0:T(4,128)S(1)} %get-tuple-element.377.arr_ref, bf16[4,4,4,8192]{3,2,1,0:T(4,128)(2,1)S(1)} %get-tuple-element.399.tok_ref, f32[1,8192]{1,0:T(1,128)S(1)} %get-tuple-element.400.gain_ref, ...), custom_call_target="tpu_custom_call" | custom-call | tf_op jit(solution)/shard_map/while/body/eval_jaxpr/pallas_call | solution.py:123
  336.4 1.6 fusion.8
  338.0 3.0 collective-permute-done
  341.6 7.0 %eval_jaxpr.8 = (f32[4,8192]{1,0:T(4,128)}, bf16[4,8192]{1,0:T(4,128)(2,1)}) custom-call(s32[4]{0:T(128)} %pad_add_fusion.2.sc_ref, f32[4,8192]{1,0:T(4,128)S(1)} %get-tuple-element.377.arr_ref, bf16[4,4,4,8192]{3,2,1,0:T(4,128)(2,1)S(1)} %get-tuple-element.399.tok_ref, f32[1,8192]{1,0:T(1,128)S(1)} %get-tuple-element.400.gain_ref, ...), custom_call_target="tpu_custom_call" | custom-call | tf_op jit(solution)/shard_map/while/body/eval_jaxpr/pallas_call | solution.py:123
  348.6 1.6 fusion.8
  350.2 3.0 collective-permute-done
  353.9 7.0 %eval_jaxpr.8 = (f32[4,8192]{1,0:T(4,128)}, bf16[4,8192]{1,0:T(4,128)(2,1)}) custom-call(s32[4]{0:T(128)} %pad_add_fusion.2.sc_ref, f32[4,8192]{1,0:T(4,128)S(1)} %get-tuple-element.377.arr_ref, bf16[4,4,4,8192]{3,2,1,0:T(4,128)(2,1)S(1)} %get-tuple-element.399.tok_ref, f32[1,8192]{1,0:T(1,128)S(1)} %get-tuple-element.400.gain_ref, ...), custom_call_target="tpu_custom_call" | custom-call | tf_op jit(solution)/shard_map/while/body/eval_jaxpr/pallas_call | solution.py:123
  360.9 1.6 fusion.8
  362.5 3.0 collective-permute-done
  366.1 7.0 %eval_jaxpr.8 = (f32[4,8192]{1,0:T(4,128)}, bf16[4,8192]{1,0:T(4,128)(2,1)}) custom-call(s32[4]{0:T(128)} %pad_add_fusion.2.sc_ref, f32[4,8192]{1,0:T(4,128)S(1)} %get-tuple-element.377.arr_ref, bf16[4,4,4,8192]{3,2,1,0:T(4,128)(2,1)S(1)} %get-tuple-element.399.tok_ref, f32[1,8192]{1,0:T(1,128)S(1)} %get-tuple-element.400.gain_ref, ...), custom_call_target="tpu_custom_call" | custom-call | tf_op jit(solution)/shard_map/while/body/eval_jaxpr/pallas_call | solution.py:123
  373.1 1.6 fusion.8
  374.7 3.0 collective-permute-done
  378.4 7.0 %eval_jaxpr.8 = (f32[4,8192]{1,0:T(4,128)}, bf16[4,8192]{1,0:T(4,128)(2,1)}) custom-call(s32[4]{0:T(128)} %pad_add_fusion.2.sc_ref, f32[4,8192]{1,0:T(4,128)S(1)} %get-tuple-element.377.arr_ref, bf16[4,4,4,8192]{3,2,1,0:T(4,128)(2,1)S(1)} %get-tuple-element.399.tok_ref, f32[1,8192]{1,0:T(1,128)S(1)} %get-tuple-element.400.gain_ref, ...), custom_call_target="tpu_custom_call" | custom-call | tf_op jit(solution)/shard_map/while/body/eval_jaxpr/pallas_call | solution.py:123
  385.4 1.6 fusion.8
  387.0 3.0 collective-permute-done
  390.6 7.0 %eval_jaxpr.8 = (f32[4,8192]{1,0:T(4,128)}, bf16[4,8192]{1,0:T(4,128)(2,1)}) custom-call(s32[4]{0:T(128)} %pad_add_fusion.2.sc_ref, f32[4,8192]{1,0:T(4,128)S(1)} %get-tuple-element.377.arr_ref, bf16[4,4,4,8192]{3,2,1,0:T(4,128)(2,1)S(1)} %get-tuple-element.399.tok_ref, f32[1,8192]{1,0:T(1,128)S(1)} %get-tuple-element.400.gain_ref, ...), custom_call_target="tpu_custom_call" | custom-call | tf_op jit(solution)/shard_map/while/body/eval_jaxpr/pallas_call | solution.py:123
  399.2 3.0 collective-permute-done
  402.9 7.0 %eval_jaxpr.8 = (f32[4,8192]{1,0:T(4,128)}, bf16[4,8192]{1,0:T(4,128)(2,1)}) custom-call(s32[4]{0:T(128)} %pad_add_fusion.2.sc_ref, f32[4,8192]{1,0:T(4,128)S(1)} %get-tuple-element.377.arr_ref, bf16[4,4,4,8192]{3,2,1,0:T(4,128)(2,1)S(1)} %get-tuple-element.399.tok_ref, f32[1,8192]{1,0:T(1,128)S(1)} %get-tuple-element.400.gain_ref, ...), custom_call_target="tpu_custom_call" | custom-call | tf_op jit(solution)/shard_map/while/body/eval_jaxpr/pallas_call | solution.py:123
  409.9 1.6 fusion.8
  411.5 3.0 collective-permute-done
  415.1 7.0 %eval_jaxpr.8 = (f32[4,8192]{1,0:T(4,128)}, bf16[4,8192]{1,0:T(4,128)(2,1)}) custom-call(s32[4]{0:T(128)} %pad_add_fusion.2.sc_ref, f32[4,8192]{1,0:T(4,128)S(1)} %get-tuple-element.377.arr_ref, bf16[4,4,4,8192]{3,2,1,0:T(4,128)(2,1)S(1)} %get-tuple-element.399.tok_ref, f32[1,8192]{1,0:T(1,128)S(1)} %get-tuple-element.400.gain_ref, ...), custom_call_target="tpu_custom_call" | custom-call | tf_op jit(solution)/shard_map/while/body/eval_jaxpr/pallas_call | solution.py:123
  423.7 3.0 collective-permute-done
  427.4 7.0 %eval_jaxpr.8 = (f32[4,8192]{1,0:T(4,128)}, bf16[4,8192]{1,0:T(4,128)(2,1)}) custom-call(s32[4]{0:T(128)} %pad_add_fusion.2.sc_ref, f32[4,8192]{1,0:T(4,128)S(1)} %get-tuple-element.377.arr_ref, bf16[4,4,4,8192]{3,2,1,0:T(4,128)(2,1)S(1)} %get-tuple-element.399.tok_ref, f32[1,8192]{1,0:T(1,128)S(1)} %get-tuple-element.400.gain_ref, ...), custom_call_target="tpu_custom_call" | custom-call | tf_op jit(solution)/shard_map/while/body/eval_jaxpr/pallas_call | solution.py:123
  434.4 1.6 fusion.8
  436.0 3.0 collective-permute-done
  439.6 7.0 %eval_jaxpr.8 = (f32[4,8192]{1,0:T(4,128)}, bf16[4,8192]{1,0:T(4,128)(2,1)}) custom-call(s32[4]{0:T(128)} %pad_add_fusion.2.sc_ref, f32[4,8192]{1,0:T(4,128)S(1)} %get-tuple-element.377.arr_ref, bf16[4,4,4,8192]{3,2,1,0:T(4,128)(2,1)S(1)} %get-tuple-element.399.tok_ref, f32[1,8192]{1,0:T(1,128)S(1)} %get-tuple-element.400.gain_ref, ...), custom_call_target="tpu_custom_call" | custom-call | tf_op jit(solution)/shard_map/while/body/eval_jaxpr/pallas_call | solution.py:123
  448.2 3.0 collective-permute-done
  451.9 7.0 %eval_jaxpr.8 = (f32[4,8192]{1,0:T(4,128)}, bf16[4,8192]{1,0:T(4,128)(2,1)}) custom-call(s32[4]{0:T(128)} %pad_add_fusion.2.sc_ref, f32[4,8192]{1,0:T(4,128)S(1)} %get-tuple-element.377.arr_ref, bf16[4,4,4,8192]{3,2,1,0:T(4,128)(2,1)S(1)} %get-tuple-element.399.tok_ref, f32[1,8192]{1,0:T(1,128)S(1)} %get-tuple-element.400.gain_ref, ...), custom_call_target="tpu_custom_call" | custom-call | tf_op jit(solution)/shard_map/while/body/eval_jaxpr/pallas_call | solution.py:123
  460.5 3.0 collective-permute-done
  (57 shorter events, 25.9 us)
Async XLA Ops:
  18.4 202.7 %all-to-all-start = ((bf16[64,32,2048]{2,1,0:T(8,128)(2,1)}), bf16[64,32,2048]{2,1,0:T(8,128)(2,1)}, u32[]{:S(2)}, u32[]{:S(2)}) async-start(bf16[64,32,2048]{2,1,0:T(8,128)(2,1)} %broadcast_select_fusion), calls=%async_computation | async-start | bytes 16777216 | tf_op jit(solution)/shard_map/all_to_all | solution.py:142
  226.4 4.2 copy-start
  238.3 4.6 collective-permute-start
  250.6 4.6 collective-permute-start
  262.8 4.6 collective-permute-start
  275.1 4.6 collective-permute-start
  287.3 4.6 collective-permute-start
  299.6 4.6 collective-permute-start
  311.9 4.6 collective-permute-start
  324.1 4.6 collective-permute-start
  336.4 4.6 collective-permute-start
  348.6 4.6 collective-permute-start
  360.9 4.6 collective-permute-start
  373.1 4.6 collective-permute-start
  385.4 4.6 collective-permute-start
  397.6 4.6 collective-permute-start
  409.9 4.6 collective-permute-start
  422.1 4.6 collective-permute-start
  434.4 4.6 collective-permute-start
  446.6 4.6 collective-permute-start
  458.9 4.6 collective-permute-start

commit v3 on v2

--- a/solution.py
+++ b/solution.py
@@ -138,10 +138,10 @@
     particle_cache = jnp.concatenate([history, jnp.transpose(recent, (1, 0, 2))], axis=1)
     owners = ancestors.reshape(shards, part_dev)
     picked = jnp.max(jnp.where(owners // part_dev == own_index, owners % part_dev, 0), axis=1)
-    outgoing = jnp.take(particle_cache, picked, axis=0)
+    outgoing = jnp.take(particle_cache, picked, axis=0, mode="clip")
     incoming = lax.all_to_all(outgoing, "dp", split_axis=0, concat_axis=0, tiled=True)
     own_ancestors = lax.dynamic_slice_in_dim(ancestors, own_index * part_dev, part_dev)
-    return jnp.take(incoming, own_ancestors // part_dev, axis=0)[None]
+    return jnp.take(incoming, own_ancestors // part_dev, axis=0, mode="clip")[None]
 
 
 def local(token_states, norm_gains, prompt_kv, history_kv, new_kv, ancestors):
@@ -165,19 +165,23 @@
     grouped_tokens = token_states.reshape(steps, groups, group_rows, model_width)
     moments = steps * section_count + groups - 1
 
-    def advance(moment, carry):
-        arrived, outbuf = carry
+    def timing(moment):
         offset = moment - section_index
         step_raw = jnp.floor_divide(offset, section_count)
         group_raw = jnp.mod(offset, section_count)
         active = (offset >= 0) & (step_raw < steps) & (group_raw < groups)
         step_now = jnp.clip(step_raw, 0, steps - 1)
         group_now = jnp.clip(group_raw, 0, groups - 1)
-        start = group_now * group_rows
-        zero = jnp.zeros((), jnp.int32)
         scalars = jnp.stack(
             [step_now, group_now, (section_index == 0).astype(jnp.int32), (step_now > 0).astype(jnp.int32)]
         ).astype(jnp.int32)
+        return active, step_now, group_now, scalars
+
+    def advance(moment, carry):
+        arrived, outbuf, scalars = carry
+        active, step_now, group_now, _ = timing(moment)
+        start = group_now * group_rows
+        zero = jnp.zeros((), jnp.int32)
         residual, mixed = stage(
             scalars, arrived, grouped_tokens, gains, prompt_keys_t, prompt, cache_keys_t, cache,
             history.shape[1],
@@ -186,14 +190,15 @@
         written = jnp.where(active, mixed[None], previous)
         outbuf = lax.dynamic_update_slice(outbuf, written, (step_now, start, zero))
         passed = passed_along(residual, "section", 1)
-        return (passed, outbuf)
+        return (passed, outbuf, timing(moment + 1)[3])
 
     start_carry = (
         jnp.zeros((group_rows, model_width), jnp.float32),
         jnp.zeros((steps, part_dev, model_width), jnp.bfloat16),
+        timing(jnp.zeros((), jnp.int32))[3],
     )
     forked_kv = fork_cache(history, recent, ancestors, part_dev)
-    _, outbuf = lax.fori_loop(0, moments, advance, start_carry)
+    _, outbuf, _ = lax.fori_loop(0, moments, advance, start_carry)
     return (outbuf[None], forked_kv)
 
 

time: 466 us -> 443 us (0.951)
  other arithmetic: 54.9 us -> 34.1 us
    another operation x19 -> x20, other arithmetic: 12.6 us -> 1.53 us  [timing(): jnp.stack([step_now, group_now, (section_index == 0).astype(jnp.int32), (...]
    select_n x3 -> x1, other arithmetic: 10.7 us -> 0.08 us  [fork_cache(): own_ancestors // part_dev]
  transfers between devices with their start and end apart: 20 -> 20, of which waited for: 20 -> 20; matrix products, arithmetic and copies ran while one was open for 9% -> 10% of each run, Pallas kernels for 0% -> 0%
where the time goes in v3:
time: 443 us; the launch traced here: 440 us
  waiting for transfers between devices  232 us (52%)
  Pallas kernels  130 us (29%)
  other arithmetic  34.1 us (8%)
  local copies, waits for them, and re-layouts  28.6 us (6%)
  starting transfers between devices  14.8 us (3%)
    all_to_all x1, waiting for transfers between devices, fork_cache(): lax.all_to_all(outgoing, 'dp', split_axis=0, concat_axis=0, tiled=True)  176 us
    pallas_call x19, Pallas kernels, stage(): pl.pallas_call(stage_kernel(rows, tokens, hist_len, hb), grid_spec=grid_s...  130 us
    ppermute x19, waiting for transfers between devices, passed_along(): return lax.ppermute(block, axis, route)  55.7 us
    dynamic_update_slice x19, other arithmetic, advance(): outbuf = lax.dynamic_update_slice(outbuf, written, (step_now, start, zero))  30.3 us
    all_to_all x1, starting transfers between devices, fork_cache(): lax.all_to_all(outgoing, 'dp', split_axis=0, concat_axis=0, tiled=True)  14.8 us
  transfers between devices with their start and end apart: 20, of which 20 were waited for; matrix products, arithmetic and copies ran while one was open for 10% of the time, Pallas kernels for 0%

profile of v3, /device:TPU:6, one launch (start us, length us, event | category | flops | bytes accessed | tf_op | source)
XLA Modules:
  0.0 440.3 jit_solution(17701599307894182263)
XLA Ops:
  1.8 3.8 copy.17
  5.9 2.1 pad_maximum_fusion
  8.0 5.3 %gather_fusion = bf16[64,32,2048]{2,1,0:T(8,128)(2,1)} fusion(bf16[16,32,2048]{2,1,0:T(8,128)(2,1)S(1)} %pad_maximum_fusion, s32[1024]{0:T(1024)S(1)} %pad_clamp_fusion.1), kind=kCustom, calls=%fused_computation | custom fusion | bytes 16777472 | tf_op jit(solution)/shard_map/jit(_take)/gather | solution.py:141
  13.2 14.8 %all-to-all-start = ((bf16[64,32,2048]{2,1,0:T(8,128)(2,1)}), bf16[64,32,2048]{2,1,0:T(8,128)(2,1)}, u32[]{:S(2)}, u32[]{:S(2)}) async-start(bf16[64,32,2048]{2,1,0:T(8,128)(2,1)} %gather_fusion), calls=%async_computation | async-start | bytes 16777216 | tf_op jit(solution)/shard_map/all_to_all | solution.py:142
  29.5 3.1 slice_bitcast_fusion
  32.6 3.9 copy.13
  37.6 2.3 copy.14
  40.1 175.9 %all-to-all-done = bf16[64,32,2048]{2,1,0:T(8,128)(2,1)} async-done(((bf16[64,32,2048]{2,1,0:T(8,128)(2,1)}), bf16[64,32,2048]{2,1,0:T(8,128)(2,1)}, u32[]{:S(2)}, u32[]{:S(2)}) %all-to-all-start) | async-done | bytes 8388640 | tf_op jit(solution)/shard_map/all_to_all | solution.py:142
  215.9 5.4 %gather_fusion.1 = bf16[16,32,2048]{2,1,0:T(8,128)(2,1)} fusion(bf16[64,32,2048]{2,1,0:T(8,128)(2,1)} %all-to-all-done, s32[1024]{0:T(1024)S(1)} %pad_clamp_fusion), kind=kCustom, calls=%fused_computation.1 | custom fusion | bytes 4194368 | tf_op jit(solution)/shard_map/jit(_take)/gather | solution.py:144
  222.4 217.9 %while.20 = (s32[]{:T(128)}, f32[4,8192]{1,0:T(4,128)S(1)}, bf16[4,16,8192]{2,1,0:T(8,128)(2,1)}, s32[4]{0:T(128)S(1)}, bf16[4,4,4,8192]{3,2,1,0:T(4,128)(2,1)S(...) while((s32[]{:T(128)}, f32[4,8192]{1,0:T(4,128)S(1)}, ...), condition=%wide.region_1.2_spmd, body=%wide.region_0.1_spmd.sunk | while | flops 32842 | bytes 721742 | solution.py:201
  222.4 6.9 %eval_jaxpr.9 = (f32[4,8192]{1,0:T(4,128)}, bf16[4,8192]{1,0:T(4,128)(2,1)}) custom-call(s32[4]{0:T(128)S(1)} %get-tuple-element.443.sc_ref, f32[4,8192]{1,0:T(4,128)S(1)} %get-tuple-element.441.arr_ref, bf16[4,4,4,8192]{3,2,1,0:T(4,128)(2,1)S(1)} %get-tuple-element.463.tok_ref, f32[1,8192]{1,0:T(1,128)S(1)} %get-tuple-element.464.gain_ref, ...), custom_call_target="tpu_custom_call" | custom-call | tf_op jit(solution)/shard_map/while/body/eval_jaxpr/pallas_call | solution.py:123
  229.3 1.6 fusion.7
  230.9 2.9 collective-permute-done
  233.9 6.9 %eval_jaxpr.9 = (f32[4,8192]{1,0:T(4,128)}, bf16[4,8192]{1,0:T(4,128)(2,1)}) custom-call(s32[4]{0:T(128)S(1)} %get-tuple-element.443.sc_ref, f32[4,8192]{1,0:T(4,128)S(1)} %get-tuple-element.441.arr_ref, bf16[4,4,4,8192]{3,2,1,0:T(4,128)(2,1)S(1)} %get-tuple-element.463.tok_ref, f32[1,8192]{1,0:T(1,128)S(1)} %get-tuple-element.464.gain_ref, ...), custom_call_target="tpu_custom_call" | custom-call | tf_op jit(solution)/shard_map/while/body/eval_jaxpr/pallas_call | solution.py:123
  240.7 1.6 fusion.7
  242.4 2.9 collective-permute-done
  245.3 6.9 %eval_jaxpr.9 = (f32[4,8192]{1,0:T(4,128)}, bf16[4,8192]{1,0:T(4,128)(2,1)}) custom-call(s32[4]{0:T(128)S(1)} %get-tuple-element.443.sc_ref, f32[4,8192]{1,0:T(4,128)S(1)} %get-tuple-element.441.arr_ref, bf16[4,4,4,8192]{3,2,1,0:T(4,128)(2,1)S(1)} %get-tuple-element.463.tok_ref, f32[1,8192]{1,0:T(1,128)S(1)} %get-tuple-element.464.gain_ref, ...), custom_call_target="tpu_custom_call" | custom-call | tf_op jit(solution)/shard_map/while/body/eval_jaxpr/pallas_call | solution.py:123
  252.2 1.6 fusion.7
  253.9 2.9 collective-permute-done
  256.8 6.9 %eval_jaxpr.9 = (f32[4,8192]{1,0:T(4,128)}, bf16[4,8192]{1,0:T(4,128)(2,1)}) custom-call(s32[4]{0:T(128)S(1)} %get-tuple-element.443.sc_ref, f32[4,8192]{1,0:T(4,128)S(1)} %get-tuple-element.441.arr_ref, bf16[4,4,4,8192]{3,2,1,0:T(4,128)(2,1)S(1)} %get-tuple-element.463.tok_ref, f32[1,8192]{1,0:T(1,128)S(1)} %get-tuple-element.464.gain_ref, ...), custom_call_target="tpu_custom_call" | custom-call | tf_op jit(solution)/shard_map/while/body/eval_jaxpr/pallas_call | solution.py:123
  263.7 1.6 fusion.7
  265.3 2.9 collective-permute-done
  268.3 6.9 %eval_jaxpr.9 = (f32[4,8192]{1,0:T(4,128)}, bf16[4,8192]{1,0:T(4,128)(2,1)}) custom-call(s32[4]{0:T(128)S(1)} %get-tuple-element.443.sc_ref, f32[4,8192]{1,0:T(4,128)S(1)} %get-tuple-element.441.arr_ref, bf16[4,4,4,8192]{3,2,1,0:T(4,128)(2,1)S(1)} %get-tuple-element.463.tok_ref, f32[1,8192]{1,0:T(1,128)S(1)} %get-tuple-element.464.gain_ref, ...), custom_call_target="tpu_custom_call" | custom-call | tf_op jit(solution)/shard_map/while/body/eval_jaxpr/pallas_call | solution.py:123
  275.1 1.6 fusion.7
  276.8 2.9 collective-permute-done
  279.7 6.9 %eval_jaxpr.9 = (f32[4,8192]{1,0:T(4,128)}, bf16[4,8192]{1,0:T(4,128)(2,1)}) custom-call(s32[4]{0:T(128)S(1)} %get-tuple-element.443.sc_ref, f32[4,8192]{1,0:T(4,128)S(1)} %get-tuple-element.441.arr_ref, bf16[4,4,4,8192]{3,2,1,0:T(4,128)(2,1)S(1)} %get-tuple-element.463.tok_ref, f32[1,8192]{1,0:T(1,128)S(1)} %get-tuple-element.464.gain_ref, ...), custom_call_target="tpu_custom_call" | custom-call | tf_op jit(solution)/shard_map/while/body/eval_jaxpr/pallas_call | solution.py:123
  286.6 1.6 fusion.7
  288.3 2.9 collective-permute-done
  291.2 6.9 %eval_jaxpr.9 = (f32[4,8192]{1,0:T(4,128)}, bf16[4,8192]{1,0:T(4,128)(2,1)}) custom-call(s32[4]{0:T(128)S(1)} %get-tuple-element.443.sc_ref, f32[4,8192]{1,0:T(4,128)S(1)} %get-tuple-element.441.arr_ref, bf16[4,4,4,8192]{3,2,1,0:T(4,128)(2,1)S(1)} %get-tuple-element.463.tok_ref, f32[1,8192]{1,0:T(1,128)S(1)} %get-tuple-element.464.gain_ref, ...), custom_call_target="tpu_custom_call" | custom-call | tf_op jit(solution)/shard_map/while/body/eval_jaxpr/pallas_call | solution.py:123
  298.1 1.6 fusion.7
  299.7 2.9 collective-permute-done
  302.7 6.9 %eval_jaxpr.9 = (f32[4,8192]{1,0:T(4,128)}, bf16[4,8192]{1,0:T(4,128)(2,1)}) custom-call(s32[4]{0:T(128)S(1)} %get-tuple-element.443.sc_ref, f32[4,8192]{1,0:T(4,128)S(1)} %get-tuple-element.441.arr_ref, bf16[4,4,4,8192]{3,2,1,0:T(4,128)(2,1)S(1)} %get-tuple-element.463.tok_ref, f32[1,8192]{1,0:T(1,128)S(1)} %get-tuple-element.464.gain_ref, ...), custom_call_target="tpu_custom_call" | custom-call | tf_op jit(solution)/shard_map/while/body/eval_jaxpr/pallas_call | solution.py:123
  309.5 1.6 fusion.7
  311.2 2.9 collective-permute-done
  314.1 6.9 %eval_jaxpr.9 = (f32[4,8192]{1,0:T(4,128)}, bf16[4,8192]{1,0:T(4,128)(2,1)}) custom-call(s32[4]{0:T(128)S(1)} %get-tuple-element.443.sc_ref, f32[4,8192]{1,0:T(4,128)S(1)} %get-tuple-element.441.arr_ref, bf16[4,4,4,8192]{3,2,1,0:T(4,128)(2,1)S(1)} %get-tuple-element.463.tok_ref, f32[1,8192]{1,0:T(1,128)S(1)} %get-tuple-element.464.gain_ref, ...), custom_call_target="tpu_custom_call" | custom-call | tf_op jit(solution)/shard_map/while/body/eval_jaxpr/pallas_call | solution.py:123
  321.0 1.6 fusion.7
  322.7 2.9 collective-permute-done
  325.6 6.9 %eval_jaxpr.9 = (f32[4,8192]{1,0:T(4,128)}, bf16[4,8192]{1,0:T(4,128)(2,1)}) custom-call(s32[4]{0:T(128)S(1)} %get-tuple-element.443.sc_ref, f32[4,8192]{1,0:T(4,128)S(1)} %get-tuple-element.441.arr_ref, bf16[4,4,4,8192]{3,2,1,0:T(4,128)(2,1)S(1)} %get-tuple-element.463.tok_ref, f32[1,8192]{1,0:T(1,128)S(1)} %get-tuple-element.464.gain_ref, ...), custom_call_target="tpu_custom_call" | custom-call | tf_op jit(solution)/shard_map/while/body/eval_jaxpr/pallas_call | solution.py:123
  332.5 1.6 fusion.7
  334.2 2.9 collective-permute-done
  337.1 6.9 %eval_jaxpr.9 = (f32[4,8192]{1,0:T(4,128)}, bf16[4,8192]{1,0:T(4,128)(2,1)}) custom-call(s32[4]{0:T(128)S(1)} %get-tuple-element.443.sc_ref, f32[4,8192]{1,0:T(4,128)S(1)} %get-tuple-element.441.arr_ref, bf16[4,4,4,8192]{3,2,1,0:T(4,128)(2,1)S(1)} %get-tuple-element.463.tok_ref, f32[1,8192]{1,0:T(1,128)S(1)} %get-tuple-element.464.gain_ref, ...), custom_call_target="tpu_custom_call" | custom-call | tf_op jit(solution)/shard_map/while/body/eval_jaxpr/pallas_call | solution.py:123
  345.6 2.9 collective-permute-done
  348.6 6.9 %eval_jaxpr.9 = (f32[4,8192]{1,0:T(4,128)}, bf16[4,8192]{1,0:T(4,128)(2,1)}) custom-call(s32[4]{0:T(128)S(1)} %get-tuple-element.443.sc_ref, f32[4,8192]{1,0:T(4,128)S(1)} %get-tuple-element.441.arr_ref, bf16[4,4,4,8192]{3,2,1,0:T(4,128)(2,1)S(1)} %get-tuple-element.463.tok_ref, f32[1,8192]{1,0:T(1,128)S(1)} %get-tuple-element.464.gain_ref, ...), custom_call_target="tpu_custom_call" | custom-call | tf_op jit(solution)/shard_map/while/body/eval_jaxpr/pallas_call | solution.py:123
  355.4 1.6 fusion.7
  357.1 2.9 collective-permute-done
  360.0 6.9 %eval_jaxpr.9 = (f32[4,8192]{1,0:T(4,128)}, bf16[4,8192]{1,0:T(4,128)(2,1)}) custom-call(s32[4]{0:T(128)S(1)} %get-tuple-element.443.sc_ref, f32[4,8192]{1,0:T(4,128)S(1)} %get-tuple-element.441.arr_ref, bf16[4,4,4,8192]{3,2,1,0:T(4,128)(2,1)S(1)} %get-tuple-element.463.tok_ref, f32[1,8192]{1,0:T(1,128)S(1)} %get-tuple-element.464.gain_ref, ...), custom_call_target="tpu_custom_call" | custom-call | tf_op jit(solution)/shard_map/while/body/eval_jaxpr/pallas_call | solution.py:123
  366.9 1.6 fusion.7
  368.6 2.9 collective-permute-done
  371.5 6.9 %eval_jaxpr.9 = (f32[4,8192]{1,0:T(4,128)}, bf16[4,8192]{1,0:T(4,128)(2,1)}) custom-call(s32[4]{0:T(128)S(1)} %get-tuple-element.443.sc_ref, f32[4,8192]{1,0:T(4,128)S(1)} %get-tuple-element.441.arr_ref, bf16[4,4,4,8192]{3,2,1,0:T(4,128)(2,1)S(1)} %get-tuple-element.463.tok_ref, f32[1,8192]{1,0:T(1,128)S(1)} %get-tuple-element.464.gain_ref, ...), custom_call_target="tpu_custom_call" | custom-call | tf_op jit(solution)/shard_map/while/body/eval_jaxpr/pallas_call | solution.py:123
  378.4 1.6 fusion.7
  380.0 2.9 collective-permute-done
  383.0 6.9 %eval_jaxpr.9 = (f32[4,8192]{1,0:T(4,128)}, bf16[4,8192]{1,0:T(4,128)(2,1)}) custom-call(s32[4]{0:T(128)S(1)} %get-tuple-element.443.sc_ref, f32[4,8192]{1,0:T(4,128)S(1)} %get-tuple-element.441.arr_ref, bf16[4,4,4,8192]{3,2,1,0:T(4,128)(2,1)S(1)} %get-tuple-element.463.tok_ref, f32[1,8192]{1,0:T(1,128)S(1)} %get-tuple-element.464.gain_ref, ...), custom_call_target="tpu_custom_call" | custom-call | tf_op jit(solution)/shard_map/while/body/eval_jaxpr/pallas_call | solution.py:123
  389.8 1.6 fusion.7
  391.5 2.9 collective-permute-done
  394.4 6.9 %eval_jaxpr.9 = (f32[4,8192]{1,0:T(4,128)}, bf16[4,8192]{1,0:T(4,128)(2,1)}) custom-call(s32[4]{0:T(128)S(1)} %get-tuple-element.443.sc_ref, f32[4,8192]{1,0:T(4,128)S(1)} %get-tuple-element.441.arr_ref, bf16[4,4,4,8192]{3,2,1,0:T(4,128)(2,1)S(1)} %get-tuple-element.463.tok_ref, f32[1,8192]{1,0:T(1,128)S(1)} %get-tuple-element.464.gain_ref, ...), custom_call_target="tpu_custom_call" | custom-call | tf_op jit(solution)/shard_map/while/body/eval_jaxpr/pallas_call | solution.py:123
  403.0 2.9 collective-permute-done
  405.9 6.9 %eval_jaxpr.9 = (f32[4,8192]{1,0:T(4,128)}, bf16[4,8192]{1,0:T(4,128)(2,1)}) custom-call(s32[4]{0:T(128)S(1)} %get-tuple-element.443.sc_ref, f32[4,8192]{1,0:T(4,128)S(1)} %get-tuple-element.441.arr_ref, bf16[4,4,4,8192]{3,2,1,0:T(4,128)(2,1)S(1)} %get-tuple-element.463.tok_ref, f32[1,8192]{1,0:T(1,128)S(1)} %get-tuple-element.464.gain_ref, ...), custom_call_target="tpu_custom_call" | custom-call | tf_op jit(solution)/shard_map/while/body/eval_jaxpr/pallas_call | solution.py:123
  414.4 2.9 collective-permute-done
  417.4 6.9 %eval_jaxpr.9 = (f32[4,8192]{1,0:T(4,128)}, bf16[4,8192]{1,0:T(4,128)(2,1)}) custom-call(s32[4]{0:T(128)S(1)} %get-tuple-element.443.sc_ref, f32[4,8192]{1,0:T(4,128)S(1)} %get-tuple-element.441.arr_ref, bf16[4,4,4,8192]{3,2,1,0:T(4,128)(2,1)S(1)} %get-tuple-element.463.tok_ref, f32[1,8192]{1,0:T(1,128)S(1)} %get-tuple-element.464.gain_ref, ...), custom_call_target="tpu_custom_call" | custom-call | tf_op jit(solution)/shard_map/while/body/eval_jaxpr/pallas_call | solution.py:123
  424.2 1.6 fusion.7
  425.9 2.9 collective-permute-done
  428.8 6.9 %eval_jaxpr.9 = (f32[4,8192]{1,0:T(4,128)}, bf16[4,8192]{1,0:T(4,128)(2,1)}) custom-call(s32[4]{0:T(128)S(1)} %get-tuple-element.443.sc_ref, f32[4,8192]{1,0:T(4,128)S(1)} %get-tuple-element.441.arr_ref, bf16[4,4,4,8192]{3,2,1,0:T(4,128)(2,1)S(1)} %get-tuple-element.463.tok_ref, f32[1,8192]{1,0:T(1,128)S(1)} %get-tuple-element.464.gain_ref, ...), custom_call_target="tpu_custom_call" | custom-call | tf_op jit(solution)/shard_map/while/body/eval_jaxpr/pallas_call | solution.py:123
  435.7 1.6 fusion.7
  437.4 2.9 collective-permute-done
  (56 shorter events, 11.4 us)
Async XLA Ops:
  0.6 5.0 %copy-start.1 = (s32[1024]{0:T(1024)S(1)}, s32[1024]{0:T(1024)}, u32[]{:S(2)}) copy-start(s32[1024]{0:T(1024)} %param.13) | copy-start | bytes 12292
  13.2 202.7 %all-to-all-start = ((bf16[64,32,2048]{2,1,0:T(8,128)(2,1)}), bf16[64,32,2048]{2,1,0:T(8,128)(2,1)}, u32[]{:S(2)}, u32[]{:S(2)}) async-start(bf16[64,32,2048]{2,1,0:T(8,128)(2,1)} %gather_fusion), calls=%async_computation | async-start | bytes 16777216 | tf_op jit(solution)/shard_map/all_to_all | solution.py:142
  40.1 182.3 %copy-start = (f32[1,8192]{1,0:T(1,128)S(1)}, f32[1,8192]{1,0:T(1,128)}, u32[]{:S(2)}) copy-start(f32[1,8192]{1,0:T(1,128)} %param.9) | copy-start | bytes 98308
  229.3 4.6 %collective-permute-start = (f32[4,8192]{1,0:T(4,128)}, f32[4,8192]{1,0:T(4,128)S(1)}, u32[]{:S(2)}, u32[]{:S(2)}) collective-permute-start(f32[4,8192]{1,0:T(4,128)} %get-tuple-element.419), channel_id=1, source_target_pairs={{192,0},{0,64},{64,128},{128,192},{193,1},{1,65},{65,129},{129,193... | collective-permute-start | bytes 393224 | tf_op jit(solution)/shard_map/while/body/eval_jaxpr/ppermute | solution.py:20
  240.7 4.6 %collective-permute-start = (f32[4,8192]{1,0:T(4,128)}, f32[4,8192]{1,0:T(4,128)S(1)}, u32[]{:S(2)}, u32[]{:S(2)}) collective-permute-start(f32[4,8192]{1,0:T(4,128)} %get-tuple-element.419), channel_id=1, source_target_pairs={{192,0},{0,64},{64,128},{128,192},{193,1},{1,65},{65,129},{129,193... | collective-permute-start | bytes 393224 | tf_op jit(solution)/shard_map/while/body/eval_jaxpr/ppermute | solution.py:20
  252.2 4.6 %collective-permute-start = (f32[4,8192]{1,0:T(4,128)}, f32[4,8192]{1,0:T(4,128)S(1)}, u32[]{:S(2)}, u32[]{:S(2)}) collective-permute-start(f32[4,8192]{1,0:T(4,128)} %get-tuple-element.419), channel_id=1, source_target_pairs={{192,0},{0,64},{64,128},{128,192},{193,1},{1,65},{65,129},{129,193... | collective-permute-start | bytes 393224 | tf_op jit(solution)/shard_map/while/body/eval_jaxpr/ppermute | solution.py:20
  263.7 4.6 %collective-permute-start = (f32[4,8192]{1,0:T(4,128)}, f32[4,8192]{1,0:T(4,128)S(1)}, u32[]{:S(2)}, u32[]{:S(2)}) collective-permute-start(f32[4,8192]{1,0:T(4,128)} %get-tuple-element.419), channel_id=1, source_target_pairs={{192,0},{0,64},{64,128},{128,192},{193,1},{1,65},{65,129},{129,193... | collective-permute-start | bytes 393224 | tf_op jit(solution)/shard_map/while/body/eval_jaxpr/ppermute | solution.py:20
  275.1 4.6 %collective-permute-start = (f32[4,8192]{1,0:T(4,128)}, f32[4,8192]{1,0:T(4,128)S(1)}, u32[]{:S(2)}, u32[]{:S(2)}) collective-permute-start(f32[4,8192]{1,0:T(4,128)} %get-tuple-element.419), channel_id=1, source_target_pairs={{192,0},{0,64},{64,128},{128,192},{193,1},{1,65},{65,129},{129,193... | collective-permute-start | bytes 393224 | tf_op jit(solution)/shard_map/while/body/eval_jaxpr/ppermute | solution.py:20
  286.6 4.6 %collective-permute-start = (f32[4,8192]{1,0:T(4,128)}, f32[4,8192]{1,0:T(4,128)S(1)}, u32[]{:S(2)}, u32[]{:S(2)}) collective-permute-start(f32[4,8192]{1,0:T(4,128)} %get-tuple-element.419), channel_id=1, source_target_pairs={{192,0},{0,64},{64,128},{128,192},{193,1},{1,65},{65,129},{129,193... | collective-permute-start | bytes 393224 | tf_op jit(solution)/shard_map/while/body/eval_jaxpr/ppermute | solution.py:20
  298.1 4.6 %collective-permute-start = (f32[4,8192]{1,0:T(4,128)}, f32[4,8192]{1,0:T(4,128)S(1)}, u32[]{:S(2)}, u32[]{:S(2)}) collective-permute-start(f32[4,8192]{1,0:T(4,128)} %get-tuple-element.419), channel_id=1, source_target_pairs={{192,0},{0,64},{64,128},{128,192},{193,1},{1,65},{65,129},{129,193... | collective-permute-start | bytes 393224 | tf_op jit(solution)/shard_map/while/body/eval_jaxpr/ppermute | solution.py:20
  309.5 4.6 %collective-permute-start = (f32[4,8192]{1,0:T(4,128)}, f32[4,8192]{1,0:T(4,128)S(1)}, u32[]{:S(2)}, u32[]{:S(2)}) collective-permute-start(f32[4,8192]{1,0:T(4,128)} %get-tuple-element.419), channel_id=1, source_target_pairs={{192,0},{0,64},{64,128},{128,192},{193,1},{1,65},{65,129},{129,193... | collective-permute-start | bytes 393224 | tf_op jit(solution)/shard_map/while/body/eval_jaxpr/ppermute | solution.py:20
  321.0 4.6 %collective-permute-start = (f32[4,8192]{1,0:T(4,128)}, f32[4,8192]{1,0:T(4,128)S(1)}, u32[]{:S(2)}, u32[]{:S(2)}) collective-permute-start(f32[4,8192]{1,0:T(4,128)} %get-tuple-element.419), channel_id=1, source_target_pairs={{192,0},{0,64},{64,128},{128,192},{193,1},{1,65},{65,129},{129,193... | collective-permute-start | bytes 393224 | tf_op jit(solution)/shard_map/while/body/eval_jaxpr/ppermute | solution.py:20
  332.5 4.6 %collective-permute-start = (f32[4,8192]{1,0:T(4,128)}, f32[4,8192]{1,0:T(4,128)S(1)}, u32[]{:S(2)}, u32[]{:S(2)}) collective-permute-start(f32[4,8192]{1,0:T(4,128)} %get-tuple-element.419), channel_id=1, source_target_pairs={{192,0},{0,64},{64,128},{128,192},{193,1},{1,65},{65,129},{129,193... | collective-permute-start | bytes 393224 | tf_op jit(solution)/shard_map/while/body/eval_jaxpr/ppermute | solution.py:20
  344.0 4.6 %collective-permute-start = (f32[4,8192]{1,0:T(4,128)}, f32[4,8192]{1,0:T(4,128)S(1)}, u32[]{:S(2)}, u32[]{:S(2)}) collective-permute-start(f32[4,8192]{1,0:T(4,128)} %get-tuple-element.419), channel_id=1, source_target_pairs={{192,0},{0,64},{64,128},{128,192},{193,1},{1,65},{65,129},{129,193... | collective-permute-start | bytes 393224 | tf_op jit(solution)/shard_map/while/body/eval_jaxpr/ppermute | solution.py:20
  355.4 4.6 %collective-permute-start = (f32[4,8192]{1,0:T(4,128)}, f32[4,8192]{1,0:T(4,128)S(1)}, u32[]{:S(2)}, u32[]{:S(2)}) collective-permute-start(f32[4,8192]{1,0:T(4,128)} %get-tuple-element.419), channel_id=1, source_target_pairs={{192,0},{0,64},{64,128},{128,192},{193,1},{1,65},{65,129},{129,193... | collective-permute-start | bytes 393224 | tf_op jit(solution)/shard_map/while/body/eval_jaxpr/ppermute | solution.py:20
  366.9 4.6 %collective-permute-start = (f32[4,8192]{1,0:T(4,128)}, f32[4,8192]{1,0:T(4,128)S(1)}, u32[]{:S(2)}, u32[]{:S(2)}) collective-permute-start(f32[4,8192]{1,0:T(4,128)} %get-tuple-element.419), channel_id=1, source_target_pairs={{192,0},{0,64},{64,128},{128,192},{193,1},{1,65},{65,129},{129,193... | collective-permute-start | bytes 393224 | tf_op jit(solution)/shard_map/while/body/eval_jaxpr/ppermute | solution.py:20
  378.4 4.6 %collective-permute-start = (f32[4,8192]{1,0:T(4,128)}, f32[4,8192]{1,0:T(4,128)S(1)}, u32[]{:S(2)}, u32[]{:S(2)}) collective-permute-start(f32[4,8192]{1,0:T(4,128)} %get-tuple-element.419), channel_id=1, source_target_pairs={{192,0},{0,64},{64,128},{128,192},{193,1},{1,65},{65,129},{129,193... | collective-permute-start | bytes 393224 | tf_op jit(solution)/shard_map/while/body/eval_jaxpr/ppermute | solution.py:20
  389.8 4.6 %collective-permute-start = (f32[4,8192]{1,0:T(4,128)}, f32[4,8192]{1,0:T(4,128)S(1)}, u32[]{:S(2)}, u32[]{:S(2)}) collective-permute-start(f32[4,8192]{1,0:T(4,128)} %get-tuple-element.419), channel_id=1, source_target_pairs={{192,0},{0,64},{64,128},{128,192},{193,1},{1,65},{65,129},{129,193... | collective-permute-start | bytes 393224 | tf_op jit(solution)/shard_map/while/body/eval_jaxpr/ppermute | solution.py:20
  401.3 4.6 %collective-permute-start = (f32[4,8192]{1,0:T(4,128)}, f32[4,8192]{1,0:T(4,128)S(1)}, u32[]{:S(2)}, u32[]{:S(2)}) collective-permute-start(f32[4,8192]{1,0:T(4,128)} %get-tuple-element.419), channel_id=1, source_target_pairs={{192,0},{0,64},{64,128},{128,192},{193,1},{1,65},{65,129},{129,193... | collective-permute-start | bytes 393224 | tf_op jit(solution)/shard_map/while/body/eval_jaxpr/ppermute | solution.py:20
  412.8 4.6 %collective-permute-start = (f32[4,8192]{1,0:T(4,128)}, f32[4,8192]{1,0:T(4,128)S(1)}, u32[]{:S(2)}, u32[]{:S(2)}) collective-permute-start(f32[4,8192]{1,0:T(4,128)} %get-tuple-element.419), channel_id=1, source_target_pairs={{192,0},{0,64},{64,128},{128,192},{193,1},{1,65},{65,129},{129,193... | collective-permute-start | bytes 393224 | tf_op jit(solution)/shard_map/while/body/eval_jaxpr/ppermute | solution.py:20
  424.2 4.6 %collective-permute-start = (f32[4,8192]{1,0:T(4,128)}, f32[4,8192]{1,0:T(4,128)S(1)}, u32[]{:S(2)}, u32[]{:S(2)}) collective-permute-start(f32[4,8192]{1,0:T(4,128)} %get-tuple-element.419), channel_id=1, source_target_pairs={{192,0},{0,64},{64,128},{128,192},{193,1},{1,65},{65,129},{129,193... | collective-permute-start | bytes 393224 | tf_op jit(solution)/shard_map/while/body/eval_jaxpr/ppermute | solution.py:20
  435.7 4.6 %collective-permute-start = (f32[4,8192]{1,0:T(4,128)}, f32[4,8192]{1,0:T(4,128)S(1)}, u32[]{:S(2)}, u32[]{:S(2)}) collective-permute-start(f32[4,8192]{1,0:T(4,128)} %get-tuple-element.419), channel_id=1, source_target_pairs={{192,0},{0,64},{64,128},{128,192},{193,1},{1,65},{65,129},{129,193... | collective-permute-start | bytes 393224 | tf_op jit(solution)/shard_map/while/body/eval_jaxpr/ppermute | solution.py:20

commit v4 on v3

--- a/solution.py
+++ b/solution.py
@@ -59,11 +59,14 @@
             head = block * head_block + h
             cols = slice(h * HEAD_DIM, (h + 1) * HEAD_DIM)
             q = q_ref[head].astype(jnp.bfloat16)
+            dims = (((1,), (1,)), ((), ()))
             prompt_scores = (
-                jnp.dot(q, pk_ref[cols, :], preferred_element_type=jnp.float32) * score_scale
+                lax.dot_general(q, pk_ref[:, cols], dims, preferred_element_type=jnp.float32)
+                * score_scale
             )
             cache_scores = (
-                jnp.dot(q, ck_ref[cols, :], preferred_element_type=jnp.float32) * score_scale
+                lax.dot_general(q, ck_ref[:, cols], dims, preferred_element_type=jnp.float32)
+                * score_scale
             )
             cache_scores = jnp.where(valid, cache_scores, NEG_FILL)
             highest = jnp.maximum(
@@ -92,7 +95,7 @@
     return kernel
 
 
-def stage(scalars, arrived, grouped_tokens, gains, prompt_keys_t, prompt, cache_keys_t, cache, hist_len):
+def stage(scalars, arrived, grouped_tokens, gains, prompt, cache, hist_len):
     rows, model_width = arrived.shape
     share = HEADS // KV_HEADS
     tokens = cache.shape[0] // (grouped_tokens.shape[1] * rows)
@@ -106,9 +109,9 @@
             pl.BlockSpec((rows, model_width), lambda i, sc: (0, 0)),
             pl.BlockSpec((None, None, rows, model_width), lambda i, sc: (sc[0], sc[1], 0, 0)),
             pl.BlockSpec((1, model_width), lambda i, sc: (0, 0)),
-            pl.BlockSpec((width, prompt_keys_t.shape[1]), lambda i, sc: (i, 0)),
+            pl.BlockSpec((prompt.shape[0], width), lambda i, sc: (0, i)),
             pl.BlockSpec((prompt.shape[0], width), lambda i, sc: (0, i + nb)),
-            pl.BlockSpec((width, rows * tokens), lambda i, sc: (i, sc[1])),
+            pl.BlockSpec((rows * tokens, width), lambda i, sc: (sc[1], i)),
             pl.BlockSpec((rows * tokens, width), lambda i, sc: (sc[1], i + nb)),
         ],
         out_specs=[
@@ -129,7 +132,7 @@
         ],
         compiler_params=pltpu.CompilerParams(dimension_semantics=("arbitrary",)),
         interpret=INTERPRET,
-    )(scalars, arrived, grouped_tokens, gains, prompt_keys_t, prompt, cache_keys_t, cache)
+    )(scalars, arrived, grouped_tokens, gains, prompt, prompt, cache, cache)
 
 
 def fork_cache(history, recent, ancestors, part_dev):
@@ -150,7 +153,6 @@
     part_dev = history_kv.shape[1]
     steps = new_kv.shape[1]
     model_width = token_states.shape[2]
-    half = KV_HEADS * HEAD_DIM
     gains = norm_gains
     prompt = prompt_kv[0]
     history = history_kv[0]
@@ -158,9 +160,7 @@
     cache = jnp.concatenate([history, jnp.transpose(recent, (1, 0, 2))], axis=1).reshape(
         -1, history.shape[2]
     )
-    prompt_keys_t = prompt[:, :half].T
-    cache_keys_t = cache[:, :half].T
-    groups = 4
+    groups = 2
     group_rows = part_dev // groups
     grouped_tokens = token_states.reshape(steps, groups, group_rows, model_width)
     moments = steps * section_count + groups - 1
@@ -183,7 +183,7 @@
         start = group_now * group_rows
         zero = jnp.zeros((), jnp.int32)
         residual, mixed = stage(
-            scalars, arrived, grouped_tokens, gains, prompt_keys_t, prompt, cache_keys_t, cache,
+            scalars, arrived, grouped_tokens, gains, prompt, cache,
             history.shape[1],
         )
         previous = lax.dynamic_slice(outbuf, (step_now, start, zero), (1, group_rows, model_width))

time: 443 us -> 454 us (1.025)
  waiting for transfers between devices: 232 us -> 260 us
  local copies, waits for them, and re-layouts: 28.6 us -> 16.8 us
    ppermute x19 -> x17, waiting for transfers between devices: 55.7 us -> 72.6 us  [passed_along(): return lax.ppermute(block, axis, route)]
    all_to_all x1, waiting for transfers between devices: 176 us -> 188 us  [fork_cache(): lax.all_to_all(outgoing, 'dp', split_axis=0, concat_axis=0, tiled=True)]
    while x2 -> x0, local copies, waits for them, and re-layouts: 6.23 us -> none  [local(): _, outbuf, _ = lax.fori_loop(0, moments, advance, start_carry)]
    pallas_call x19 -> x17, Pallas kernels: 130 us -> 128 us  [stage(): pl.pallas_call(stage_kernel(rows, tokens, hist_len, hb), grid_spec=grid_s...]
    dynamic_update_slice x19 -> x17, other arithmetic: 30.3 us -> 28.1 us  [advance(): outbuf = lax.dynamic_update_slice(outbuf, written, (step_now, start, zero))]
  transfers between devices with their start and end apart: 20 -> 18, of which waited for: 20 -> 18; matrix products, arithmetic and copies ran while one was open for 10% -> 7% of each run, Pallas kernels for 0% -> 0%
where the time goes in v4:
time: 454 us; the launch traced here: 452 us
  waiting for transfers between devices  260 us (57%)
  Pallas kernels  128 us (28%)
  other arithmetic  31.8 us (7%)
  local copies, waits for them, and re-layouts  16.8 us (4%)
  starting transfers between devices  14.8 us (3%)
    all_to_all x1, waiting for transfers between devices, fork_cache(): lax.all_to_all(outgoing, 'dp', split_axis=0, concat_axis=0, tiled=True)  188 us
    pallas_call x17, Pallas kernels, stage(): pl.pallas_call(stage_kernel(rows, tokens, hist_len, hb), grid_spec=grid_s...  128 us
    ppermute x17, waiting for transfers between devices, passed_along(): return lax.ppermute(block, axis, route)  72.6 us
    dynamic_update_slice x17, other arithmetic, advance(): outbuf = lax.dynamic_update_slice(outbuf, written, (step_now, start, zero))  28.1 us
    all_to_all x1, starting transfers between devices, fork_cache(): lax.all_to_all(outgoing, 'dp', split_axis=0, concat_axis=0, tiled=True)  14.8 us
  transfers between devices with their start and end apart: 18, of which 18 were waited for; matrix products, arithmetic and copies ran while one was open for 7% of the time, Pallas kernels for 0%

profile of v4, /device:TPU:6, one launch (start us, length us, event | category | flops | bytes accessed | tf_op | source)
XLA Modules:
  0.0 452.4 jit_solution(14243224572916860067)
XLA Ops:
  0.6 1.2 copy.14
  1.8 3.9 copy.13
  5.7 0.1 fusion.3
  5.9 2.1 pad_maximum_fusion
  8.0 5.3 %gather_fusion = bf16[64,32,2048]{2,1,0:T(8,128)(2,1)} fusion(bf16[16,32,2048]{2,1,0:T(8,128)(2,1)S(1)} %pad_maximum_fusion, s32[1024]{0:T(1024)S(1)} %pad_clamp_fusion.1), kind=kCustom, calls=%fused_computation | custom fusion | bytes 16777472 | tf_op jit(solution)/shard_map/jit(_take)/gather | solution.py:144
  13.2 14.8 %all-to-all-start = ((bf16[64,32,2048]{2,1,0:T(8,128)(2,1)}), bf16[64,32,2048]{2,1,0:T(8,128)(2,1)}, u32[]{:S(2)}, u32[]{:S(2)}) async-start(bf16[64,32,2048]{2,1,0:T(8,128)(2,1)} %gather_fusion), calls=%async_computation | async-start | bytes 16777216 | tf_op jit(solution)/shard_map/all_to_all | solution.py:145
  28.1 0.1 and_select_fusion
  28.2 0.1 pad_add_fusion.1
  28.3 187.7 %all-to-all-done = bf16[64,32,2048]{2,1,0:T(8,128)(2,1)} async-done(((bf16[64,32,2048]{2,1,0:T(8,128)(2,1)}), bf16[64,32,2048]{2,1,0:T(8,128)(2,1)}, u32[]{:S(2)}, u32[]{:S(2)}) %all-to-all-start) | async-done | bytes 8388640 | tf_op jit(solution)/shard_map/all_to_all | solution.py:145
  215.9 5.4 %gather_fusion.1 = bf16[16,32,2048]{2,1,0:T(8,128)(2,1)} fusion(bf16[64,32,2048]{2,1,0:T(8,128)(2,1)} %all-to-all-done, s32[1024]{0:T(1024)S(1)} %pad_clamp_fusion), kind=kCustom, calls=%fused_computation.1 | custom fusion | bytes 4194368 | tf_op jit(solution)/shard_map/jit(_take)/gather | solution.py:147
  221.3 1.0 broadcast_in_dim.34
  222.4 230.1 %while.20 = (s32[]{:T(128)}, f32[8,8192]{1,0:T(8,128)S(1)}, bf16[4,16,8192]{2,1,0:T(8,128)(2,1)}, s32[4]{0:T(128)S(1)}, bf16[4,2,8,8192]{3,2,1,0:T(8,128)(2,1)S(...) while((s32[]{:T(128)}, f32[8,8192]{1,0:T(8,128)S(1)}, ...), condition=%wide.region_1.2_spmd, body=%wide.region_0.1_spmd.sunk | while | flops 65610 | bytes 1442630 | solution.py:201
  222.4 7.5 %eval_jaxpr.9 = (f32[8,8192]{1,0:T(8,128)}, bf16[8,8192]{1,0:T(8,128)(2,1)}) custom-call(s32[4]{0:T(128)S(1)} %get-tuple-element.358.sc_ref, f32[8,8192]{1,0:T(8,128)S(1)} %get-tuple-element.356.arr_ref, bf16[4,2,8,8192]{3,2,1,0:T(8,128)(2,1)S(1)} %get-tuple-element.377.tok_ref, f32[1,8192]{1,0:T(1,128)S(1)} %get-tuple-element.378.gain_ref, ...), custom_call_target="tpu_custom_call" | custom-call | tf_op jit(solution)/shard_map/while/body/eval_jaxpr/pallas_call | solution.py:126
  229.9 1.7 fusion.7
  231.6 0.1 pad_add_fusion.3
  231.6 4.3 collective-permute-done
  235.9 7.5 %eval_jaxpr.9 = (f32[8,8192]{1,0:T(8,128)}, bf16[8,8192]{1,0:T(8,128)(2,1)}) custom-call(s32[4]{0:T(128)S(1)} %get-tuple-element.358.sc_ref, f32[8,8192]{1,0:T(8,128)S(1)} %get-tuple-element.356.arr_ref, bf16[4,2,8,8192]{3,2,1,0:T(8,128)(2,1)S(1)} %get-tuple-element.377.tok_ref, f32[1,8192]{1,0:T(1,128)S(1)} %get-tuple-element.378.gain_ref, ...), custom_call_target="tpu_custom_call" | custom-call | tf_op jit(solution)/shard_map/while/body/eval_jaxpr/pallas_call | solution.py:126
  243.4 1.7 fusion.7
  245.2 4.3 collective-permute-done
  249.5 7.5 %eval_jaxpr.9 = (f32[8,8192]{1,0:T(8,128)}, bf16[8,8192]{1,0:T(8,128)(2,1)}) custom-call(s32[4]{0:T(128)S(1)} %get-tuple-element.358.sc_ref, f32[8,8192]{1,0:T(8,128)S(1)} %get-tuple-element.356.arr_ref, bf16[4,2,8,8192]{3,2,1,0:T(8,128)(2,1)S(1)} %get-tuple-element.377.tok_ref, f32[1,8192]{1,0:T(1,128)S(1)} %get-tuple-element.378.gain_ref, ...), custom_call_target="tpu_custom_call" | custom-call | tf_op jit(solution)/shard_map/while/body/eval_jaxpr/pallas_call | solution.py:126
  257.0 1.7 fusion.7
  258.7 4.3 collective-permute-done
  263.0 7.5 %eval_jaxpr.9 = (f32[8,8192]{1,0:T(8,128)}, bf16[8,8192]{1,0:T(8,128)(2,1)}) custom-call(s32[4]{0:T(128)S(1)} %get-tuple-element.358.sc_ref, f32[8,8192]{1,0:T(8,128)S(1)} %get-tuple-element.356.arr_ref, bf16[4,2,8,8192]{3,2,1,0:T(8,128)(2,1)S(1)} %get-tuple-element.377.tok_ref, f32[1,8192]{1,0:T(1,128)S(1)} %get-tuple-element.378.gain_ref, ...), custom_call_target="tpu_custom_call" | custom-call | tf_op jit(solution)/shard_map/while/body/eval_jaxpr/pallas_call | solution.py:126
  270.5 1.7 fusion.7
  272.2 4.3 collective-permute-done
  276.5 7.5 %eval_jaxpr.9 = (f32[8,8192]{1,0:T(8,128)}, bf16[8,8192]{1,0:T(8,128)(2,1)}) custom-call(s32[4]{0:T(128)S(1)} %get-tuple-element.358.sc_ref, f32[8,8192]{1,0:T(8,128)S(1)} %get-tuple-element.356.arr_ref, bf16[4,2,8,8192]{3,2,1,0:T(8,128)(2,1)S(1)} %get-tuple-element.377.tok_ref, f32[1,8192]{1,0:T(1,128)S(1)} %get-tuple-element.378.gain_ref, ...), custom_call_target="tpu_custom_call" | custom-call | tf_op jit(solution)/shard_map/while/body/eval_jaxpr/pallas_call | solution.py:126
  284.0 1.7 fusion.7
  285.8 4.3 collective-permute-done
  290.1 7.5 %eval_jaxpr.9 = (f32[8,8192]{1,0:T(8,128)}, bf16[8,8192]{1,0:T(8,128)(2,1)}) custom-call(s32[4]{0:T(128)S(1)} %get-tuple-element.358.sc_ref, f32[8,8192]{1,0:T(8,128)S(1)} %get-tuple-element.356.arr_ref, bf16[4,2,8,8192]{3,2,1,0:T(8,128)(2,1)S(1)} %get-tuple-element.377.tok_ref, f32[1,8192]{1,0:T(1,128)S(1)} %get-tuple-element.378.gain_ref, ...), custom_call_target="tpu_custom_call" | custom-call | tf_op jit(solution)/shard_map/while/body/eval_jaxpr/pallas_call | solution.py:126
  297.6 1.7 fusion.7
  299.3 4.3 collective-permute-done
  303.6 7.5 %eval_jaxpr.9 = (f32[8,8192]{1,0:T(8,128)}, bf16[8,8192]{1,0:T(8,128)(2,1)}) custom-call(s32[4]{0:T(128)S(1)} %get-tuple-element.358.sc_ref, f32[8,8192]{1,0:T(8,128)S(1)} %get-tuple-element.356.arr_ref, bf16[4,2,8,8192]{3,2,1,0:T(8,128)(2,1)S(1)} %get-tuple-element.377.tok_ref, f32[1,8192]{1,0:T(1,128)S(1)} %get-tuple-element.378.gain_ref, ...), custom_call_target="tpu_custom_call" | custom-call | tf_op jit(solution)/shard_map/while/body/eval_jaxpr/pallas_call | solution.py:126
  311.1 1.7 fusion.7
  312.8 4.3 collective-permute-done
  317.1 7.5 %eval_jaxpr.9 = (f32[8,8192]{1,0:T(8,128)}, bf16[8,8192]{1,0:T(8,128)(2,1)}) custom-call(s32[4]{0:T(128)S(1)} %get-tuple-element.358.sc_ref, f32[8,8192]{1,0:T(8,128)S(1)} %get-tuple-element.356.arr_ref, bf16[4,2,8,8192]{3,2,1,0:T(8,128)(2,1)S(1)} %get-tuple-element.377.tok_ref, f32[1,8192]{1,0:T(1,128)S(1)} %get-tuple-element.378.gain_ref, ...), custom_call_target="tpu_custom_call" | custom-call | tf_op jit(solution)/shard_map/while/body/eval_jaxpr/pallas_call | solution.py:126
  324.6 1.7 fusion.7
  326.4 4.3 collective-permute-done
  330.7 7.5 %eval_jaxpr.9 = (f32[8,8192]{1,0:T(8,128)}, bf16[8,8192]{1,0:T(8,128)(2,1)}) custom-call(s32[4]{0:T(128)S(1)} %get-tuple-element.358.sc_ref, f32[8,8192]{1,0:T(8,128)S(1)} %get-tuple-element.356.arr_ref, bf16[4,2,8,8192]{3,2,1,0:T(8,128)(2,1)S(1)} %get-tuple-element.377.tok_ref, f32[1,8192]{1,0:T(1,128)S(1)} %get-tuple-element.378.gain_ref, ...), custom_call_target="tpu_custom_call" | custom-call | tf_op jit(solution)/shard_map/while/body/eval_jaxpr/pallas_call | solution.py:126
  338.2 1.7 fusion.7
  339.9 4.3 collective-permute-done
  344.2 7.5 %eval_jaxpr.9 = (f32[8,8192]{1,0:T(8,128)}, bf16[8,8192]{1,0:T(8,128)(2,1)}) custom-call(s32[4]{0:T(128)S(1)} %get-tuple-element.358.sc_ref, f32[8,8192]{1,0:T(8,128)S(1)} %get-tuple-element.356.arr_ref, bf16[4,2,8,8192]{3,2,1,0:T(8,128)(2,1)S(1)} %get-tuple-element.377.tok_ref, f32[1,8192]{1,0:T(1,128)S(1)} %get-tuple-element.378.gain_ref, ...), custom_call_target="tpu_custom_call" | custom-call | tf_op jit(solution)/shard_map/while/body/eval_jaxpr/pallas_call | solution.py:126
  351.7 1.7 fusion.7
  353.4 4.3 collective-permute-done
  357.7 7.5 %eval_jaxpr.9 = (f32[8,8192]{1,0:T(8,128)}, bf16[8,8192]{1,0:T(8,128)(2,1)}) custom-call(s32[4]{0:T(128)S(1)} %get-tuple-element.358.sc_ref, f32[8,8192]{1,0:T(8,128)S(1)} %get-tuple-element.356.arr_ref, bf16[4,2,8,8192]{3,2,1,0:T(8,128)(2,1)S(1)} %get-tuple-element.377.tok_ref, f32[1,8192]{1,0:T(1,128)S(1)} %get-tuple-element.378.gain_ref, ...), custom_call_target="tpu_custom_call" | custom-call | tf_op jit(solution)/shard_map/while/body/eval_jaxpr/pallas_call | solution.py:126
  365.2 1.7 fusion.7
  367.0 4.3 collective-permute-done
  371.2 7.5 %eval_jaxpr.9 = (f32[8,8192]{1,0:T(8,128)}, bf16[8,8192]{1,0:T(8,128)(2,1)}) custom-call(s32[4]{0:T(128)S(1)} %get-tuple-element.358.sc_ref, f32[8,8192]{1,0:T(8,128)S(1)} %get-tuple-element.356.arr_ref, bf16[4,2,8,8192]{3,2,1,0:T(8,128)(2,1)S(1)} %get-tuple-element.377.tok_ref, f32[1,8192]{1,0:T(1,128)S(1)} %get-tuple-element.378.gain_ref, ...), custom_call_target="tpu_custom_call" | custom-call | tf_op jit(solution)/shard_map/while/body/eval_jaxpr/pallas_call | solution.py:126
  378.8 1.7 fusion.7
  380.5 4.3 collective-permute-done
  384.8 7.5 %eval_jaxpr.9 = (f32[8,8192]{1,0:T(8,128)}, bf16[8,8192]{1,0:T(8,128)(2,1)}) custom-call(s32[4]{0:T(128)S(1)} %get-tuple-element.358.sc_ref, f32[8,8192]{1,0:T(8,128)S(1)} %get-tuple-element.356.arr_ref, bf16[4,2,8,8192]{3,2,1,0:T(8,128)(2,1)S(1)} %get-tuple-element.377.tok_ref, f32[1,8192]{1,0:T(1,128)S(1)} %get-tuple-element.378.gain_ref, ...), custom_call_target="tpu_custom_call" | custom-call | tf_op jit(solution)/shard_map/while/body/eval_jaxpr/pallas_call | solution.py:126
  392.3 1.7 fusion.7
  394.0 4.3 collective-permute-done
  398.3 7.5 %eval_jaxpr.9 = (f32[8,8192]{1,0:T(8,128)}, bf16[8,8192]{1,0:T(8,128)(2,1)}) custom-call(s32[4]{0:T(128)S(1)} %get-tuple-element.358.sc_ref, f32[8,8192]{1,0:T(8,128)S(1)} %get-tuple-element.356.arr_ref, bf16[4,2,8,8192]{3,2,1,0:T(8,128)(2,1)S(1)} %get-tuple-element.377.tok_ref, f32[1,8192]{1,0:T(1,128)S(1)} %get-tuple-element.378.gain_ref, ...), custom_call_target="tpu_custom_call" | custom-call | tf_op jit(solution)/shard_map/while/body/eval_jaxpr/pallas_call | solution.py:126
  405.8 1.7 fusion.7
  407.6 4.3 collective-permute-done
  411.8 7.5 %eval_jaxpr.9 = (f32[8,8192]{1,0:T(8,128)}, bf16[8,8192]{1,0:T(8,128)(2,1)}) custom-call(s32[4]{0:T(128)S(1)} %get-tuple-element.358.sc_ref, f32[8,8192]{1,0:T(8,128)S(1)} %get-tuple-element.356.arr_ref, bf16[4,2,8,8192]{3,2,1,0:T(8,128)(2,1)S(1)} %get-tuple-element.377.tok_ref, f32[1,8192]{1,0:T(1,128)S(1)} %get-tuple-element.378.gain_ref, ...), custom_call_target="tpu_custom_call" | custom-call | tf_op jit(solution)/shard_map/while/body/eval_jaxpr/pallas_call | solution.py:126
  419.4 1.7 fusion.7
  421.1 4.3 collective-permute-done
  425.4 7.5 %eval_jaxpr.9 = (f32[8,8192]{1,0:T(8,128)}, bf16[8,8192]{1,0:T(8,128)(2,1)}) custom-call(s32[4]{0:T(128)S(1)} %get-tuple-element.358.sc_ref, f32[8,8192]{1,0:T(8,128)S(1)} %get-tuple-element.356.arr_ref, bf16[4,2,8,8192]{3,2,1,0:T(8,128)(2,1)S(1)} %get-tuple-element.377.tok_ref, f32[1,8192]{1,0:T(1,128)S(1)} %get-tuple-element.378.gain_ref, ...), custom_call_target="tpu_custom_call" | custom-call | tf_op jit(solution)/shard_map/while/body/eval_jaxpr/pallas_call | solution.py:126
  432.9 1.7 fusion.7
  434.6 4.3 collective-permute-done
  438.9 7.5 %eval_jaxpr.9 = (f32[8,8192]{1,0:T(8,128)}, bf16[8,8192]{1,0:T(8,128)(2,1)}) custom-call(s32[4]{0:T(128)S(1)} %get-tuple-element.358.sc_ref, f32[8,8192]{1,0:T(8,128)S(1)} %get-tuple-element.356.arr_ref, bf16[4,2,8,8192]{3,2,1,0:T(8,128)(2,1)S(1)} %get-tuple-element.377.tok_ref, f32[1,8192]{1,0:T(1,128)S(1)} %get-tuple-element.378.gain_ref, ...), custom_call_target="tpu_custom_call" | custom-call | tf_op jit(solution)/shard_map/while/body/eval_jaxpr/pallas_call | solution.py:126
  446.4 1.7 fusion.7
  448.2 4.3 collective-permute-done
  (43 shorter events, 1.4 us)
Async XLA Ops:
  1.8 3.9 copy-start.2
  13.2 202.7 %all-to-all-start = ((bf16[64,32,2048]{2,1,0:T(8,128)(2,1)}), bf16[64,32,2048]{2,1,0:T(8,128)(2,1)}, u32[]{:S(2)}, u32[]{:S(2)}) async-start(bf16[64,32,2048]{2,1,0:T(8,128)(2,1)} %gather_fusion), calls=%async_computation | async-start | bytes 16777216 | tf_op jit(solution)/shard_map/all_to_all | solution.py:145
  28.2 194.1 %copy-start = (bf16[4,16,8192]{2,1,0:T(8,128)(2,1)S(1)}, bf16[4,16,8192]{2,1,0:T(8,128)(2,1)}, u32[]{:S(2)}) copy-start(bf16[4,16,8192]{2,1,0:T(8,128)(2,1)} %param.8) | copy-start | bytes 3145732
  28.2 194.1 %copy-start.1 = (f32[1,8192]{1,0:T(1,128)S(1)}, f32[1,8192]{1,0:T(1,128)}, u32[]{:S(2)}) copy-start(f32[1,8192]{1,0:T(1,128)} %param.9) | copy-start | bytes 98308
  229.9 6.0 %collective-permute-start = (f32[8,8192]{1,0:T(8,128)}, f32[8,8192]{1,0:T(8,128)S(1)}, u32[]{:S(2)}, u32[]{:S(2)}) collective-permute-start(f32[8,8192]{1,0:T(8,128)} %get-tuple-element.335), channel_id=1, source_target_pairs={{192,0},{0,64},{64,128},{128,192},{193,1},{1,65},{65,129},{129,193... | collective-permute-start | bytes 786440 | tf_op jit(solution)/shard_map/while/body/eval_jaxpr/ppermute | solution.py:20
  243.4 6.0 %collective-permute-start = (f32[8,8192]{1,0:T(8,128)}, f32[8,8192]{1,0:T(8,128)S(1)}, u32[]{:S(2)}, u32[]{:S(2)}) collective-permute-start(f32[8,8192]{1,0:T(8,128)} %get-tuple-element.335), channel_id=1, source_target_pairs={{192,0},{0,64},{64,128},{128,192},{193,1},{1,65},{65,129},{129,193... | collective-permute-start | bytes 786440 | tf_op jit(solution)/shard_map/while/body/eval_jaxpr/ppermute | solution.py:20
  257.0 6.0 %collective-permute-start = (f32[8,8192]{1,0:T(8,128)}, f32[8,8192]{1,0:T(8,128)S(1)}, u32[]{:S(2)}, u32[]{:S(2)}) collective-permute-start(f32[8,8192]{1,0:T(8,128)} %get-tuple-element.335), channel_id=1, source_target_pairs={{192,0},{0,64},{64,128},{128,192},{193,1},{1,65},{65,129},{129,193... | collective-permute-start | bytes 786440 | tf_op jit(solution)/shard_map/while/body/eval_jaxpr/ppermute | solution.py:20
  270.5 6.0 %collective-permute-start = (f32[8,8192]{1,0:T(8,128)}, f32[8,8192]{1,0:T(8,128)S(1)}, u32[]{:S(2)}, u32[]{:S(2)}) collective-permute-start(f32[8,8192]{1,0:T(8,128)} %get-tuple-element.335), channel_id=1, source_target_pairs={{192,0},{0,64},{64,128},{128,192},{193,1},{1,65},{65,129},{129,193... | collective-permute-start | bytes 786440 | tf_op jit(solution)/shard_map/while/body/eval_jaxpr/ppermute | solution.py:20
  284.0 6.0 %collective-permute-start = (f32[8,8192]{1,0:T(8,128)}, f32[8,8192]{1,0:T(8,128)S(1)}, u32[]{:S(2)}, u32[]{:S(2)}) collective-permute-start(f32[8,8192]{1,0:T(8,128)} %get-tuple-element.335), channel_id=1, source_target_pairs={{192,0},{0,64},{64,128},{128,192},{193,1},{1,65},{65,129},{129,193... | collective-permute-start | bytes 786440 | tf_op jit(solution)/shard_map/while/body/eval_jaxpr/ppermute | solution.py:20
  297.6 6.0 %collective-permute-start = (f32[8,8192]{1,0:T(8,128)}, f32[8,8192]{1,0:T(8,128)S(1)}, u32[]{:S(2)}, u32[]{:S(2)}) collective-permute-start(f32[8,8192]{1,0:T(8,128)} %get-tuple-element.335), channel_id=1, source_target_pairs={{192,0},{0,64},{64,128},{128,192},{193,1},{1,65},{65,129},{129,193... | collective-permute-start | bytes 786440 | tf_op jit(solution)/shard_map/while/body/eval_jaxpr/ppermute | solution.py:20
  311.1 6.0 %collective-permute-start = (f32[8,8192]{1,0:T(8,128)}, f32[8,8192]{1,0:T(8,128)S(1)}, u32[]{:S(2)}, u32[]{:S(2)}) collective-permute-start(f32[8,8192]{1,0:T(8,128)} %get-tuple-element.335), channel_id=1, source_target_pairs={{192,0},{0,64},{64,128},{128,192},{193,1},{1,65},{65,129},{129,193... | collective-permute-start | bytes 786440 | tf_op jit(solution)/shard_map/while/body/eval_jaxpr/ppermute | solution.py:20
  324.6 6.0 %collective-permute-start = (f32[8,8192]{1,0:T(8,128)}, f32[8,8192]{1,0:T(8,128)S(1)}, u32[]{:S(2)}, u32[]{:S(2)}) collective-permute-start(f32[8,8192]{1,0:T(8,128)} %get-tuple-element.335), channel_id=1, source_target_pairs={{192,0},{0,64},{64,128},{128,192},{193,1},{1,65},{65,129},{129,193... | collective-permute-start | bytes 786440 | tf_op jit(solution)/shard_map/while/body/eval_jaxpr/ppermute | solution.py:20
  338.2 6.0 %collective-permute-start = (f32[8,8192]{1,0:T(8,128)}, f32[8,8192]{1,0:T(8,128)S(1)}, u32[]{:S(2)}, u32[]{:S(2)}) collective-permute-start(f32[8,8192]{1,0:T(8,128)} %get-tuple-element.335), channel_id=1, source_target_pairs={{192,0},{0,64},{64,128},{128,192},{193,1},{1,65},{65,129},{129,193... | collective-permute-start | bytes 786440 | tf_op jit(solution)/shard_map/while/body/eval_jaxpr/ppermute | solution.py:20
  351.7 6.0 %collective-permute-start = (f32[8,8192]{1,0:T(8,128)}, f32[8,8192]{1,0:T(8,128)S(1)}, u32[]{:S(2)}, u32[]{:S(2)}) collective-permute-start(f32[8,8192]{1,0:T(8,128)} %get-tuple-element.335), channel_id=1, source_target_pairs={{192,0},{0,64},{64,128},{128,192},{193,1},{1,65},{65,129},{129,193... | collective-permute-start | bytes 786440 | tf_op jit(solution)/shard_map/while/body/eval_jaxpr/ppermute | solution.py:20
  365.2 6.0 %collective-permute-start = (f32[8,8192]{1,0:T(8,128)}, f32[8,8192]{1,0:T(8,128)S(1)}, u32[]{:S(2)}, u32[]{:S(2)}) collective-permute-start(f32[8,8192]{1,0:T(8,128)} %get-tuple-element.335), channel_id=1, source_target_pairs={{192,0},{0,64},{64,128},{128,192},{193,1},{1,65},{65,129},{129,193... | collective-permute-start | bytes 786440 | tf_op jit(solution)/shard_map/while/body/eval_jaxpr/ppermute | solution.py:20
  378.8 6.0 %collective-permute-start = (f32[8,8192]{1,0:T(8,128)}, f32[8,8192]{1,0:T(8,128)S(1)}, u32[]{:S(2)}, u32[]{:S(2)}) collective-permute-start(f32[8,8192]{1,0:T(8,128)} %get-tuple-element.335), channel_id=1, source_target_pairs={{192,0},{0,64},{64,128},{128,192},{193,1},{1,65},{65,129},{129,193... | collective-permute-start | bytes 786440 | tf_op jit(solution)/shard_map/while/body/eval_jaxpr/ppermute | solution.py:20
  392.3 6.0 %collective-permute-start = (f32[8,8192]{1,0:T(8,128)}, f32[8,8192]{1,0:T(8,128)S(1)}, u32[]{:S(2)}, u32[]{:S(2)}) collective-permute-start(f32[8,8192]{1,0:T(8,128)} %get-tuple-element.335), channel_id=1, source_target_pairs={{192,0},{0,64},{64,128},{128,192},{193,1},{1,65},{65,129},{129,193... | collective-permute-start | bytes 786440 | tf_op jit(solution)/shard_map/while/body/eval_jaxpr/ppermute | solution.py:20
  405.8 6.0 %collective-permute-start = (f32[8,8192]{1,0:T(8,128)}, f32[8,8192]{1,0:T(8,128)S(1)}, u32[]{:S(2)}, u32[]{:S(2)}) collective-permute-start(f32[8,8192]{1,0:T(8,128)} %get-tuple-element.335), channel_id=1, source_target_pairs={{192,0},{0,64},{64,128},{128,192},{193,1},{1,65},{65,129},{129,193... | collective-permute-start | bytes 786440 | tf_op jit(solution)/shard_map/while/body/eval_jaxpr/ppermute | solution.py:20
  419.4 6.0 %collective-permute-start = (f32[8,8192]{1,0:T(8,128)}, f32[8,8192]{1,0:T(8,128)S(1)}, u32[]{:S(2)}, u32[]{:S(2)}) collective-permute-start(f32[8,8192]{1,0:T(8,128)} %get-tuple-element.335), channel_id=1, source_target_pairs={{192,0},{0,64},{64,128},{128,192},{193,1},{1,65},{65,129},{129,193... | collective-permute-start | bytes 786440 | tf_op jit(solution)/shard_map/while/body/eval_jaxpr/ppermute | solution.py:20
  432.9 6.0 %collective-permute-start = (f32[8,8192]{1,0:T(8,128)}, f32[8,8192]{1,0:T(8,128)S(1)}, u32[]{:S(2)}, u32[]{:S(2)}) collective-permute-start(f32[8,8192]{1,0:T(8,128)} %get-tuple-element.335), channel_id=1, source_target_pairs={{192,0},{0,64},{64,128},{128,192},{193,1},{1,65},{65,129},{129,193... | collective-permute-start | bytes 786440 | tf_op jit(solution)/shard_map/while/body/eval_jaxpr/ppermute | solution.py:20
  446.4 6.0 %collective-permute-start = (f32[8,8192]{1,0:T(8,128)}, f32[8,8192]{1,0:T(8,128)S(1)}, u32[]{:S(2)}, u32[]{:S(2)}) collective-permute-start(f32[8,8192]{1,0:T(8,128)} %get-tuple-element.335), channel_id=1, source_target_pairs={{192,0},{0,64},{64,128},{128,192},{193,1},{1,65},{65,129},{129,193... | collective-permute-start | bytes 786440 | tf_op jit(solution)/shard_map/while/body/eval_jaxpr/ppermute | solution.py:20

commit v5 on v4

--- a/solution.py
+++ b/solution.py
@@ -51,7 +51,7 @@
                 q_ref[k] = queries[:, cols].reshape(rows * share, HEAD_DIM)
 
         step_now = sc_ref[0]
-        width = ck_ref.shape[1]
+        width = ck_ref.shape[0]
         row_id = lax.broadcasted_iota(jnp.int32, (rows * share, width), 0)
         col_id = lax.broadcasted_iota(jnp.int32, (rows * share, width), 1)
         valid = (row_id // share == col_id // tokens) & (col_id % tokens < hist + 1 + step_now)
@@ -77,13 +77,14 @@
             denominator = jnp.sum(prompt_exp, -1, keepdims=True) + jnp.sum(
                 cache_exp, -1, keepdims=True
             )
+            inverse = 1.0 / denominator
             mixed = jnp.dot(
-                (prompt_exp / denominator).astype(jnp.bfloat16),
+                (prompt_exp * inverse).astype(jnp.bfloat16),
                 pv_ref[:, cols],
                 preferred_element_type=jnp.float32,
             )
             mixed = mixed + jnp.dot(
-                (cache_exp / denominator).astype(jnp.bfloat16),
+                (cache_exp * inverse).astype(jnp.bfloat16),
                 cv_ref[:, cols],
                 preferred_element_type=jnp.float32,
             )
@@ -160,7 +161,7 @@
     cache = jnp.concatenate([history, jnp.transpose(recent, (1, 0, 2))], axis=1).reshape(
         -1, history.shape[2]
     )
-    groups = 2
+    groups = 4
     group_rows = part_dev // groups
     grouped_tokens = token_states.reshape(steps, groups, group_rows, model_width)
     moments = steps * section_count + groups - 1

time: 454 us -> 449 us (0.989)
  waiting for transfers between devices: 260 us -> 242 us
  Pallas kernels: 128 us -> 137 us
    ppermute x17 -> x19, waiting for transfers between devices: 72.6 us -> 55.7 us  [passed_along(): return lax.ppermute(block, axis, route)]
    pallas_call x17 -> x19, Pallas kernels: 128 us -> 137 us  [stage(): pl.pallas_call(stage_kernel(rows, tokens, hist_len, hb), grid_spec=grid_s...]
    dynamic_update_slice x17 -> x19, other arithmetic: 28.1 us -> 30.3 us  [advance(): outbuf = lax.dynamic_update_slice(outbuf, written, (step_now, start, zero))]
  transfers between devices with their start and end apart: 18 -> 20, of which waited for: 18 -> 20; matrix products, arithmetic and copies ran while one was open for 7% -> 7% of each run, Pallas kernels for 0% -> 0%
where the time goes in v5:
time: 449 us; the launch traced here: 447 us
  waiting for transfers between devices  242 us (54%)
  Pallas kernels  137 us (31%)
  other arithmetic  34.1 us (8%)
  local copies, waits for them, and re-layouts  18.3 us (4%)
  starting transfers between devices  14.8 us (3%)
    all_to_all x1, waiting for transfers between devices, fork_cache(): lax.all_to_all(outgoing, 'dp', split_axis=0, concat_axis=0, tiled=True)  186 us
    pallas_call x19, Pallas kernels, stage(): pl.pallas_call(stage_kernel(rows, tokens, hist_len, hb), grid_spec=grid_s...  137 us
    ppermute x19, waiting for transfers between devices, passed_along(): return lax.ppermute(block, axis, route)  55.7 us
    dynamic_update_slice x19, other arithmetic, advance(): outbuf = lax.dynamic_update_slice(outbuf, written, (step_now, start, zero))  30.3 us
    all_to_all x1, starting transfers between devices, fork_cache(): lax.all_to_all(outgoing, 'dp', split_axis=0, concat_axis=0, tiled=True)  14.8 us
  transfers between devices with their start and end apart: 20, of which 20 were waited for; matrix products, arithmetic and copies ran while one was open for 7% of the time, Pallas kernels for 0%

profile of v5, /device:TPU:6, one launch (start us, length us, event | category | flops | bytes accessed | tf_op | source)
XLA Modules:
  0.0 446.6 jit_solution(12102408964015973340)
XLA Ops:
  1.8 3.8 copy.13
  5.9 2.1 pad_maximum_fusion
  8.0 5.3 %gather_fusion = bf16[64,32,2048]{2,1,0:T(8,128)(2,1)} fusion(bf16[16,32,2048]{2,1,0:T(8,128)(2,1)S(1)} %pad_maximum_fusion, s32[1024]{0:T(1024)S(1)} %pad_clamp_fusion.1), kind=kCustom, calls=%fused_computation | custom fusion | bytes 16777472 | tf_op jit(solution)/shard_map/jit(_take)/gather | solution.py:145
  13.2 14.8 %all-to-all-start = ((bf16[64,32,2048]{2,1,0:T(8,128)(2,1)}), bf16[64,32,2048]{2,1,0:T(8,128)(2,1)}, u32[]{:S(2)}, u32[]{:S(2)}) async-start(bf16[64,32,2048]{2,1,0:T(8,128)(2,1)} %gather_fusion), calls=%async_computation | async-start | bytes 16777216 | tf_op jit(solution)/shard_map/all_to_all | solution.py:146
  29.7 186.2 %all-to-all-done = bf16[64,32,2048]{2,1,0:T(8,128)(2,1)} async-done(((bf16[64,32,2048]{2,1,0:T(8,128)(2,1)}), bf16[64,32,2048]{2,1,0:T(8,128)(2,1)}, u32[]{:S(2)}, u32[]{:S(2)}) %all-to-all-start) | async-done | bytes 8388640 | tf_op jit(solution)/shard_map/all_to_all | solution.py:146
  215.9 5.4 %gather_fusion.1 = bf16[16,32,2048]{2,1,0:T(8,128)(2,1)} fusion(bf16[64,32,2048]{2,1,0:T(8,128)(2,1)} %all-to-all-done, s32[1024]{0:T(1024)S(1)} %pad_clamp_fusion), kind=kCustom, calls=%fused_computation.1 | custom fusion | bytes 4194368 | tf_op jit(solution)/shard_map/jit(_take)/gather | solution.py:148
  222.4 224.2 %while.20 = (s32[]{:T(128)}, f32[4,8192]{1,0:T(4,128)S(1)}, bf16[4,16,8192]{2,1,0:T(8,128)(2,1)}, s32[4]{0:T(128)S(1)}, bf16[4,4,4,8192]{3,2,1,0:T(4,128)(2,1)S(...) while((s32[]{:T(128)}, f32[4,8192]{1,0:T(4,128)S(1)}, ...), condition=%wide.region_1.2_spmd, body=%wide.region_0.1_spmd.sunk | while | flops 32842 | bytes 721726 | solution.py:202
  222.4 7.2 %eval_jaxpr.9 = (f32[4,8192]{1,0:T(4,128)}, bf16[4,8192]{1,0:T(4,128)(2,1)}) custom-call(s32[4]{0:T(128)S(1)} %get-tuple-element.357.sc_ref, f32[4,8192]{1,0:T(4,128)S(1)} %get-tuple-element.355.arr_ref, bf16[4,4,4,8192]{3,2,1,0:T(4,128)(2,1)S(1)} %get-tuple-element.375.tok_ref, f32[1,8192]{1,0:T(1,128)S(1)} %get-tuple-element.376.gain_ref, ...), custom_call_target="tpu_custom_call" | custom-call | tf_op jit(solution)/shard_map/while/body/eval_jaxpr/pallas_call | solution.py:127
  229.6 1.6 fusion.7
  231.3 2.9 collective-permute-done
  234.2 7.2 %eval_jaxpr.9 = (f32[4,8192]{1,0:T(4,128)}, bf16[4,8192]{1,0:T(4,128)(2,1)}) custom-call(s32[4]{0:T(128)S(1)} %get-tuple-element.357.sc_ref, f32[4,8192]{1,0:T(4,128)S(1)} %get-tuple-element.355.arr_ref, bf16[4,4,4,8192]{3,2,1,0:T(4,128)(2,1)S(1)} %get-tuple-element.375.tok_ref, f32[1,8192]{1,0:T(1,128)S(1)} %get-tuple-element.376.gain_ref, ...), custom_call_target="tpu_custom_call" | custom-call | tf_op jit(solution)/shard_map/while/body/eval_jaxpr/pallas_call | solution.py:127
  241.4 1.6 fusion.7
  243.1 2.9 collective-permute-done
  246.0 7.2 %eval_jaxpr.9 = (f32[4,8192]{1,0:T(4,128)}, bf16[4,8192]{1,0:T(4,128)(2,1)}) custom-call(s32[4]{0:T(128)S(1)} %get-tuple-element.357.sc_ref, f32[4,8192]{1,0:T(4,128)S(1)} %get-tuple-element.355.arr_ref, bf16[4,4,4,8192]{3,2,1,0:T(4,128)(2,1)S(1)} %get-tuple-element.375.tok_ref, f32[1,8192]{1,0:T(1,128)S(1)} %get-tuple-element.376.gain_ref, ...), custom_call_target="tpu_custom_call" | custom-call | tf_op jit(solution)/shard_map/while/body/eval_jaxpr/pallas_call | solution.py:127
  253.2 1.6 fusion.7
  254.9 2.9 collective-permute-done
  257.8 7.2 %eval_jaxpr.9 = (f32[4,8192]{1,0:T(4,128)}, bf16[4,8192]{1,0:T(4,128)(2,1)}) custom-call(s32[4]{0:T(128)S(1)} %get-tuple-element.357.sc_ref, f32[4,8192]{1,0:T(4,128)S(1)} %get-tuple-element.355.arr_ref, bf16[4,4,4,8192]{3,2,1,0:T(4,128)(2,1)S(1)} %get-tuple-element.375.tok_ref, f32[1,8192]{1,0:T(1,128)S(1)} %get-tuple-element.376.gain_ref, ...), custom_call_target="tpu_custom_call" | custom-call | tf_op jit(solution)/shard_map/while/body/eval_jaxpr/pallas_call | solution.py:127
  265.0 1.6 fusion.7
  266.7 2.9 collective-permute-done
  269.6 7.2 %eval_jaxpr.9 = (f32[4,8192]{1,0:T(4,128)}, bf16[4,8192]{1,0:T(4,128)(2,1)}) custom-call(s32[4]{0:T(128)S(1)} %get-tuple-element.357.sc_ref, f32[4,8192]{1,0:T(4,128)S(1)} %get-tuple-element.355.arr_ref, bf16[4,4,4,8192]{3,2,1,0:T(4,128)(2,1)S(1)} %get-tuple-element.375.tok_ref, f32[1,8192]{1,0:T(1,128)S(1)} %get-tuple-element.376.gain_ref, ...), custom_call_target="tpu_custom_call" | custom-call | tf_op jit(solution)/shard_map/while/body/eval_jaxpr/pallas_call | solution.py:127
  276.8 1.6 fusion.7
  278.5 2.9 collective-permute-done
  281.4 7.2 %eval_jaxpr.9 = (f32[4,8192]{1,0:T(4,128)}, bf16[4,8192]{1,0:T(4,128)(2,1)}) custom-call(s32[4]{0:T(128)S(1)} %get-tuple-element.357.sc_ref, f32[4,8192]{1,0:T(4,128)S(1)} %get-tuple-element.355.arr_ref, bf16[4,4,4,8192]{3,2,1,0:T(4,128)(2,1)S(1)} %get-tuple-element.375.tok_ref, f32[1,8192]{1,0:T(1,128)S(1)} %get-tuple-element.376.gain_ref, ...), custom_call_target="tpu_custom_call" | custom-call | tf_op jit(solution)/shard_map/while/body/eval_jaxpr/pallas_call | solution.py:127
  288.6 1.6 fusion.7
  290.3 2.9 collective-permute-done
  293.2 7.2 %eval_jaxpr.9 = (f32[4,8192]{1,0:T(4,128)}, bf16[4,8192]{1,0:T(4,128)(2,1)}) custom-call(s32[4]{0:T(128)S(1)} %get-tuple-element.357.sc_ref, f32[4,8192]{1,0:T(4,128)S(1)} %get-tuple-element.355.arr_ref, bf16[4,4,4,8192]{3,2,1,0:T(4,128)(2,1)S(1)} %get-tuple-element.375.tok_ref, f32[1,8192]{1,0:T(1,128)S(1)} %get-tuple-element.376.gain_ref, ...), custom_call_target="tpu_custom_call" | custom-call | tf_op jit(solution)/shard_map/while/body/eval_jaxpr/pallas_call | solution.py:127
  300.4 1.6 fusion.7
  302.1 2.9 collective-permute-done
  305.0 7.2 %eval_jaxpr.9 = (f32[4,8192]{1,0:T(4,128)}, bf16[4,8192]{1,0:T(4,128)(2,1)}) custom-call(s32[4]{0:T(128)S(1)} %get-tuple-element.357.sc_ref, f32[4,8192]{1,0:T(4,128)S(1)} %get-tuple-element.355.arr_ref, bf16[4,4,4,8192]{3,2,1,0:T(4,128)(2,1)S(1)} %get-tuple-element.375.tok_ref, f32[1,8192]{1,0:T(1,128)S(1)} %get-tuple-element.376.gain_ref, ...), custom_call_target="tpu_custom_call" | custom-call | tf_op jit(solution)/shard_map/while/body/eval_jaxpr/pallas_call | solution.py:127
  312.2 1.6 fusion.7
  313.9 2.9 collective-permute-done
  316.8 7.2 %eval_jaxpr.9 = (f32[4,8192]{1,0:T(4,128)}, bf16[4,8192]{1,0:T(4,128)(2,1)}) custom-call(s32[4]{0:T(128)S(1)} %get-tuple-element.357.sc_ref, f32[4,8192]{1,0:T(4,128)S(1)} %get-tuple-element.355.arr_ref, bf16[4,4,4,8192]{3,2,1,0:T(4,128)(2,1)S(1)} %get-tuple-element.375.tok_ref, f32[1,8192]{1,0:T(1,128)S(1)} %get-tuple-element.376.gain_ref, ...), custom_call_target="tpu_custom_call" | custom-call | tf_op jit(solution)/shard_map/while/body/eval_jaxpr/pallas_call | solution.py:127
  324.0 1.6 fusion.7
  325.7 2.9 collective-permute-done
  328.6 7.2 %eval_jaxpr.9 = (f32[4,8192]{1,0:T(4,128)}, bf16[4,8192]{1,0:T(4,128)(2,1)}) custom-call(s32[4]{0:T(128)S(1)} %get-tuple-element.357.sc_ref, f32[4,8192]{1,0:T(4,128)S(1)} %get-tuple-element.355.arr_ref, bf16[4,4,4,8192]{3,2,1,0:T(4,128)(2,1)S(1)} %get-tuple-element.375.tok_ref, f32[1,8192]{1,0:T(1,128)S(1)} %get-tuple-element.376.gain_ref, ...), custom_call_target="tpu_custom_call" | custom-call | tf_op jit(solution)/shard_map/while/body/eval_jaxpr/pallas_call | solution.py:127
  335.8 1.6 fusion.7
  337.5 2.9 collective-permute-done
  340.4 7.2 %eval_jaxpr.9 = (f32[4,8192]{1,0:T(4,128)}, bf16[4,8192]{1,0:T(4,128)(2,1)}) custom-call(s32[4]{0:T(128)S(1)} %get-tuple-element.357.sc_ref, f32[4,8192]{1,0:T(4,128)S(1)} %get-tuple-element.355.arr_ref, bf16[4,4,4,8192]{3,2,1,0:T(4,128)(2,1)S(1)} %get-tuple-element.375.tok_ref, f32[1,8192]{1,0:T(1,128)S(1)} %get-tuple-element.376.gain_ref, ...), custom_call_target="tpu_custom_call" | custom-call | tf_op jit(solution)/shard_map/while/body/eval_jaxpr/pallas_call | solution.py:127
  347.6 1.6 fusion.7
  349.3 2.9 collective-permute-done
  352.2 7.2 %eval_jaxpr.9 = (f32[4,8192]{1,0:T(4,128)}, bf16[4,8192]{1,0:T(4,128)(2,1)}) custom-call(s32[4]{0:T(128)S(1)} %get-tuple-element.357.sc_ref, f32[4,8192]{1,0:T(4,128)S(1)} %get-tuple-element.355.arr_ref, bf16[4,4,4,8192]{3,2,1,0:T(4,128)(2,1)S(1)} %get-tuple-element.375.tok_ref, f32[1,8192]{1,0:T(1,128)S(1)} %get-tuple-element.376.gain_ref, ...), custom_call_target="tpu_custom_call" | custom-call | tf_op jit(solution)/shard_map/while/body/eval_jaxpr/pallas_call | solution.py:127
  359.4 1.6 fusion.7
  361.1 2.9 collective-permute-done
  364.0 7.2 %eval_jaxpr.9 = (f32[4,8192]{1,0:T(4,128)}, bf16[4,8192]{1,0:T(4,128)(2,1)}) custom-call(s32[4]{0:T(128)S(1)} %get-tuple-element.357.sc_ref, f32[4,8192]{1,0:T(4,128)S(1)} %get-tuple-element.355.arr_ref, bf16[4,4,4,8192]{3,2,1,0:T(4,128)(2,1)S(1)} %get-tuple-element.375.tok_ref, f32[1,8192]{1,0:T(1,128)S(1)} %get-tuple-element.376.gain_ref, ...), custom_call_target="tpu_custom_call" | custom-call | tf_op jit(solution)/shard_map/while/body/eval_jaxpr/pallas_call | solution.py:127
  371.2 1.6 fusion.7
  372.9 2.9 collective-permute-done
  375.8 7.2 %eval_jaxpr.9 = (f32[4,8192]{1,0:T(4,128)}, bf16[4,8192]{1,0:T(4,128)(2,1)}) custom-call(s32[4]{0:T(128)S(1)} %get-tuple-element.357.sc_ref, f32[4,8192]{1,0:T(4,128)S(1)} %get-tuple-element.355.arr_ref, bf16[4,4,4,8192]{3,2,1,0:T(4,128)(2,1)S(1)} %get-tuple-element.375.tok_ref, f32[1,8192]{1,0:T(1,128)S(1)} %get-tuple-element.376.gain_ref, ...), custom_call_target="tpu_custom_call" | custom-call | tf_op jit(solution)/shard_map/while/body/eval_jaxpr/pallas_call | solution.py:127
  383.0 1.6 fusion.7
  384.7 2.9 collective-permute-done
  387.6 7.2 %eval_jaxpr.9 = (f32[4,8192]{1,0:T(4,128)}, bf16[4,8192]{1,0:T(4,128)(2,1)}) custom-call(s32[4]{0:T(128)S(1)} %get-tuple-element.357.sc_ref, f32[4,8192]{1,0:T(4,128)S(1)} %get-tuple-element.355.arr_ref, bf16[4,4,4,8192]{3,2,1,0:T(4,128)(2,1)S(1)} %get-tuple-element.375.tok_ref, f32[1,8192]{1,0:T(1,128)S(1)} %get-tuple-element.376.gain_ref, ...), custom_call_target="tpu_custom_call" | custom-call | tf_op jit(solution)/shard_map/while/body/eval_jaxpr/pallas_call | solution.py:127
  394.8 1.6 fusion.7
  396.5 2.9 collective-permute-done
  399.4 7.2 %eval_jaxpr.9 = (f32[4,8192]{1,0:T(4,128)}, bf16[4,8192]{1,0:T(4,128)(2,1)}) custom-call(s32[4]{0:T(128)S(1)} %get-tuple-element.357.sc_ref, f32[4,8192]{1,0:T(4,128)S(1)} %get-tuple-element.355.arr_ref, bf16[4,4,4,8192]{3,2,1,0:T(4,128)(2,1)S(1)} %get-tuple-element.375.tok_ref, f32[1,8192]{1,0:T(1,128)S(1)} %get-tuple-element.376.gain_ref, ...), custom_call_target="tpu_custom_call" | custom-call | tf_op jit(solution)/shard_map/while/body/eval_jaxpr/pallas_call | solution.py:127
  406.6 1.6 fusion.7
  408.3 2.9 collective-permute-done
  411.2 7.2 %eval_jaxpr.9 = (f32[4,8192]{1,0:T(4,128)}, bf16[4,8192]{1,0:T(4,128)(2,1)}) custom-call(s32[4]{0:T(128)S(1)} %get-tuple-element.357.sc_ref, f32[4,8192]{1,0:T(4,128)S(1)} %get-tuple-element.355.arr_ref, bf16[4,4,4,8192]{3,2,1,0:T(4,128)(2,1)S(1)} %get-tuple-element.375.tok_ref, f32[1,8192]{1,0:T(1,128)S(1)} %get-tuple-element.376.gain_ref, ...), custom_call_target="tpu_custom_call" | custom-call | tf_op jit(solution)/shard_map/while/body/eval_jaxpr/pallas_call | solution.py:127
  418.4 1.6 fusion.7
  420.1 2.9 collective-permute-done
  423.0 7.2 %eval_jaxpr.9 = (f32[4,8192]{1,0:T(4,128)}, bf16[4,8192]{1,0:T(4,128)(2,1)}) custom-call(s32[4]{0:T(128)S(1)} %get-tuple-element.357.sc_ref, f32[4,8192]{1,0:T(4,128)S(1)} %get-tuple-element.355.arr_ref, bf16[4,4,4,8192]{3,2,1,0:T(4,128)(2,1)S(1)} %get-tuple-element.375.tok_ref, f32[1,8192]{1,0:T(1,128)S(1)} %get-tuple-element.376.gain_ref, ...), custom_call_target="tpu_custom_call" | custom-call | tf_op jit(solution)/shard_map/while/body/eval_jaxpr/pallas_call | solution.py:127
  430.2 1.6 fusion.7
  431.9 2.9 collective-permute-done
  434.8 7.2 %eval_jaxpr.9 = (f32[4,8192]{1,0:T(4,128)}, bf16[4,8192]{1,0:T(4,128)(2,1)}) custom-call(s32[4]{0:T(128)S(1)} %get-tuple-element.357.sc_ref, f32[4,8192]{1,0:T(4,128)S(1)} %get-tuple-element.355.arr_ref, bf16[4,4,4,8192]{3,2,1,0:T(4,128)(2,1)S(1)} %get-tuple-element.375.tok_ref, f32[1,8192]{1,0:T(1,128)S(1)} %get-tuple-element.376.gain_ref, ...), custom_call_target="tpu_custom_call" | custom-call | tf_op jit(solution)/shard_map/while/body/eval_jaxpr/pallas_call | solution.py:127
  442.0 1.6 fusion.7
  443.7 2.9 collective-permute-done
  (52 shorter events, 5.6 us)
Async XLA Ops:
  0.6 5.0 %copy-start.1 = (s32[1024]{0:T(1024)S(1)}, s32[1024]{0:T(1024)}, u32[]{:S(2)}) copy-start(s32[1024]{0:T(1024)} %param.13) | copy-start | bytes 12292
  13.2 202.7 %all-to-all-start = ((bf16[64,32,2048]{2,1,0:T(8,128)(2,1)}), bf16[64,32,2048]{2,1,0:T(8,128)(2,1)}, u32[]{:S(2)}, u32[]{:S(2)}) async-start(bf16[64,32,2048]{2,1,0:T(8,128)(2,1)} %gather_fusion), calls=%async_computation | async-start | bytes 16777216 | tf_op jit(solution)/shard_map/all_to_all | solution.py:146
  29.7 192.7 %copy-start = (f32[1,8192]{1,0:T(1,128)S(1)}, f32[1,8192]{1,0:T(1,128)}, u32[]{:S(2)}) copy-start(f32[1,8192]{1,0:T(1,128)} %param.9) | copy-start | bytes 98308
  229.6 4.6 %collective-permute-start = (f32[4,8192]{1,0:T(4,128)}, f32[4,8192]{1,0:T(4,128)S(1)}, u32[]{:S(2)}, u32[]{:S(2)}) collective-permute-start(f32[4,8192]{1,0:T(4,128)} %get-tuple-element.335), channel_id=1, source_target_pairs={{192,0},{0,64},{64,128},{128,192},{193,1},{1,65},{65,129},{129,193... | collective-permute-start | bytes 393224 | tf_op jit(solution)/shard_map/while/body/eval_jaxpr/ppermute | solution.py:20
  241.4 4.6 %collective-permute-start = (f32[4,8192]{1,0:T(4,128)}, f32[4,8192]{1,0:T(4,128)S(1)}, u32[]{:S(2)}, u32[]{:S(2)}) collective-permute-start(f32[4,8192]{1,0:T(4,128)} %get-tuple-element.335), channel_id=1, source_target_pairs={{192,0},{0,64},{64,128},{128,192},{193,1},{1,65},{65,129},{129,193... | collective-permute-start | bytes 393224 | tf_op jit(solution)/shard_map/while/body/eval_jaxpr/ppermute | solution.py:20
  253.2 4.6 %collective-permute-start = (f32[4,8192]{1,0:T(4,128)}, f32[4,8192]{1,0:T(4,128)S(1)}, u32[]{:S(2)}, u32[]{:S(2)}) collective-permute-start(f32[4,8192]{1,0:T(4,128)} %get-tuple-element.335), channel_id=1, source_target_pairs={{192,0},{0,64},{64,128},{128,192},{193,1},{1,65},{65,129},{129,193... | collective-permute-start | bytes 393224 | tf_op jit(solution)/shard_map/while/body/eval_jaxpr/ppermute | solution.py:20
  265.0 4.6 %collective-permute-start = (f32[4,8192]{1,0:T(4,128)}, f32[4,8192]{1,0:T(4,128)S(1)}, u32[]{:S(2)}, u32[]{:S(2)}) collective-permute-start(f32[4,8192]{1,0:T(4,128)} %get-tuple-element.335), channel_id=1, source_target_pairs={{192,0},{0,64},{64,128},{128,192},{193,1},{1,65},{65,129},{129,193... | collective-permute-start | bytes 393224 | tf_op jit(solution)/shard_map/while/body/eval_jaxpr/ppermute | solution.py:20
  276.8 4.6 %collective-permute-start = (f32[4,8192]{1,0:T(4,128)}, f32[4,8192]{1,0:T(4,128)S(1)}, u32[]{:S(2)}, u32[]{:S(2)}) collective-permute-start(f32[4,8192]{1,0:T(4,128)} %get-tuple-element.335), channel_id=1, source_target_pairs={{192,0},{0,64},{64,128},{128,192},{193,1},{1,65},{65,129},{129,193... | collective-permute-start | bytes 393224 | tf_op jit(solution)/shard_map/while/body/eval_jaxpr/ppermute | solution.py:20
  288.6 4.6 %collective-permute-start = (f32[4,8192]{1,0:T(4,128)}, f32[4,8192]{1,0:T(4,128)S(1)}, u32[]{:S(2)}, u32[]{:S(2)}) collective-permute-start(f32[4,8192]{1,0:T(4,128)} %get-tuple-element.335), channel_id=1, source_target_pairs={{192,0},{0,64},{64,128},{128,192},{193,1},{1,65},{65,129},{129,193... | collective-permute-start | bytes 393224 | tf_op jit(solution)/shard_map/while/body/eval_jaxpr/ppermute | solution.py:20
  300.4 4.6 %collective-permute-start = (f32[4,8192]{1,0:T(4,128)}, f32[4,8192]{1,0:T(4,128)S(1)}, u32[]{:S(2)}, u32[]{:S(2)}) collective-permute-start(f32[4,8192]{1,0:T(4,128)} %get-tuple-element.335), channel_id=1, source_target_pairs={{192,0},{0,64},{64,128},{128,192},{193,1},{1,65},{65,129},{129,193... | collective-permute-start | bytes 393224 | tf_op jit(solution)/shard_map/while/body/eval_jaxpr/ppermute | solution.py:20
  312.2 4.6 %collective-permute-start = (f32[4,8192]{1,0:T(4,128)}, f32[4,8192]{1,0:T(4,128)S(1)}, u32[]{:S(2)}, u32[]{:S(2)}) collective-permute-start(f32[4,8192]{1,0:T(4,128)} %get-tuple-element.335), channel_id=1, source_target_pairs={{192,0},{0,64},{64,128},{128,192},{193,1},{1,65},{65,129},{129,193... | collective-permute-start | bytes 393224 | tf_op jit(solution)/shard_map/while/body/eval_jaxpr/ppermute | solution.py:20
  324.0 4.6 %collective-permute-start = (f32[4,8192]{1,0:T(4,128)}, f32[4,8192]{1,0:T(4,128)S(1)}, u32[]{:S(2)}, u32[]{:S(2)}) collective-permute-start(f32[4,8192]{1,0:T(4,128)} %get-tuple-element.335), channel_id=1, source_target_pairs={{192,0},{0,64},{64,128},{128,192},{193,1},{1,65},{65,129},{129,193... | collective-permute-start | bytes 393224 | tf_op jit(solution)/shard_map/while/body/eval_jaxpr/ppermute | solution.py:20
  335.8 4.6 %collective-permute-start = (f32[4,8192]{1,0:T(4,128)}, f32[4,8192]{1,0:T(4,128)S(1)}, u32[]{:S(2)}, u32[]{:S(2)}) collective-permute-start(f32[4,8192]{1,0:T(4,128)} %get-tuple-element.335), channel_id=1, source_target_pairs={{192,0},{0,64},{64,128},{128,192},{193,1},{1,65},{65,129},{129,193... | collective-permute-start | bytes 393224 | tf_op jit(solution)/shard_map/while/body/eval_jaxpr/ppermute | solution.py:20
  347.6 4.6 %collective-permute-start = (f32[4,8192]{1,0:T(4,128)}, f32[4,8192]{1,0:T(4,128)S(1)}, u32[]{:S(2)}, u32[]{:S(2)}) collective-permute-start(f32[4,8192]{1,0:T(4,128)} %get-tuple-element.335), channel_id=1, source_target_pairs={{192,0},{0,64},{64,128},{128,192},{193,1},{1,65},{65,129},{129,193... | collective-permute-start | bytes 393224 | tf_op jit(solution)/shard_map/while/body/eval_jaxpr/ppermute | solution.py:20
  359.4 4.6 %collective-permute-start = (f32[4,8192]{1,0:T(4,128)}, f32[4,8192]{1,0:T(4,128)S(1)}, u32[]{:S(2)}, u32[]{:S(2)}) collective-permute-start(f32[4,8192]{1,0:T(4,128)} %get-tuple-element.335), channel_id=1, source_target_pairs={{192,0},{0,64},{64,128},{128,192},{193,1},{1,65},{65,129},{129,193... | collective-permute-start | bytes 393224 | tf_op jit(solution)/shard_map/while/body/eval_jaxpr/ppermute | solution.py:20
  371.2 4.6 %collective-permute-start = (f32[4,8192]{1,0:T(4,128)}, f32[4,8192]{1,0:T(4,128)S(1)}, u32[]{:S(2)}, u32[]{:S(2)}) collective-permute-start(f32[4,8192]{1,0:T(4,128)} %get-tuple-element.335), channel_id=1, source_target_pairs={{192,0},{0,64},{64,128},{128,192},{193,1},{1,65},{65,129},{129,193... | collective-permute-start | bytes 393224 | tf_op jit(solution)/shard_map/while/body/eval_jaxpr/ppermute | solution.py:20
  383.0 4.6 %collective-permute-start = (f32[4,8192]{1,0:T(4,128)}, f32[4,8192]{1,0:T(4,128)S(1)}, u32[]{:S(2)}, u32[]{:S(2)}) collective-permute-start(f32[4,8192]{1,0:T(4,128)} %get-tuple-element.335), channel_id=1, source_target_pairs={{192,0},{0,64},{64,128},{128,192},{193,1},{1,65},{65,129},{129,193... | collective-permute-start | bytes 393224 | tf_op jit(solution)/shard_map/while/body/eval_jaxpr/ppermute | solution.py:20
  394.8 4.6 %collective-permute-start = (f32[4,8192]{1,0:T(4,128)}, f32[4,8192]{1,0:T(4,128)S(1)}, u32[]{:S(2)}, u32[]{:S(2)}) collective-permute-start(f32[4,8192]{1,0:T(4,128)} %get-tuple-element.335), channel_id=1, source_target_pairs={{192,0},{0,64},{64,128},{128,192},{193,1},{1,65},{65,129},{129,193... | collective-permute-start | bytes 393224 | tf_op jit(solution)/shard_map/while/body/eval_jaxpr/ppermute | solution.py:20
  406.6 4.6 %collective-permute-start = (f32[4,8192]{1,0:T(4,128)}, f32[4,8192]{1,0:T(4,128)S(1)}, u32[]{:S(2)}, u32[]{:S(2)}) collective-permute-start(f32[4,8192]{1,0:T(4,128)} %get-tuple-element.335), channel_id=1, source_target_pairs={{192,0},{0,64},{64,128},{128,192},{193,1},{1,65},{65,129},{129,193... | collective-permute-start | bytes 393224 | tf_op jit(solution)/shard_map/while/body/eval_jaxpr/ppermute | solution.py:20
  418.4 4.6 %collective-permute-start = (f32[4,8192]{1,0:T(4,128)}, f32[4,8192]{1,0:T(4,128)S(1)}, u32[]{:S(2)}, u32[]{:S(2)}) collective-permute-start(f32[4,8192]{1,0:T(4,128)} %get-tuple-element.335), channel_id=1, source_target_pairs={{192,0},{0,64},{64,128},{128,192},{193,1},{1,65},{65,129},{129,193... | collective-permute-start | bytes 393224 | tf_op jit(solution)/shard_map/while/body/eval_jaxpr/ppermute | solution.py:20
  430.2 4.6 %collective-permute-start = (f32[4,8192]{1,0:T(4,128)}, f32[4,8192]{1,0:T(4,128)S(1)}, u32[]{:S(2)}, u32[]{:S(2)}) collective-permute-start(f32[4,8192]{1,0:T(4,128)} %get-tuple-element.335), channel_id=1, source_target_pairs={{192,0},{0,64},{64,128},{128,192},{193,1},{1,65},{65,129},{129,193... | collective-permute-start | bytes 393224 | tf_op jit(solution)/shard_map/while/body/eval_jaxpr/ppermute | solution.py:20
  442.0 4.6 %collective-permute-start = (f32[4,8192]{1,0:T(4,128)}, f32[4,8192]{1,0:T(4,128)S(1)}, u32[]{:S(2)}, u32[]{:S(2)}) collective-permute-start(f32[4,8192]{1,0:T(4,128)} %get-tuple-element.335), channel_id=1, source_target_pairs={{192,0},{0,64},{64,128},{128,192},{193,1},{1,65},{65,129},{129,193... | collective-permute-start | bytes 393224 | tf_op jit(solution)/shard_map/while/body/eval_jaxpr/ppermute | solution.py:20

commit v6 on v5

--- a/solution.py
+++ b/solution.py
@@ -24,7 +24,7 @@
     return values * lax.rsqrt(jnp.mean(values * values, axis=-1, keepdims=True) + 1e-05)
 
 
-HEAD_BLOCK = 2
+HEAD_BLOCK = 4
 INTERPRET = False
 
 
@@ -55,20 +55,29 @@
         row_id = lax.broadcasted_iota(jnp.int32, (rows * share, width), 0)
         col_id = lax.broadcasted_iota(jnp.int32, (rows * share, width), 1)
         valid = (row_id // share == col_id // tokens) & (col_id % tokens < hist + 1 + step_now)
+        dims = (((1,), (1,)), ((), ()))
+
+        def scores(h):
+            head = block * head_block + h
+            cols = slice(h * HEAD_DIM, (h + 1) * HEAD_DIM)
+            q = q_ref[head].astype(jnp.bfloat16)
+            prompt_scores = (
+                lax.dot_general(q, pk_ref[:, cols], dims, preferred_element_type=jnp.float32)
+                * score_scale
+            )
+            cache_scores = (
+                lax.dot_general(q, ck_ref[:, cols], dims, preferred_element_type=jnp.float32)
+                * score_scale
+            )
+            return prompt_scores, jnp.where(valid, cache_scores, NEG_FILL)
+
+        pending = scores(0)
         for h in range(head_block):
             head = block * head_block + h
             cols = slice(h * HEAD_DIM, (h + 1) * HEAD_DIM)
-            q = q_ref[head].astype(jnp.bfloat16)
-            dims = (((1,), (1,)), ((), ()))
-            prompt_scores = (
-                lax.dot_general(q, pk_ref[:, cols], dims, preferred_element_type=jnp.float32)
-                * score_scale
-            )
-            cache_scores = (
-                lax.dot_general(q, ck_ref[:, cols], dims, preferred_element_type=jnp.float32)
-                * score_scale
-            )
-            cache_scores = jnp.where(valid, cache_scores, NEG_FILL)
+            prompt_scores, cache_scores = pending
+            if h + 1 < head_block:
+                pending = scores(h + 1)
             highest = jnp.maximum(
                 jnp.max(prompt_scores, -1, keepdims=True), jnp.max(cache_scores, -1, keepdims=True)
             )

time: 449 us -> 416 us (0.927)
  Pallas kernels: 137 us -> 106 us
    pallas_call x19, Pallas kernels: 137 us -> 106 us  [stage(): pl.pallas_call(stage_kernel(rows, tokens, hist_len, hb), grid_spec=grid_s...]
  transfers between devices with their start and end apart: 20 -> 20, of which waited for: 20 -> 20; matrix products, arithmetic and copies ran while one was open for 7% -> 8% of each run, Pallas kernels for 0% -> 0%
where the time goes in v6:
time: 416 us
  waiting for transfers between devices  242 us (58%)
  Pallas kernels  106 us (25%)
  other arithmetic  34.1 us (8%)
  local copies, waits for them, and re-layouts  18.3 us (4%)
  starting transfers between devices  14.8 us (4%)
    all_to_all x1, waiting for transfers between devices, fork_cache(): lax.all_to_all(outgoing, 'dp', split_axis=0, concat_axis=0, tiled=True)  186 us
    pallas_call x19, Pallas kernels, stage(): pl.pallas_call(stage_kernel(rows, tokens, hist_len, hb), grid_spec=grid_s...  106 us
    ppermute x19, waiting for transfers between devices, passed_along(): return lax.ppermute(block, axis, route)  55.7 us
    dynamic_update_slice x19, other arithmetic, advance(): outbuf = lax.dynamic_update_slice(outbuf, written, (step_now, start, zero))  30.2 us
    all_to_all x1, starting transfers between devices, fork_cache(): lax.all_to_all(outgoing, 'dp', split_axis=0, concat_axis=0, tiled=True)  14.8 us
  transfers between devices with their start and end apart: 20, of which 20 were waited for; matrix products, arithmetic and copies ran while one was open for 8% of the time, Pallas kernels for 0%

profile of v6, /device:TPU:6, one launch (start us, length us, event | category | flops | bytes accessed | tf_op | source)
XLA Modules:
  0.0 415.7 jit_solution(405122573869024994)
XLA Ops:
  1.8 3.8 copy.13
  5.9 2.1 pad_maximum_fusion
  8.0 5.3 %gather_fusion = bf16[64,32,2048]{2,1,0:T(8,128)(2,1)} fusion(bf16[16,32,2048]{2,1,0:T(8,128)(2,1)S(1)} %pad_maximum_fusion, s32[1024]{0:T(1024)S(1)} %pad_clamp_fusion.1), kind=kCustom, calls=%fused_computation | custom fusion | bytes 16777472 | tf_op jit(solution)/shard_map/jit(_take)/gather | solution.py:154
  13.2 14.8 %all-to-all-start = ((bf16[64,32,2048]{2,1,0:T(8,128)(2,1)}), bf16[64,32,2048]{2,1,0:T(8,128)(2,1)}, u32[]{:S(2)}, u32[]{:S(2)}) async-start(bf16[64,32,2048]{2,1,0:T(8,128)(2,1)} %gather_fusion), calls=%async_computation | async-start | bytes 16777216 | tf_op jit(solution)/shard_map/all_to_all | solution.py:155
  29.7 186.2 %all-to-all-done = bf16[64,32,2048]{2,1,0:T(8,128)(2,1)} async-done(((bf16[64,32,2048]{2,1,0:T(8,128)(2,1)}), bf16[64,32,2048]{2,1,0:T(8,128)(2,1)}, u32[]{:S(2)}, u32[]{:S(2)}) %all-to-all-start) | async-done | bytes 8388640 | tf_op jit(solution)/shard_map/all_to_all | solution.py:155
  215.9 5.4 %gather_fusion.1 = bf16[16,32,2048]{2,1,0:T(8,128)(2,1)} fusion(bf16[64,32,2048]{2,1,0:T(8,128)(2,1)} %all-to-all-done, s32[1024]{0:T(1024)S(1)} %pad_clamp_fusion), kind=kCustom, calls=%fused_computation.1 | custom fusion | bytes 4194368 | tf_op jit(solution)/shard_map/jit(_take)/gather | solution.py:157
  222.4 193.3 %while.20 = (s32[]{:T(128)}, f32[4,8192]{1,0:T(4,128)S(1)}, bf16[4,16,8192]{2,1,0:T(8,128)(2,1)}, s32[4]{0:T(128)S(1)}, bf16[4,4,4,8192]{3,2,1,0:T(4,128)(2,1)S(...) while((s32[]{:T(128)}, f32[4,8192]{1,0:T(4,128)S(1)}, ...), condition=%wide.region_1.2_spmd, body=%wide.region_0.1_spmd.sunk | while | flops 32842 | bytes 721726 | solution.py:211
  222.4 5.6 %eval_jaxpr.9 = (f32[4,8192]{1,0:T(4,128)}, bf16[4,8192]{1,0:T(4,128)(2,1)}) custom-call(s32[4]{0:T(128)S(1)} %get-tuple-element.357.sc_ref, f32[4,8192]{1,0:T(4,128)S(1)} %get-tuple-element.355.arr_ref, bf16[4,4,4,8192]{3,2,1,0:T(4,128)(2,1)S(1)} %get-tuple-element.375.tok_ref, f32[1,8192]{1,0:T(1,128)S(1)} %get-tuple-element.376.gain_ref, ...), custom_call_target="tpu_custom_call" | custom-call | tf_op jit(solution)/shard_map/while/body/eval_jaxpr/pallas_call | solution.py:136
  228.0 1.6 fusion.7
  229.6 2.9 collective-permute-done
  232.6 5.6 %eval_jaxpr.9 = (f32[4,8192]{1,0:T(4,128)}, bf16[4,8192]{1,0:T(4,128)(2,1)}) custom-call(s32[4]{0:T(128)S(1)} %get-tuple-element.357.sc_ref, f32[4,8192]{1,0:T(4,128)S(1)} %get-tuple-element.355.arr_ref, bf16[4,4,4,8192]{3,2,1,0:T(4,128)(2,1)S(1)} %get-tuple-element.375.tok_ref, f32[1,8192]{1,0:T(1,128)S(1)} %get-tuple-element.376.gain_ref, ...), custom_call_target="tpu_custom_call" | custom-call | tf_op jit(solution)/shard_map/while/body/eval_jaxpr/pallas_call | solution.py:136
  238.1 1.6 fusion.7
  239.8 2.9 collective-permute-done
  242.7 5.6 %eval_jaxpr.9 = (f32[4,8192]{1,0:T(4,128)}, bf16[4,8192]{1,0:T(4,128)(2,1)}) custom-call(s32[4]{0:T(128)S(1)} %get-tuple-element.357.sc_ref, f32[4,8192]{1,0:T(4,128)S(1)} %get-tuple-element.355.arr_ref, bf16[4,4,4,8192]{3,2,1,0:T(4,128)(2,1)S(1)} %get-tuple-element.375.tok_ref, f32[1,8192]{1,0:T(1,128)S(1)} %get-tuple-element.376.gain_ref, ...), custom_call_target="tpu_custom_call" | custom-call | tf_op jit(solution)/shard_map/while/body/eval_jaxpr/pallas_call | solution.py:136
  248.3 1.6 fusion.7
  250.0 2.9 collective-permute-done
  252.9 5.6 %eval_jaxpr.9 = (f32[4,8192]{1,0:T(4,128)}, bf16[4,8192]{1,0:T(4,128)(2,1)}) custom-call(s32[4]{0:T(128)S(1)} %get-tuple-element.357.sc_ref, f32[4,8192]{1,0:T(4,128)S(1)} %get-tuple-element.355.arr_ref, bf16[4,4,4,8192]{3,2,1,0:T(4,128)(2,1)S(1)} %get-tuple-element.375.tok_ref, f32[1,8192]{1,0:T(1,128)S(1)} %get-tuple-element.376.gain_ref, ...), custom_call_target="tpu_custom_call" | custom-call | tf_op jit(solution)/shard_map/while/body/eval_jaxpr/pallas_call | solution.py:136
  258.5 1.6 fusion.7
  260.2 2.9 collective-permute-done
  263.1 5.6 %eval_jaxpr.9 = (f32[4,8192]{1,0:T(4,128)}, bf16[4,8192]{1,0:T(4,128)(2,1)}) custom-call(s32[4]{0:T(128)S(1)} %get-tuple-element.357.sc_ref, f32[4,8192]{1,0:T(4,128)S(1)} %get-tuple-element.355.arr_ref, bf16[4,4,4,8192]{3,2,1,0:T(4,128)(2,1)S(1)} %get-tuple-element.375.tok_ref, f32[1,8192]{1,0:T(1,128)S(1)} %get-tuple-element.376.gain_ref, ...), custom_call_target="tpu_custom_call" | custom-call | tf_op jit(solution)/shard_map/while/body/eval_jaxpr/pallas_call | solution.py:136
  268.7 1.6 fusion.7
  270.3 2.9 collective-permute-done
  273.3 5.6 %eval_jaxpr.9 = (f32[4,8192]{1,0:T(4,128)}, bf16[4,8192]{1,0:T(4,128)(2,1)}) custom-call(s32[4]{0:T(128)S(1)} %get-tuple-element.357.sc_ref, f32[4,8192]{1,0:T(4,128)S(1)} %get-tuple-element.355.arr_ref, bf16[4,4,4,8192]{3,2,1,0:T(4,128)(2,1)S(1)} %get-tuple-element.375.tok_ref, f32[1,8192]{1,0:T(1,128)S(1)} %get-tuple-element.376.gain_ref, ...), custom_call_target="tpu_custom_call" | custom-call | tf_op jit(solution)/shard_map/while/body/eval_jaxpr/pallas_call | solution.py:136
  278.8 1.6 fusion.7
  280.5 2.9 collective-permute-done
  283.4 5.6 %eval_jaxpr.9 = (f32[4,8192]{1,0:T(4,128)}, bf16[4,8192]{1,0:T(4,128)(2,1)}) custom-call(s32[4]{0:T(128)S(1)} %get-tuple-element.357.sc_ref, f32[4,8192]{1,0:T(4,128)S(1)} %get-tuple-element.355.arr_ref, bf16[4,4,4,8192]{3,2,1,0:T(4,128)(2,1)S(1)} %get-tuple-element.375.tok_ref, f32[1,8192]{1,0:T(1,128)S(1)} %get-tuple-element.376.gain_ref, ...), custom_call_target="tpu_custom_call" | custom-call | tf_op jit(solution)/shard_map/while/body/eval_jaxpr/pallas_call | solution.py:136
  289.0 1.6 fusion.7
  290.7 2.9 collective-permute-done
  293.6 5.6 %eval_jaxpr.9 = (f32[4,8192]{1,0:T(4,128)}, bf16[4,8192]{1,0:T(4,128)(2,1)}) custom-call(s32[4]{0:T(128)S(1)} %get-tuple-element.357.sc_ref, f32[4,8192]{1,0:T(4,128)S(1)} %get-tuple-element.355.arr_ref, bf16[4,4,4,8192]{3,2,1,0:T(4,128)(2,1)S(1)} %get-tuple-element.375.tok_ref, f32[1,8192]{1,0:T(1,128)S(1)} %get-tuple-element.376.gain_ref, ...), custom_call_target="tpu_custom_call" | custom-call | tf_op jit(solution)/shard_map/while/body/eval_jaxpr/pallas_call | solution.py:136
  299.2 1.6 fusion.7
  300.8 2.9 collective-permute-done
  303.8 5.6 %eval_jaxpr.9 = (f32[4,8192]{1,0:T(4,128)}, bf16[4,8192]{1,0:T(4,128)(2,1)}) custom-call(s32[4]{0:T(128)S(1)} %get-tuple-element.357.sc_ref, f32[4,8192]{1,0:T(4,128)S(1)} %get-tuple-element.355.arr_ref, bf16[4,4,4,8192]{3,2,1,0:T(4,128)(2,1)S(1)} %get-tuple-element.375.tok_ref, f32[1,8192]{1,0:T(1,128)S(1)} %get-tuple-element.376.gain_ref, ...), custom_call_target="tpu_custom_call" | custom-call | tf_op jit(solution)/shard_map/while/body/eval_jaxpr/pallas_call | solution.py:136
  309.3 1.6 fusion.7
  311.0 2.9 collective-permute-done
  313.9 5.6 %eval_jaxpr.9 = (f32[4,8192]{1,0:T(4,128)}, bf16[4,8192]{1,0:T(4,128)(2,1)}) custom-call(s32[4]{0:T(128)S(1)} %get-tuple-element.357.sc_ref, f32[4,8192]{1,0:T(4,128)S(1)} %get-tuple-element.355.arr_ref, bf16[4,4,4,8192]{3,2,1,0:T(4,128)(2,1)S(1)} %get-tuple-element.375.tok_ref, f32[1,8192]{1,0:T(1,128)S(1)} %get-tuple-element.376.gain_ref, ...), custom_call_target="tpu_custom_call" | custom-call | tf_op jit(solution)/shard_map/while/body/eval_jaxpr/pallas_call | solution.py:136
  319.5 1.6 fusion.7
  321.2 2.9 collective-permute-done
  324.1 5.6 %eval_jaxpr.9 = (f32[4,8192]{1,0:T(4,128)}, bf16[4,8192]{1,0:T(4,128)(2,1)}) custom-call(s32[4]{0:T(128)S(1)} %get-tuple-element.357.sc_ref, f32[4,8192]{1,0:T(4,128)S(1)} %get-tuple-element.355.arr_ref, bf16[4,4,4,8192]{3,2,1,0:T(4,128)(2,1)S(1)} %get-tuple-element.375.tok_ref, f32[1,8192]{1,0:T(1,128)S(1)} %get-tuple-element.376.gain_ref, ...), custom_call_target="tpu_custom_call" | custom-call | tf_op jit(solution)/shard_map/while/body/eval_jaxpr/pallas_call | solution.py:136
  329.7 1.6 fusion.7
  331.4 2.9 collective-permute-done
  334.3 5.6 %eval_jaxpr.9 = (f32[4,8192]{1,0:T(4,128)}, bf16[4,8192]{1,0:T(4,128)(2,1)}) custom-call(s32[4]{0:T(128)S(1)} %get-tuple-element.357.sc_ref, f32[4,8192]{1,0:T(4,128)S(1)} %get-tuple-element.355.arr_ref, bf16[4,4,4,8192]{3,2,1,0:T(4,128)(2,1)S(1)} %get-tuple-element.375.tok_ref, f32[1,8192]{1,0:T(1,128)S(1)} %get-tuple-element.376.gain_ref, ...), custom_call_target="tpu_custom_call" | custom-call | tf_op jit(solution)/shard_map/while/body/eval_jaxpr/pallas_call | solution.py:136
  339.9 1.6 fusion.7
  341.5 2.9 collective-permute-done
  344.5 5.6 %eval_jaxpr.9 = (f32[4,8192]{1,0:T(4,128)}, bf16[4,8192]{1,0:T(4,128)(2,1)}) custom-call(s32[4]{0:T(128)S(1)} %get-tuple-element.357.sc_ref, f32[4,8192]{1,0:T(4,128)S(1)} %get-tuple-element.355.arr_ref, bf16[4,4,4,8192]{3,2,1,0:T(4,128)(2,1)S(1)} %get-tuple-element.375.tok_ref, f32[1,8192]{1,0:T(1,128)S(1)} %get-tuple-element.376.gain_ref, ...), custom_call_target="tpu_custom_call" | custom-call | tf_op jit(solution)/shard_map/while/body/eval_jaxpr/pallas_call | solution.py:136
  350.0 1.6 fusion.7
  351.7 2.9 collective-permute-done
  354.6 5.6 %eval_jaxpr.9 = (f32[4,8192]{1,0:T(4,128)}, bf16[4,8192]{1,0:T(4,128)(2,1)}) custom-call(s32[4]{0:T(128)S(1)} %get-tuple-element.357.sc_ref, f32[4,8192]{1,0:T(4,128)S(1)} %get-tuple-element.355.arr_ref, bf16[4,4,4,8192]{3,2,1,0:T(4,128)(2,1)S(1)} %get-tuple-element.375.tok_ref, f32[1,8192]{1,0:T(1,128)S(1)} %get-tuple-element.376.gain_ref, ...), custom_call_target="tpu_custom_call" | custom-call | tf_op jit(solution)/shard_map/while/body/eval_jaxpr/pallas_call | solution.py:136
  360.2 1.6 fusion.7
  361.9 2.9 collective-permute-done
  364.8 5.6 %eval_jaxpr.9 = (f32[4,8192]{1,0:T(4,128)}, bf16[4,8192]{1,0:T(4,128)(2,1)}) custom-call(s32[4]{0:T(128)S(1)} %get-tuple-element.357.sc_ref, f32[4,8192]{1,0:T(4,128)S(1)} %get-tuple-element.355.arr_ref, bf16[4,4,4,8192]{3,2,1,0:T(4,128)(2,1)S(1)} %get-tuple-element.375.tok_ref, f32[1,8192]{1,0:T(1,128)S(1)} %get-tuple-element.376.gain_ref, ...), custom_call_target="tpu_custom_call" | custom-call | tf_op jit(solution)/shard_map/while/body/eval_jaxpr/pallas_call | solution.py:136
  370.4 1.6 fusion.7
  372.0 2.9 collective-permute-done
  375.0 5.6 %eval_jaxpr.9 = (f32[4,8192]{1,0:T(4,128)}, bf16[4,8192]{1,0:T(4,128)(2,1)}) custom-call(s32[4]{0:T(128)S(1)} %get-tuple-element.357.sc_ref, f32[4,8192]{1,0:T(4,128)S(1)} %get-tuple-element.355.arr_ref, bf16[4,4,4,8192]{3,2,1,0:T(4,128)(2,1)S(1)} %get-tuple-element.375.tok_ref, f32[1,8192]{1,0:T(1,128)S(1)} %get-tuple-element.376.gain_ref, ...), custom_call_target="tpu_custom_call" | custom-call | tf_op jit(solution)/shard_map/while/body/eval_jaxpr/pallas_call | solution.py:136
  380.6 1.6 fusion.7
  382.2 2.9 collective-permute-done
  385.2 5.6 %eval_jaxpr.9 = (f32[4,8192]{1,0:T(4,128)}, bf16[4,8192]{1,0:T(4,128)(2,1)}) custom-call(s32[4]{0:T(128)S(1)} %get-tuple-element.357.sc_ref, f32[4,8192]{1,0:T(4,128)S(1)} %get-tuple-element.355.arr_ref, bf16[4,4,4,8192]{3,2,1,0:T(4,128)(2,1)S(1)} %get-tuple-element.375.tok_ref, f32[1,8192]{1,0:T(1,128)S(1)} %get-tuple-element.376.gain_ref, ...), custom_call_target="tpu_custom_call" | custom-call | tf_op jit(solution)/shard_map/while/body/eval_jaxpr/pallas_call | solution.py:136
  390.7 1.6 fusion.7
  392.4 2.9 collective-permute-done
  395.3 5.6 %eval_jaxpr.9 = (f32[4,8192]{1,0:T(4,128)}, bf16[4,8192]{1,0:T(4,128)(2,1)}) custom-call(s32[4]{0:T(128)S(1)} %get-tuple-element.357.sc_ref, f32[4,8192]{1,0:T(4,128)S(1)} %get-tuple-element.355.arr_ref, bf16[4,4,4,8192]{3,2,1,0:T(4,128)(2,1)S(1)} %get-tuple-element.375.tok_ref, f32[1,8192]{1,0:T(1,128)S(1)} %get-tuple-element.376.gain_ref, ...), custom_call_target="tpu_custom_call" | custom-call | tf_op jit(solution)/shard_map/while/body/eval_jaxpr/pallas_call | solution.py:136
  400.9 1.6 fusion.7
  402.6 2.9 collective-permute-done
  405.5 5.6 %eval_jaxpr.9 = (f32[4,8192]{1,0:T(4,128)}, bf16[4,8192]{1,0:T(4,128)(2,1)}) custom-call(s32[4]{0:T(128)S(1)} %get-tuple-element.357.sc_ref, f32[4,8192]{1,0:T(4,128)S(1)} %get-tuple-element.355.arr_ref, bf16[4,4,4,8192]{3,2,1,0:T(4,128)(2,1)S(1)} %get-tuple-element.375.tok_ref, f32[1,8192]{1,0:T(1,128)S(1)} %get-tuple-element.376.gain_ref, ...), custom_call_target="tpu_custom_call" | custom-call | tf_op jit(solution)/shard_map/while/body/eval_jaxpr/pallas_call | solution.py:136
  411.1 1.6 fusion.7
  412.7 2.9 collective-permute-done
  (52 shorter events, 5.6 us)
Async XLA Ops:
  0.6 5.0 %copy-start.1 = (s32[1024]{0:T(1024)S(1)}, s32[1024]{0:T(1024)}, u32[]{:S(2)}) copy-start(s32[1024]{0:T(1024)} %param.13) | copy-start | bytes 12292
  13.2 202.7 %all-to-all-start = ((bf16[64,32,2048]{2,1,0:T(8,128)(2,1)}), bf16[64,32,2048]{2,1,0:T(8,128)(2,1)}, u32[]{:S(2)}, u32[]{:S(2)}) async-start(bf16[64,32,2048]{2,1,0:T(8,128)(2,1)} %gather_fusion), calls=%async_computation | async-start | bytes 16777216 | tf_op jit(solution)/shard_map/all_to_all | solution.py:155
  29.7 192.7 %copy-start = (f32[1,8192]{1,0:T(1,128)S(1)}, f32[1,8192]{1,0:T(1,128)}, u32[]{:S(2)}) copy-start(f32[1,8192]{1,0:T(1,128)} %param.9) | copy-start | bytes 98308
  228.0 4.6 %collective-permute-start = (f32[4,8192]{1,0:T(4,128)}, f32[4,8192]{1,0:T(4,128)S(1)}, u32[]{:S(2)}, u32[]{:S(2)}) collective-permute-start(f32[4,8192]{1,0:T(4,128)} %get-tuple-element.335), channel_id=1, source_target_pairs={{192,0},{0,64},{64,128},{128,192},{193,1},{1,65},{65,129},{129,193... | collective-permute-start | bytes 393224 | tf_op jit(solution)/shard_map/while/body/eval_jaxpr/ppermute | solution.py:20
  238.1 4.6 %collective-permute-start = (f32[4,8192]{1,0:T(4,128)}, f32[4,8192]{1,0:T(4,128)S(1)}, u32[]{:S(2)}, u32[]{:S(2)}) collective-permute-start(f32[4,8192]{1,0:T(4,128)} %get-tuple-element.335), channel_id=1, source_target_pairs={{192,0},{0,64},{64,128},{128,192},{193,1},{1,65},{65,129},{129,193... | collective-permute-start | bytes 393224 | tf_op jit(solution)/shard_map/while/body/eval_jaxpr/ppermute | solution.py:20
  248.3 4.6 %collective-permute-start = (f32[4,8192]{1,0:T(4,128)}, f32[4,8192]{1,0:T(4,128)S(1)}, u32[]{:S(2)}, u32[]{:S(2)}) collective-permute-start(f32[4,8192]{1,0:T(4,128)} %get-tuple-element.335), channel_id=1, source_target_pairs={{192,0},{0,64},{64,128},{128,192},{193,1},{1,65},{65,129},{129,193... | collective-permute-start | bytes 393224 | tf_op jit(solution)/shard_map/while/body/eval_jaxpr/ppermute | solution.py:20
  258.5 4.6 %collective-permute-start = (f32[4,8192]{1,0:T(4,128)}, f32[4,8192]{1,0:T(4,128)S(1)}, u32[]{:S(2)}, u32[]{:S(2)}) collective-permute-start(f32[4,8192]{1,0:T(4,128)} %get-tuple-element.335), channel_id=1, source_target_pairs={{192,0},{0,64},{64,128},{128,192},{193,1},{1,65},{65,129},{129,193... | collective-permute-start | bytes 393224 | tf_op jit(solution)/shard_map/while/body/eval_jaxpr/ppermute | solution.py:20
  268.7 4.6 %collective-permute-start = (f32[4,8192]{1,0:T(4,128)}, f32[4,8192]{1,0:T(4,128)S(1)}, u32[]{:S(2)}, u32[]{:S(2)}) collective-permute-start(f32[4,8192]{1,0:T(4,128)} %get-tuple-element.335), channel_id=1, source_target_pairs={{192,0},{0,64},{64,128},{128,192},{193,1},{1,65},{65,129},{129,193... | collective-permute-start | bytes 393224 | tf_op jit(solution)/shard_map/while/body/eval_jaxpr/ppermute | solution.py:20
  278.8 4.6 %collective-permute-start = (f32[4,8192]{1,0:T(4,128)}, f32[4,8192]{1,0:T(4,128)S(1)}, u32[]{:S(2)}, u32[]{:S(2)}) collective-permute-start(f32[4,8192]{1,0:T(4,128)} %get-tuple-element.335), channel_id=1, source_target_pairs={{192,0},{0,64},{64,128},{128,192},{193,1},{1,65},{65,129},{129,193... | collective-permute-start | bytes 393224 | tf_op jit(solution)/shard_map/while/body/eval_jaxpr/ppermute | solution.py:20
  289.0 4.6 %collective-permute-start = (f32[4,8192]{1,0:T(4,128)}, f32[4,8192]{1,0:T(4,128)S(1)}, u32[]{:S(2)}, u32[]{:S(2)}) collective-permute-start(f32[4,8192]{1,0:T(4,128)} %get-tuple-element.335), channel_id=1, source_target_pairs={{192,0},{0,64},{64,128},{128,192},{193,1},{1,65},{65,129},{129,193... | collective-permute-start | bytes 393224 | tf_op jit(solution)/shard_map/while/body/eval_jaxpr/ppermute | solution.py:20
  299.2 4.6 %collective-permute-start = (f32[4,8192]{1,0:T(4,128)}, f32[4,8192]{1,0:T(4,128)S(1)}, u32[]{:S(2)}, u32[]{:S(2)}) collective-permute-start(f32[4,8192]{1,0:T(4,128)} %get-tuple-element.335), channel_id=1, source_target_pairs={{192,0},{0,64},{64,128},{128,192},{193,1},{1,65},{65,129},{129,193... | collective-permute-start | bytes 393224 | tf_op jit(solution)/shard_map/while/body/eval_jaxpr/ppermute | solution.py:20
  309.3 4.6 %collective-permute-start = (f32[4,8192]{1,0:T(4,128)}, f32[4,8192]{1,0:T(4,128)S(1)}, u32[]{:S(2)}, u32[]{:S(2)}) collective-permute-start(f32[4,8192]{1,0:T(4,128)} %get-tuple-element.335), channel_id=1, source_target_pairs={{192,0},{0,64},{64,128},{128,192},{193,1},{1,65},{65,129},{129,193... | collective-permute-start | bytes 393224 | tf_op jit(solution)/shard_map/while/body/eval_jaxpr/ppermute | solution.py:20
  319.5 4.6 %collective-permute-start = (f32[4,8192]{1,0:T(4,128)}, f32[4,8192]{1,0:T(4,128)S(1)}, u32[]{:S(2)}, u32[]{:S(2)}) collective-permute-start(f32[4,8192]{1,0:T(4,128)} %get-tuple-element.335), channel_id=1, source_target_pairs={{192,0},{0,64},{64,128},{128,192},{193,1},{1,65},{65,129},{129,193... | collective-permute-start | bytes 393224 | tf_op jit(solution)/shard_map/while/body/eval_jaxpr/ppermute | solution.py:20
  329.7 4.6 %collective-permute-start = (f32[4,8192]{1,0:T(4,128)}, f32[4,8192]{1,0:T(4,128)S(1)}, u32[]{:S(2)}, u32[]{:S(2)}) collective-permute-start(f32[4,8192]{1,0:T(4,128)} %get-tuple-element.335), channel_id=1, source_target_pairs={{192,0},{0,64},{64,128},{128,192},{193,1},{1,65},{65,129},{129,193... | collective-permute-start | bytes 393224 | tf_op jit(solution)/shard_map/while/body/eval_jaxpr/ppermute | solution.py:20
  339.9 4.6 %collective-permute-start = (f32[4,8192]{1,0:T(4,128)}, f32[4,8192]{1,0:T(4,128)S(1)}, u32[]{:S(2)}, u32[]{:S(2)}) collective-permute-start(f32[4,8192]{1,0:T(4,128)} %get-tuple-element.335), channel_id=1, source_target_pairs={{192,0},{0,64},{64,128},{128,192},{193,1},{1,65},{65,129},{129,193... | collective-permute-start | bytes 393224 | tf_op jit(solution)/shard_map/while/body/eval_jaxpr/ppermute | solution.py:20
  350.0 4.6 %collective-permute-start = (f32[4,8192]{1,0:T(4,128)}, f32[4,8192]{1,0:T(4,128)S(1)}, u32[]{:S(2)}, u32[]{:S(2)}) collective-permute-start(f32[4,8192]{1,0:T(4,128)} %get-tuple-element.335), channel_id=1, source_target_pairs={{192,0},{0,64},{64,128},{128,192},{193,1},{1,65},{65,129},{129,193... | collective-permute-start | bytes 393224 | tf_op jit(solution)/shard_map/while/body/eval_jaxpr/ppermute | solution.py:20
  360.2 4.6 %collective-permute-start = (f32[4,8192]{1,0:T(4,128)}, f32[4,8192]{1,0:T(4,128)S(1)}, u32[]{:S(2)}, u32[]{:S(2)}) collective-permute-start(f32[4,8192]{1,0:T(4,128)} %get-tuple-element.335), channel_id=1, source_target_pairs={{192,0},{0,64},{64,128},{128,192},{193,1},{1,65},{65,129},{129,193... | collective-permute-start | bytes 393224 | tf_op jit(solution)/shard_map/while/body/eval_jaxpr/ppermute | solution.py:20
  370.4 4.6 %collective-permute-start = (f32[4,8192]{1,0:T(4,128)}, f32[4,8192]{1,0:T(4,128)S(1)}, u32[]{:S(2)}, u32[]{:S(2)}) collective-permute-start(f32[4,8192]{1,0:T(4,128)} %get-tuple-element.335), channel_id=1, source_target_pairs={{192,0},{0,64},{64,128},{128,192},{193,1},{1,65},{65,129},{129,193... | collective-permute-start | bytes 393224 | tf_op jit(solution)/shard_map/while/body/eval_jaxpr/ppermute | solution.py:20
  380.6 4.6 %collective-permute-start = (f32[4,8192]{1,0:T(4,128)}, f32[4,8192]{1,0:T(4,128)S(1)}, u32[]{:S(2)}, u32[]{:S(2)}) collective-permute-start(f32[4,8192]{1,0:T(4,128)} %get-tuple-element.335), channel_id=1, source_target_pairs={{192,0},{0,64},{64,128},{128,192},{193,1},{1,65},{65,129},{129,193... | collective-permute-start | bytes 393224 | tf_op jit(solution)/shard_map/while/body/eval_jaxpr/ppermute | solution.py:20
  390.7 4.6 %collective-permute-start = (f32[4,8192]{1,0:T(4,128)}, f32[4,8192]{1,0:T(4,128)S(1)}, u32[]{:S(2)}, u32[]{:S(2)}) collective-permute-start(f32[4,8192]{1,0:T(4,128)} %get-tuple-element.335), channel_id=1, source_target_pairs={{192,0},{0,64},{64,128},{128,192},{193,1},{1,65},{65,129},{129,193... | collective-permute-start | bytes 393224 | tf_op jit(solution)/shard_map/while/body/eval_jaxpr/ppermute | solution.py:20
  400.9 4.6 %collective-permute-start = (f32[4,8192]{1,0:T(4,128)}, f32[4,8192]{1,0:T(4,128)S(1)}, u32[]{:S(2)}, u32[]{:S(2)}) collective-permute-start(f32[4,8192]{1,0:T(4,128)} %get-tuple-element.335), channel_id=1, source_target_pairs={{192,0},{0,64},{64,128},{128,192},{193,1},{1,65},{65,129},{129,193... | collective-permute-start | bytes 393224 | tf_op jit(solution)/shard_map/while/body/eval_jaxpr/ppermute | solution.py:20
  411.1 4.6 %collective-permute-start = (f32[4,8192]{1,0:T(4,128)}, f32[4,8192]{1,0:T(4,128)S(1)}, u32[]{:S(2)}, u32[]{:S(2)}) collective-permute-start(f32[4,8192]{1,0:T(4,128)} %get-tuple-element.335), channel_id=1, source_target_pairs={{192,0},{0,64},{64,128},{128,192},{193,1},{1,65},{65,129},{129,193... | collective-permute-start | bytes 393224 | tf_op jit(solution)/shard_map/while/body/eval_jaxpr/ppermute | solution.py:20
